TPU v7x, 512 devices: a whole 4x4x16 slice. The times are simulated.
512 devices in a mesh: req: 128 (over z, x, core), head: 4 (over y).
Axes of the slice: x: 4, y: 4, z: 16, core: 2. Of those that a mesh axis runs over, the one named last changes fastest.
Arguments:
- query_proj: bfloat16 [32768, 2048], P('req', 'head'), may hold values from -6 to 6
- key_proj: bfloat16 [32768, 2048], P('req', 'head'), may hold values from -6 to 6
- value_proj: bfloat16 [32768, 2048], P('req', 'head'), may hold values from -6 to 6
- lengths: int32 [64], replicated, may hold values from 1 to 8, 256 in all
- page_table: int32 [256], P('req'), may hold values from 0 to 255, as said below
- out_weight: bfloat16 [2048, 4096], P('req', 'head'), may hold values from -0.125 to 0.125
- out_bias: float32 [4096], P('head'), may hold values from -3 to 3
Outputs:
- attended: bfloat16 [32768, 4096], P('req', 'head')
- kv_pages: bfloat16 [256, 2, 128, 2048], P('req', None, None, 'head')
Inputs may be any that keep to these rules, and one draw needn't show every extreme that they name: page_table is a permutation in which page b of the stream goes to one of the pages 2 * (b // 2) to 2 * (b // 2) + 1.
All inputs are finite; a program needn't handle non-finite values.
Results may differ from a plain program's by a relative error of at most 0.0046.
Values may be sent and summed in bfloat16 or wider, within the bound.
No kernel may reach another device: no remote copies, remote signals or barrier semaphores. Data moves between devices by JAX's collectives and lax.ppermute only.
A program may use at most 64 MiB of HBM per device.

v0:
```python
import math

import jax
import jax.numpy as jnp
from jax import lax
from jax.sharding import PartitionSpec as P

DH = 128
ROT = 32
PAGE = 128
BLK_DEV = 2
REACH = 4
TOK_DEV = 256


rope_base = 10000.0


def passed_along(array, axis, by):
    count = lax.axis_size(axis)
    pairs = [(i, i + by) for i in range(count) if 0 <= i + by < count]
    return lax.ppermute(array, axis, pairs)


def request_info(lengths, token_index):
    request_ends = jnp.cumsum(lengths) * PAGE
    request_starts = request_ends - lengths * PAGE
    inside = request_starts[None, :] <= token_index[:, None]
    request_id = jnp.sum(inside.astype(jnp.int32), axis=1) - 1
    opening = jnp.max(jnp.where(inside, request_starts[None, :], 0), axis=1)
    return (request_id, token_index - opening)


def rotate_heads(projected, position):
    values_f32 = projected.astype(jnp.float32)
    half_rot = ROT // 2
    frequency = jnp.exp(
        jnp.arange(half_rot, dtype=jnp.float32) * (-2.0 * math.log(rope_base) / ROT)
    )
    angles = position.astype(jnp.float32)[:, None] * frequency[None, :]
    cosine = jnp.cos(angles)[:, None, :]
    sine = jnp.sin(angles)[:, None, :]
    front_half = values_f32[..., :half_rot]
    back_half = values_f32[..., half_rot:ROT]
    turned = jnp.concatenate(
        [
            front_half * cosine - back_half * sine,
            back_half * cosine + front_half * sine,
            values_f32[..., ROT:],
        ],
        axis=-1,
    )
    return turned.astype(jnp.bfloat16)


def attend_block(query_rot, key_rot, value_rows, query_id, query_token, key_id, key_token):
    scores = jnp.einsum("qhd,khd->hqk", query_rot, key_rot, preferred_element_type=jnp.float32) * (
        1.0 / math.sqrt(DH)
    )
    allowed = (query_id[:, None] == key_id[None, :]) & (key_token[None, :] <= query_token[:, None])
    scores = jnp.where(allowed[None], scores, -jnp.inf)
    row_max = jnp.max(scores, axis=-1, keepdims=True)
    raised = jnp.exp(scores - row_max)
    probs = (raised / jnp.sum(raised, axis=-1, keepdims=True)).astype(jnp.bfloat16)
    mixed = jnp.einsum("hqk,khd->qhd", probs, value_rows, preferred_element_type=jnp.float32)
    return mixed.astype(jnp.bfloat16)


def local(query_proj, key_proj, value_proj, lengths, page_table, out_weight, out_bias):
    local_heads = query_proj.shape[1] // DH
    device_rank = lax.axis_index("req")
    first_token = device_rank * TOK_DEV
    own_tokens = first_token + jnp.arange(TOK_DEV, dtype=jnp.int32)
    request_id, position = request_info(lengths, own_tokens)
    query_rot = rotate_heads(query_proj.reshape(TOK_DEV, local_heads, DH), position)
    key_flat = rotate_heads(key_proj.reshape(TOK_DEV, local_heads, DH), position).reshape(
        TOK_DEV, local_heads * DH
    )
    key_list = [key_flat]
    value_list = [value_proj]
    for distance in range(1, REACH + 1):
        far_key, far_value = passed_along((key_flat, value_proj), "req", distance)
        key_list.append(far_key)
        value_list.append(far_value)
    key_stack = jnp.stack(key_list[::-1], axis=0)
    value_stack = jnp.stack(value_list[::-1], axis=0)
    key_rows = (REACH + 1) * TOK_DEV
    key_all = key_stack.reshape(key_rows, local_heads, DH)
    value_all = value_stack.reshape(key_rows, local_heads, DH)
    key_tokens = first_token - REACH * TOK_DEV + jnp.arange(key_rows, dtype=jnp.int32)
    key_id, key_position = request_info(lengths, key_tokens)
    mixed = attend_block(query_rot, key_all, value_all, request_id, own_tokens, key_id, key_tokens)
    heads_out = mixed.reshape(TOK_DEV, local_heads * DH)
    weight_all_rows = lax.all_gather(out_weight, "req", axis=0, tiled=True)
    weight_own_rows = lax.all_to_all(
        weight_all_rows, "head", split_axis=0, concat_axis=1, tiled=True
    )
    partial_value = jnp.dot(heads_out, weight_own_rows, preferred_element_type=jnp.float32)
    summed = lax.psum_scatter(partial_value, "head", scatter_dimension=1, tiled=True)
    attended = (summed + out_bias).astype(jnp.bfloat16)
    local_page = page_table - device_rank * BLK_DEV
    picker = (local_page[:, None] == jnp.arange(BLK_DEV, dtype=jnp.int32)[None, :]).astype(
        jnp.bfloat16
    )
    page_blocks = jnp.stack(
        [
            key_flat.reshape(BLK_DEV, PAGE, local_heads * DH),
            value_proj.reshape(BLK_DEV, PAGE, local_heads * DH),
        ],
        axis=1,
    )
    kv_pages = jnp.einsum(
        "bp,bctd->pctd", picker, page_blocks, preferred_element_type=jnp.float32
    ).astype(jnp.bfloat16)
    return (attended, kv_pages)


def solution(mesh):
    placed = (
        P("req", "head"),
        P("req", "head"),
        P("req", "head"),
        P(),
        P("req"),
        P("req", "head"),
        P("head"),
    )
    return jax.shard_map(
        local,
        mesh=mesh,
        in_specs=placed,
        out_specs=(P("req", "head"), P("req", None, None, "head")),
        check_vma=False,
    )
```

profile of v0, /device:TPU:1, one launch (start us, length us, event | category | flops | bytes accessed | tf_op | source)
XLA Modules:
  0.0 291.5 jit_solution(7986303135102277170)
XLA Ops:
  7.9 0.7 copy.62
  10.0 1.1 copy.68
  12.0 6.2 %collective-permute-start.4 = (bf16[256,512]{0,1:T(8,128)(2,1)S(1)}, bf16[256,512]{0,1:T(8,128)(2,1)}, u32[]{:S(2)}, u32[]{:S(2)}) collective-permute-start(bf16[256,512]{0,1:T(8,128)(2,1)S(1)} %bitcast.44), channel_id=1, source_target_pairs={{0,16},{4,20},{8,24},{12,28},{16,32},{20,36},{24,40},{28,44},{32,4... | collective-permute-start | bytes 786440 | tf_op jit(solution)/shard_map/ppermute | solution.py:22
  18.2 4.3 %collective-permute-start.5 = (bf16[256,512]{0,1:T(8,128)(2,1)S(1)}, bf16[256,512]{0,1:T(8,128)(2,1)}, u32[]{:S(2)}, u32[]{:S(2)}) collective-permute-start(bf16[256,512]{0,1:T(8,128)(2,1)S(1)} %bitcast.45), channel_id=1, source_target_pairs={{0,12},{4,16},{8,20},{12,24},{16,28},{20,32},{24,36},{28,40},{32,4... | collective-permute-start | bytes 786440 | tf_op jit(solution)/shard_map/ppermute | solution.py:22
  22.5 2.4 collective-permute-start.6
  24.9 1.9 collective-permute-start.7
  26.9 5.3 %collective-permute-start = (bf16[256,512]{1,0:T(8,128)(2,1)S(1)}, bf16[256,512]{1,0:T(8,128)(2,1)}, u32[]{:S(2)}, u32[]{:S(2)}) collective-permute-start(bf16[256,512]{1,0:T(8,128)(2,1)S(1)} %copy-done.2), channel_id=1, source_target_pairs={{0,16},{4,20},{8,24},{12,28},{16,32},{20,36},{24,40},{28,44},{32,4... | collective-permute-start | bytes 786440 | tf_op jit(solution)/shard_map/ppermute | solution.py:22
  33.1 135.1 %all-gather.2.cloned.1.call-done = bf16[2048,1024]{1,0:T(8,128)(2,1)} async-done(((bf16[16,1024]{1,0:T(8,128)(2,1)}), bf16[2048,1024]{1,0:T(8,128)(2,1)}) %all-gather.2.cloned.1.call-update) | async-done | bytes 4194320 | tf_op jit(solution)/shard_map/all_gather | solution.py:94
  168.1 4.8 %all-to-all-start = ((bf16[4,512,1024]{2,1,0:T(8,128)(2,1)}), bf16[4,512,1024]{2,1,0:T(8,128)(2,1)}, u32[]{:S(2)}, u32[]{:S(2)}) async-start(bf16[4,512,1024]{2,1,0:T(8,128)(2,1)} %bitcast.43), calls=%async_computation | async-start | bytes 8388608 | tf_op jit(solution)/shard_map/all_to_all | solution.py:95
  173.4 1.0 pad_maximum_fusion.2
  174.4 3.7 %collective-permute-start.1 = (bf16[256,512]{1,0:T(8,128)(2,1)S(1)}, bf16[256,512]{1,0:T(8,128)(2,1)S(1)}, u32[]{:S(2)}, u32[]{:S(2)}) collective-permute-start(bf16[256,512]{1,0:T(8,128)(2,1)S(1)} %copy-done.2), channel_id=1, source_target_pairs={{0,12},{4,16},{8,20},{12,24},{16,28},{20,32},{24,36},{28,40},{32,4... | collective-permute-start | bytes 786440 | tf_op jit(solution)/shard_map/ppermute | solution.py:22
  178.0 1.7 bitcast_dynamic-update-slice_fusion.3
  179.7 2.5 collective-permute-start.2
  182.3 1.0 bitcast_dynamic-update-slice_fusion.8
  183.2 1.9 collective-permute-start.3
  185.2 1.7 bitcast_dynamic-update-slice_fusion.2
  186.8 0.7 bitcast_dynamic-update-slice_fusion.1
  187.6 0.7 bitcast_dynamic-update-slice_fusion
  188.3 0.7 constant_dynamic-update-slice_fusion
  189.1 1.6 copy.73
  190.7 1.3 reshape.211
  192.0 1.0 bitcast_dynamic-update-slice_fusion.6
  193.0 1.0 bitcast_dynamic-update-slice_fusion.5
  194.0 1.3 reshape.209
  195.8 3.1 %exponential_reduce_fusion = f32[4,256]{1,0:T(4,128)S(1)} fusion(bf16[256,4,128]{2,0,1:T(8,128)(2,1)} %pad_maximum_fusion.2, pred[256,1280]{1,0:T(8,128)(4,1)S(1)} %compare_and_fusion, bf16[1280,4,128]{2,1,0:T(4,128)(2,1)S(1)} %copy-done), kind=kOutput, calls=%fused_computation.4 | convolution fusion | flops 340788480 | bytes 1904640 | tf_op jit(solution)/shard_map/sub | solution.py:63
  198.8 4.5 %fusion.5 = bf16[4,128,256]{2,1,0:T(8,128)(2,1)} fusion(f32[4,256]{1,0:T(4,128)S(1)} %exponential_reduce_fusion, bf16[1280,4,128]{2,1,0:T(4,128)(2,1)S(1)} %copy-done.1, bf16[256,4,128]{2,0,1:T(8,128)(2,1)} %pad_maximum_fusion.2, pred[256,1280]{1,0:T(8,128)(4,1)S(1)} %compare_and_fusion, bf16[1280,4,128]{2,1,0:T(4,128)(2,1)S(1)} %copy-done), kind=kOutput, calls=%fused_computation.10 | convolution fusion | flops 677775616 | bytes 3477504 | tf_op jit(solution)/shard_map/hqk,khd->qhd/dot_general | solution.py:65
  203.3 18.3 %all-to-all-done = bf16[4,512,1024]{2,1,0:T(8,128)(2,1)} async-done(((bf16[4,512,1024]{2,1,0:T(8,128)(2,1)}), bf16[4,512,1024]{2,1,0:T(8,128)(2,1)}, u32[]{:S(2)}, u32[]{:S(2)}) %all-to-all-start) | async-done | bytes 4194336 | tf_op jit(solution)/shard_map/all_to_all | solution.py:95
  221.6 6.2 %copy.76 = bf16[512,4,1024]{0,2,1:T(8,128)(2,1)} copy(bf16[512,4,1024]{2,0,1:T(8,128)(2,1)} %bitcast.18) | data formatting | bytes 8388608 | tf_op jit(solution)/shard_map/all_to_all | solution.py:95
  227.9 5.5 %fusion.32 = f32[256,4096]{1,0:T(8,128)} fusion(bf16[256,512]{0,1:T(8,128)(2,1)S(1)} %bitcast.53, bf16[512,4096]{0,1:T(8,128)(2,1)} %bitcast.42), kind=kOutput, calls=%fused_computation.56 | convolution fusion | flops 1073741824 | bytes 8650752 | tf_op jit(solution)/shard_map/dot_general | solution.py:98
  234.8 0.9 copy.80
  235.7 46.8 %reduce-scatter.2.cloned.1.call-done = f32[256,1024]{1,0:T(8,128)} async-done(((f32[256,4096]{1,0:T(8,128)}), f32[256,1024]{1,0:T(8,128)}) %reduce-scatter.2.cloned.1.call-update) | async-done | bytes 1048592 | tf_op jit(solution)/shard_map/reduce_scatter | solution.py:99
  282.5 2.1 add_convert_fusion
  (61 shorter events, 6.1 us)
Async XLA Ops:
  7.2 160.9 %all-gather.2.cloned.1.call-start = ((), (), s32[]{:S(2)}) async-start(), calls=%async_computation.2 | async-start | bytes 4227072 | tf_op jit(solution)/shard_map/all_gather | solution.py:94
  11.5 15.3 %copy-start.2 = (bf16[256,512]{1,0:T(8,128)(2,1)S(1)}, bf16[256,512]{1,0:T(8,128)(2,1)}, u32[]{:S(2)}) copy-start(bf16[256,512]{1,0:T(8,128)(2,1)} %param.9) | copy-start | bytes 786436
  11.6 20.6 %copy-start.4 = (bf16[256,512]{1,0:T(8,128)(2,1)S(1)}, bf16[256,512]{1,0:T(8,128)(2,1)}, u32[]{:S(2)}) copy-start(bf16[256,512]{1,0:T(8,128)(2,1)} %param.7) | copy-start | bytes 786436
  12.0 162.4 %collective-permute-start.4 = (bf16[256,512]{0,1:T(8,128)(2,1)S(1)}, bf16[256,512]{0,1:T(8,128)(2,1)}, u32[]{:S(2)}, u32[]{:S(2)}) collective-permute-start(bf16[256,512]{0,1:T(8,128)(2,1)S(1)} %bitcast.44), channel_id=1, source_target_pairs={{0,16},{4,20},{8,24},{12,28},{16,32},{20,36},{24,40},{28,44},{32,4... | collective-permute-start | bytes 786440 | tf_op jit(solution)/shard_map/ppermute | solution.py:22
  18.2 165.1 %collective-permute-start.5 = (bf16[256,512]{0,1:T(8,128)(2,1)S(1)}, bf16[256,512]{0,1:T(8,128)(2,1)}, u32[]{:S(2)}, u32[]{:S(2)}) collective-permute-start(bf16[256,512]{0,1:T(8,128)(2,1)S(1)} %bitcast.45), channel_id=1, source_target_pairs={{0,12},{4,16},{8,20},{12,24},{16,28},{20,32},{24,36},{28,40},{32,4... | collective-permute-start | bytes 786440 | tf_op jit(solution)/shard_map/ppermute | solution.py:22
  22.5 164.3 %collective-permute-start.6 = (bf16[256,512]{0,1:T(8,128)(2,1)S(1)}, bf16[256,512]{0,1:T(8,128)(2,1)S(1)}, u32[]{:S(2)}, u32[]{:S(2)}) collective-permute-start(bf16[256,512]{0,1:T(8,128)(2,1)S(1)} %bitcast.46), channel_id=1, source_target_pairs={{0,8},{4,12},{8,16},{12,20},{16,24},{20,28},{24,32},{28,36},{32,40... | collective-permute-start | bytes 786440 | tf_op jit(solution)/shard_map/ppermute | solution.py:22
  24.9 162.6 %collective-permute-start.7 = (bf16[256,512]{0,1:T(8,128)(2,1)S(1)}, bf16[256,512]{0,1:T(8,128)(2,1)S(1)}, u32[]{:S(2)}, u32[]{:S(2)}) collective-permute-start(bf16[256,512]{0,1:T(8,128)(2,1)S(1)} %bitcast.47), channel_id=1, source_target_pairs={{0,4},{4,8},{8,12},{12,16},{16,20},{20,24},{24,28},{28,32},{32,36}... | collective-permute-start | bytes 786440 | tf_op jit(solution)/shard_map/ppermute | solution.py:22
  26.9 152.9 %collective-permute-start = (bf16[256,512]{1,0:T(8,128)(2,1)S(1)}, bf16[256,512]{1,0:T(8,128)(2,1)}, u32[]{:S(2)}, u32[]{:S(2)}) collective-permute-start(bf16[256,512]{1,0:T(8,128)(2,1)S(1)} %copy-done.2), channel_id=1, source_target_pairs={{0,16},{4,20},{8,24},{12,28},{16,32},{20,36},{24,40},{28,44},{32,4... | collective-permute-start | bytes 786440 | tf_op jit(solution)/shard_map/ppermute | solution.py:22
  168.1 53.5 %all-to-all-start = ((bf16[4,512,1024]{2,1,0:T(8,128)(2,1)}), bf16[4,512,1024]{2,1,0:T(8,128)(2,1)}, u32[]{:S(2)}, u32[]{:S(2)}) async-start(bf16[4,512,1024]{2,1,0:T(8,128)(2,1)} %bitcast.43), calls=%async_computation | async-start | bytes 8388608 | tf_op jit(solution)/shard_map/all_to_all | solution.py:95
  172.9 109.6 %reduce-scatter.2.cloned.1.call-start = ((), (), s32[]{:S(2)}) async-start(), calls=%async_computation.3 | async-start | bytes 5242880 | tf_op jit(solution)/shard_map/reduce_scatter | solution.py:99
  174.4 14.0 %collective-permute-start.1 = (bf16[256,512]{1,0:T(8,128)(2,1)S(1)}, bf16[256,512]{1,0:T(8,128)(2,1)S(1)}, u32[]{:S(2)}, u32[]{:S(2)}) collective-permute-start(bf16[256,512]{1,0:T(8,128)(2,1)S(1)} %copy-done.2), channel_id=1, source_target_pairs={{0,12},{4,16},{8,20},{12,24},{16,28},{20,32},{24,36},{28,40},{32,4... | collective-permute-start | bytes 786440 | tf_op jit(solution)/shard_map/ppermute | solution.py:22
  179.7 12.2 %collective-permute-start.2 = (bf16[256,512]{1,0:T(8,128)(2,1)S(1)}, bf16[256,512]{1,0:T(8,128)(2,1)}, u32[]{:S(2)}, u32[]{:S(2)}) collective-permute-start(bf16[256,512]{1,0:T(8,128)(2,1)S(1)} %copy-done.2), channel_id=1, source_target_pairs={{0,8},{4,12},{8,16},{12,20},{16,24},{20,28},{24,32},{28,36},{32,40... | collective-permute-start | bytes 786440 | tf_op jit(solution)/shard_map/ppermute | solution.py:22
  183.2 9.7 %collective-permute-start.3 = (bf16[256,512]{1,0:T(8,128)(2,1)S(1)}, bf16[256,512]{1,0:T(8,128)(2,1)}, u32[]{:S(2)}, u32[]{:S(2)}) collective-permute-start(bf16[256,512]{1,0:T(8,128)(2,1)S(1)} %copy-done.2), channel_id=1, source_target_pairs={{0,4},{4,8},{8,12},{12,16},{16,20},{20,24},{24,28},{28,32},{32,36}... | collective-permute-start | bytes 786440 | tf_op jit(solution)/shard_map/ppermute | solution.py:22
  194.0 1.8 copy-start
  195.7 3.1 %copy-start.1 = (bf16[1280,4,128]{2,1,0:T(4,128)(2,1)S(1)}, bf16[1280,4,128]{2,1,0:T(4,128)(2,1)}, u32[]{:S(2)}) copy-start(bf16[1280,4,128]{2,1,0:T(4,128)(2,1)} %reshape.209) | copy-start | bytes 3932164
  221.6 6.2 %copy-start.3 = (bf16[4,128,256]{2,1,0:T(8,128)(2,1)S(1)}, bf16[4,128,256]{2,1,0:T(8,128)(2,1)}, u32[]{:S(2)}) copy-start(bf16[4,128,256]{2,1,0:T(8,128)(2,1)} %fusion.5) | copy-start | bytes 786436
  233.3 0.8 copy-start.6
  234.1 48.4 %copy-start.5 = (f32[1024]{0:T(1024)S(1)}, f32[1024]{0:T(1024)}, u32[]{:S(2)}) copy-start(f32[1024]{0:T(1024)} %param.13) | copy-start | bytes 12292
Sparse Core Ops, SparseCore 0:
  11.1 156.9 all-gather.1
  233.5 49.0 reduce-scatter.1
where the time goes:
time: 292 us; the launch traced here: 291 us
  waiting for transfers between devices  201 us (69%)
  starting transfers between devices  33.2 us (11%)
  local copies, waits for them, and re-layouts  24.1 us (8%)
  between operations  14.4 us (5%)
  matrix products  13.7 us (5%)
  other arithmetic  5.11 us (2%)
    all_gather x1, waiting for transfers between devices, local(): weight_all_rows = lax.all_gather(out_weight, 'req', axis=0, tiled=True)  135 us
    reduce_scatter x1, waiting for transfers between devices, local(): lax.psum_scatter(partial_value, 'head', scatter_dimension=1, tiled=True)  46.8 us
    ppermute x8, starting transfers between devices, passed_along(): return lax.ppermute(array, axis, pairs)  28.3 us
    all_to_all x1, waiting for transfers between devices, local(): lax.all_to_all(weight_all_rows, 'head', split_axis=0, concat_axis=1, tile...  18.3 us
    unnamed x27, local copies, waits for them, and re-layouts  10.7 us
    all_to_all x1, local copies, waits for them, and re-layouts, local(): lax.all_to_all(weight_all_rows, 'head', split_axis=0, concat_axis=1, tile...  6.23 us
  transfers between devices with their start and end apart: 11, of which 3 were waited for; matrix products, arithmetic and copies ran while one was open for 10% of the time, Pallas kernels for 0%

commit v1 on v0

--- a/solution.py
+++ b/solution.py
@@ -3,7 +3,7 @@
 import jax
 import jax.numpy as jnp
 from jax import lax
-from jax.sharding import PartitionSpec as P
+from jax.sharding import Mesh, PartitionSpec as P
 
 DH = 128
 ROT = 32
@@ -14,6 +14,9 @@
 
 
 rope_base = 10000.0
+
+
+REQ = ("z", "x", "core")
 
 
 def passed_along(array, axis, by):
@@ -68,7 +71,7 @@
 
 def local(query_proj, key_proj, value_proj, lengths, page_table, out_weight, out_bias):
     local_heads = query_proj.shape[1] // DH
-    device_rank = lax.axis_index("req")
+    device_rank = lax.axis_index(REQ)
     first_token = device_rank * TOK_DEV
     own_tokens = first_token + jnp.arange(TOK_DEV, dtype=jnp.int32)
     request_id, position = request_info(lengths, own_tokens)
@@ -79,7 +82,7 @@
     key_list = [key_flat]
     value_list = [value_proj]
     for distance in range(1, REACH + 1):
-        far_key, far_value = passed_along((key_flat, value_proj), "req", distance)
+        far_key, far_value = passed_along((key_flat, value_proj), REQ, distance)
         key_list.append(far_key)
         value_list.append(far_value)
     key_stack = jnp.stack(key_list[::-1], axis=0)
@@ -91,12 +94,11 @@
     key_id, key_position = request_info(lengths, key_tokens)
     mixed = attend_block(query_rot, key_all, value_all, request_id, own_tokens, key_id, key_tokens)
     heads_out = mixed.reshape(TOK_DEV, local_heads * DH)
-    weight_all_rows = lax.all_gather(out_weight, "req", axis=0, tiled=True)
-    weight_own_rows = lax.all_to_all(
-        weight_all_rows, "head", split_axis=0, concat_axis=1, tiled=True
-    )
-    partial_value = jnp.dot(heads_out, weight_own_rows, preferred_element_type=jnp.float32)
-    summed = lax.psum_scatter(partial_value, "head", scatter_dimension=1, tiled=True)
+    weight_rows = lax.all_gather(out_weight, "core", axis=0, tiled=True)
+    weight_rows = lax.all_gather(weight_rows, "x", axis=0, tiled=True)
+    weight_rows = lax.all_gather(weight_rows, "z", axis=0, tiled=True)
+    heads_all = lax.all_gather(heads_out, "head", axis=1, tiled=True)
+    summed = jnp.dot(heads_all, weight_rows, preferred_element_type=jnp.float32)
     attended = (summed + out_bias).astype(jnp.bfloat16)
     local_page = page_table - device_rank * BLK_DEV
     picker = (local_page[:, None] == jnp.arange(BLK_DEV, dtype=jnp.int32)[None, :]).astype(
@@ -116,19 +118,27 @@
 
 
 def solution(mesh):
+    devices = mesh.devices
+    cores = len({d.core_on_chip for d in devices.flat})
+    columns = len({d.coords[0] for d in devices.flat})
+    req_size, head_size = devices.shape
+    split = Mesh(
+        devices.reshape(req_size // (columns * cores), columns, cores, head_size),
+        ("z", "x", "core", "head"),
+    )
     placed = (
-        P("req", "head"),
-        P("req", "head"),
-        P("req", "head"),
+        P(REQ, "head"),
+        P(REQ, "head"),
+        P(REQ, "head"),
         P(),
-        P("req"),
-        P("req", "head"),
+        P(REQ),
+        P(REQ, "head"),
         P("head"),
     )
     return jax.shard_map(
         local,
-        mesh=mesh,
+        mesh=split,
         in_specs=placed,
-        out_specs=(P("req", "head"), P("req", None, None, "head")),
+        out_specs=(P(REQ, "head"), P(REQ, None, None, "head")),
         check_vma=False,
     )

time: 292 us -> 201 us (0.69)
  the two profiles are of different devices: /device:TPU:1 before, /device:TPU:2 now
where the time goes in v1:
time: 201 us; the launch traced here: 200 us
  waiting for transfers between devices  100 us (50%)
  starting transfers between devices  34 us (17%)
  blocking collectives  19.1 us (10%)
  local copies, waits for them, and re-layouts  17.7 us (9%)
  between operations  14.5 us (7%)
  matrix products  12.8 us (6%)
  other arithmetic  2.33 us (1%)
    all_gather x1, waiting for transfers between devices, local(): weight_rows = lax.all_gather(weight_rows, 'z', axis=0, tiled=True)  80.5 us
    ppermute x8, starting transfers between devices, passed_along(): return lax.ppermute(array, axis, pairs)  33.9 us
    all_gather x1, waiting for transfers between devices, local(): heads_all = lax.all_gather(heads_out, 'head', axis=1, tiled=True)  18.8 us
    all_gather x1, blocking collectives, local(): weight_rows = lax.all_gather(weight_rows, 'x', axis=0, tiled=True)  16 us
    unnamed x29, local copies, waits for them, and re-layouts  10.7 us
    dot_general x1, matrix products, local(): summed = jnp.dot(heads_all, weight_rows, preferred_element_type=jnp.float32)  4.59 us
    dot_general x1, matrix products, attend_block(): jnp.einsum('hqk,khd->qhd', probs, value_rows, preferred_element_type=jnp....  4.48 us
  transfers between devices with their start and end apart: 10, of which 3 were waited for; matrix products, arithmetic and copies ran while one was open for 7% of the time, Pallas kernels for 0%

profile of v1, /device:TPU:2, one launch (start us, length us, event | category | flops | bytes accessed | tf_op | source)
XLA Modules:
  0.0 200.4 jit_solution(546849596047994481)
XLA Ops:
  7.2 1.1 copy.50
  8.4 0.7 copy.44
  10.7 4.0 %collective-permute-start.4 = (bf16[256,512]{0,1:T(8,128)(2,1)S(1)}, bf16[256,512]{0,1:T(8,128)(2,1)S(1)}, u32[]{:S(2)}, u32[]{:S(2)}) collective-permute-start(bf16[256,512]{0,1:T(8,128)(2,1)S(1)} %bitcast.39), channel_id=1, source_target_pairs={{0,16},{4,20},{8,24},{12,28},{16,32},{20,36},{24,40},{28,44},{32,4... | collective-permute-start | bytes 786440 | tf_op jit(solution)/shard_map/ppermute | solution.py:25
  14.7 3.0 %collective-permute-start.5 = (bf16[256,512]{0,1:T(8,128)(2,1)S(1)}, bf16[256,512]{0,1:T(8,128)(2,1)}, u32[]{:S(2)}, u32[]{:S(2)}) collective-permute-start(bf16[256,512]{0,1:T(8,128)(2,1)S(1)} %bitcast.40), channel_id=1, source_target_pairs={{0,12},{4,16},{8,20},{12,24},{16,28},{20,32},{24,36},{28,40},{32,4... | collective-permute-start | bytes 786440 | tf_op jit(solution)/shard_map/ppermute | solution.py:25
  17.7 3.3 %collective-permute-start.6 = (bf16[256,512]{0,1:T(8,128)(2,1)S(1)}, bf16[256,512]{0,1:T(8,128)(2,1)}, u32[]{:S(2)}, u32[]{:S(2)}) collective-permute-start(bf16[256,512]{0,1:T(8,128)(2,1)S(1)} %bitcast.41), channel_id=1, source_target_pairs={{0,8},{4,12},{8,16},{12,20},{16,24},{20,28},{24,32},{28,36},{32,40... | collective-permute-start | bytes 786440 | tf_op jit(solution)/shard_map/ppermute | solution.py:25
  21.0 3.5 %collective-permute-start.7 = (bf16[256,512]{0,1:T(8,128)(2,1)S(1)}, bf16[256,512]{0,1:T(8,128)(2,1)}, u32[]{:S(2)}, u32[]{:S(2)}) collective-permute-start(bf16[256,512]{0,1:T(8,128)(2,1)S(1)} %bitcast.42), channel_id=1, source_target_pairs={{0,4},{4,8},{8,12},{12,16},{16,20},{20,24},{24,28},{28,32},{32,36}... | collective-permute-start | bytes 786440 | tf_op jit(solution)/shard_map/ppermute | solution.py:25
  24.6 4.4 %collective-permute-start = (bf16[256,512]{1,0:T(8,128)(2,1)S(1)}, bf16[256,512]{1,0:T(8,128)(2,1)S(1)}, u32[]{:S(2)}, u32[]{:S(2)}) collective-permute-start(bf16[256,512]{1,0:T(8,128)(2,1)S(1)} %copy-done.2), channel_id=1, source_target_pairs={{0,16},{4,20},{8,24},{12,28},{16,32},{20,36},{24,40},{28,44},{32,4... | collective-permute-start | bytes 786440 | tf_op jit(solution)/shard_map/ppermute | solution.py:25
  30.2 1.0 pad_maximum_fusion.2
  31.2 2.1 %collective-permute-start.1 = (bf16[256,512]{1,0:T(8,128)(2,1)S(1)}, bf16[256,512]{1,0:T(8,128)(2,1)S(1)}, u32[]{:S(2)}, u32[]{:S(2)}) collective-permute-start(bf16[256,512]{1,0:T(8,128)(2,1)S(1)} %copy-done.2), channel_id=1, source_target_pairs={{0,12},{4,16},{8,20},{12,24},{16,28},{20,32},{24,36},{28,40},{32,4... | collective-permute-start | bytes 786440 | tf_op jit(solution)/shard_map/ppermute | solution.py:25
  33.3 0.7 bitcast_dynamic-update-slice_fusion.3
  34.0 0.6 collective-permute-done
  34.7 9.2 %collective-permute-start.2 = (bf16[256,512]{1,0:T(8,128)(2,1)S(1)}, bf16[256,512]{1,0:T(8,128)(2,1)}, u32[]{:S(2)}, u32[]{:S(2)}) collective-permute-start(bf16[256,512]{1,0:T(8,128)(2,1)S(1)} %copy-done.2), channel_id=1, source_target_pairs={{0,8},{4,12},{8,16},{12,20},{16,24},{20,28},{24,32},{28,36},{32,40... | collective-permute-start | bytes 786440 | tf_op jit(solution)/shard_map/ppermute | solution.py:25
  43.9 4.4 %collective-permute-start.3 = (bf16[256,512]{1,0:T(8,128)(2,1)S(1)}, bf16[256,512]{1,0:T(8,128)(2,1)}, u32[]{:S(2)}, u32[]{:S(2)}) collective-permute-start(bf16[256,512]{1,0:T(8,128)(2,1)S(1)} %copy-done.2), channel_id=1, source_target_pairs={{0,4},{4,8},{8,12},{12,16},{16,20},{20,24},{24,28},{28,32},{32,36}... | collective-permute-start | bytes 786440 | tf_op jit(solution)/shard_map/ppermute | solution.py:25
  48.2 1.7 bitcast_dynamic-update-slice_fusion.2
  49.9 1.7 bitcast_dynamic-update-slice_fusion.1
  51.6 1.7 bitcast_dynamic-update-slice_fusion
  53.3 0.7 constant_dynamic-update-slice_fusion
  54.0 1.6 copy.55
  55.6 1.2 reshape.208
  56.8 1.0 bitcast_dynamic-update-slice_fusion.6
  57.8 1.0 bitcast_dynamic-update-slice_fusion.5
  58.8 1.2 reshape.206
  60.1 0.5 copy-done
  60.6 3.1 %exponential_reduce_fusion = f32[4,256]{1,0:T(4,128)S(1)} fusion(bf16[256,4,128]{2,0,1:T(8,128)(2,1)} %pad_maximum_fusion.2, pred[256,1280]{1,0:T(8,128)(4,1)S(1)} %compare_and_fusion, bf16[1280,4,128]{2,1,0:T(4,128)(2,1)S(1)} %copy-done), kind=kOutput, calls=%fused_computation.4 | convolution fusion | flops 340788480 | bytes 1904640 | tf_op jit(solution)/shard_map/sub | solution.py:66
  63.7 4.5 %fusion.6 = bf16[4,128,256]{2,1,0:T(8,128)(2,1)} fusion(f32[4,256]{1,0:T(4,128)S(1)} %exponential_reduce_fusion, bf16[1280,4,128]{2,1,0:T(4,128)(2,1)S(1)} %copy-done.1, bf16[256,4,128]{2,0,1:T(8,128)(2,1)} %pad_maximum_fusion.2, pred[256,1280]{1,0:T(8,128)(4,1)S(1)} %compare_and_fusion, bf16[1280,4,128]{2,1,0:T(4,128)(2,1)S(1)} %copy-done), kind=kOutput, calls=%fused_computation.12 | convolution fusion | flops 677775616 | bytes 3477504 | tf_op jit(solution)/shard_map/hqk,khd->qhd/dot_general | solution.py:68
  68.2 3.1 %all_gather.13 = bf16[32,1024]{1,0:T(8,128)(2,1)S(1)} all-gather(bf16[16,1024]{1,0:T(8,128)(2,1)S(1)} %copy-done.4), channel_id=1, replica_groups=mesh['z'=16,'x'=4,'core'=2,'head'=4] {'core'}, dimensions={0}, use_global_device_ids=true | all-gather | bytes 98304 | tf_op jit(solution)/shard_map/all_gather | solution.py:97
  71.3 16.0 %all_gather.14 = bf16[128,1024]{1,0:T(8,128)(2,1)} all-gather(bf16[32,1024]{1,0:T(8,128)(2,1)S(1)} %all_gather.13), channel_id=1, replica_groups=mesh['z'=16,'x'=4,'core'=2,'head'=4] {'x'}, dimensions={0}, use_global_device_ids=true | all-gather | bytes 327680 | tf_op jit(solution)/shard_map/all_gather | solution.py:98
  88.2 0.7 convolution_convert_fusion
  88.9 0.9 copy.61
  89.7 18.8 %all-gather.3.cloned.1.call-done = bf16[256,2048]{0,1:T(8,128)(2,1)} async-done(((bf16[256,512]{0,1:T(8,128)(2,1)}), bf16[256,2048]{0,1:T(8,128)(2,1)}) %all-gather.3.cloned.1.call-update) | async-done | bytes 1048592 | tf_op jit(solution)/shard_map/all_gather | solution.py:100
  108.5 80.5 %all-gather.5.cloned.1.call-done = bf16[2048,1024]{1,0:T(8,128)(2,1)} async-done(((bf16[128,1024]{1,0:T(8,128)(2,1)}), bf16[2048,1024]{1,0:T(8,128)(2,1)}) %all-gather.5.cloned.1.call-update) | async-done | bytes 4194320 | tf_op jit(solution)/shard_map/all_gather | solution.py:99
  189.0 4.6 %fusion.5 = bf16[256,1024]{1,0:T(8,128)(2,1)} fusion(bf16[256,2048]{0,1:T(8,128)(2,1)} %all-gather.3.cloned.1.call-done, bf16[2048,1024]{1,0:T(8,128)(2,1)} %all-gather.5.cloned.1.call-done, f32[1024]{0:T(1024)S(1)} %copy-done.6), kind=kOutput, calls=%fused_computation.10 | convolution fusion | flops 1074266112 | bytes 5771264 | tf_op jit(solution)/shard_map/dot_general | solution.py:101
  (61 shorter events, 3.6 us)
Async XLA Ops:
  7.2 2.2 %copy-start.5 = (s32[64]{0:T(128)S(1)}, s32[64]{0:T(128)}, u32[]{:S(2)}) copy-start(s32[64]{0:T(128)} %param.10) | copy-start | bytes 772
  7.2 101.3 %all-gather.3.cloned.1.call-start = ((), (), s32[]{:S(2)}) async-start(), calls=%async_computation | async-start | bytes 1310720 | tf_op jit(solution)/shard_map/all_gather | solution.py:100
  10.2 14.3 %copy-start.2 = (bf16[256,512]{1,0:T(8,128)(2,1)S(1)}, bf16[256,512]{1,0:T(8,128)(2,1)}, u32[]{:S(2)}) copy-start(bf16[256,512]{1,0:T(8,128)(2,1)} %param.9) | copy-start | bytes 786436
  10.2 18.7 %copy-start.3 = (bf16[256,512]{1,0:T(8,128)(2,1)S(1)}, bf16[256,512]{1,0:T(8,128)(2,1)}, u32[]{:S(2)}) copy-start(bf16[256,512]{1,0:T(8,128)(2,1)} %param.7) | copy-start | bytes 786436
  10.7 20.5 %collective-permute-start.4 = (bf16[256,512]{0,1:T(8,128)(2,1)S(1)}, bf16[256,512]{0,1:T(8,128)(2,1)S(1)}, u32[]{:S(2)}, u32[]{:S(2)}) collective-permute-start(bf16[256,512]{0,1:T(8,128)(2,1)S(1)} %bitcast.39), channel_id=1, source_target_pairs={{0,16},{4,20},{8,24},{12,28},{16,32},{20,36},{24,40},{28,44},{32,4... | collective-permute-start | bytes 786440 | tf_op jit(solution)/shard_map/ppermute | solution.py:25
  14.7 29.1 %collective-permute-start.5 = (bf16[256,512]{0,1:T(8,128)(2,1)S(1)}, bf16[256,512]{0,1:T(8,128)(2,1)}, u32[]{:S(2)}, u32[]{:S(2)}) collective-permute-start(bf16[256,512]{0,1:T(8,128)(2,1)S(1)} %bitcast.40), channel_id=1, source_target_pairs={{0,12},{4,16},{8,20},{12,24},{16,28},{20,32},{24,36},{28,40},{32,4... | collective-permute-start | bytes 786440 | tf_op jit(solution)/shard_map/ppermute | solution.py:25
  17.7 32.2 %collective-permute-start.6 = (bf16[256,512]{0,1:T(8,128)(2,1)S(1)}, bf16[256,512]{0,1:T(8,128)(2,1)}, u32[]{:S(2)}, u32[]{:S(2)}) collective-permute-start(bf16[256,512]{0,1:T(8,128)(2,1)S(1)} %bitcast.41), channel_id=1, source_target_pairs={{0,8},{4,12},{8,16},{12,20},{16,24},{20,28},{24,32},{28,36},{32,40... | collective-permute-start | bytes 786440 | tf_op jit(solution)/shard_map/ppermute | solution.py:25
  21.0 30.5 %collective-permute-start.7 = (bf16[256,512]{0,1:T(8,128)(2,1)S(1)}, bf16[256,512]{0,1:T(8,128)(2,1)}, u32[]{:S(2)}, u32[]{:S(2)}) collective-permute-start(bf16[256,512]{0,1:T(8,128)(2,1)S(1)} %bitcast.42), channel_id=1, source_target_pairs={{0,4},{4,8},{8,12},{12,16},{16,20},{20,24},{24,28},{28,32},{32,36}... | collective-permute-start | bytes 786440 | tf_op jit(solution)/shard_map/ppermute | solution.py:25
  24.6 10.1 %collective-permute-start = (bf16[256,512]{1,0:T(8,128)(2,1)S(1)}, bf16[256,512]{1,0:T(8,128)(2,1)S(1)}, u32[]{:S(2)}, u32[]{:S(2)}) collective-permute-start(bf16[256,512]{1,0:T(8,128)(2,1)S(1)} %copy-done.2), channel_id=1, source_target_pairs={{0,16},{4,20},{8,24},{12,28},{16,32},{20,36},{24,40},{28,44},{32,4... | collective-permute-start | bytes 786440 | tf_op jit(solution)/shard_map/ppermute | solution.py:25
  31.2 22.1 %collective-permute-start.1 = (bf16[256,512]{1,0:T(8,128)(2,1)S(1)}, bf16[256,512]{1,0:T(8,128)(2,1)S(1)}, u32[]{:S(2)}, u32[]{:S(2)}) collective-permute-start(bf16[256,512]{1,0:T(8,128)(2,1)S(1)} %copy-done.2), channel_id=1, source_target_pairs={{0,12},{4,16},{8,20},{12,24},{16,28},{20,32},{24,36},{28,40},{32,4... | collective-permute-start | bytes 786440 | tf_op jit(solution)/shard_map/ppermute | solution.py:25
  34.7 22.2 %collective-permute-start.2 = (bf16[256,512]{1,0:T(8,128)(2,1)S(1)}, bf16[256,512]{1,0:T(8,128)(2,1)}, u32[]{:S(2)}, u32[]{:S(2)}) collective-permute-start(bf16[256,512]{1,0:T(8,128)(2,1)S(1)} %copy-done.2), channel_id=1, source_target_pairs={{0,8},{4,12},{8,16},{12,20},{16,24},{20,28},{24,32},{28,36},{32,40... | collective-permute-start | bytes 786440 | tf_op jit(solution)/shard_map/ppermute | solution.py:25
  43.9 13.9 %collective-permute-start.3 = (bf16[256,512]{1,0:T(8,128)(2,1)S(1)}, bf16[256,512]{1,0:T(8,128)(2,1)}, u32[]{:S(2)}, u32[]{:S(2)}) collective-permute-start(bf16[256,512]{1,0:T(8,128)(2,1)S(1)} %copy-done.2), channel_id=1, source_target_pairs={{0,4},{4,8},{8,12},{12,16},{16,20},{20,24},{24,28},{28,32},{32,36}... | collective-permute-start | bytes 786440 | tf_op jit(solution)/shard_map/ppermute | solution.py:25
  58.8 1.8 copy-start
  60.6 3.1 %copy-start.1 = (bf16[1280,4,128]{2,1,0:T(4,128)(2,1)S(1)}, bf16[1280,4,128]{2,1,0:T(4,128)(2,1)}, u32[]{:S(2)}) copy-start(bf16[1280,4,128]{2,1,0:T(4,128)(2,1)} %reshape.206) | copy-start | bytes 3932164
  63.7 4.6 %copy-start.4 = (bf16[16,1024]{1,0:T(8,128)(2,1)S(1)}, bf16[16,1024]{1,0:T(8,128)(2,1)}, u32[]{:S(2)}) copy-start(bf16[16,1024]{1,0:T(8,128)(2,1)} %param.12) | copy-start | bytes 98308
  68.2 20.0 %copy-start.7 = (s32[2]{0:T(128)S(1)}, s32[2]{0:T(128)}, u32[]{:S(2)}) copy-start(s32[2]{0:T(128)} %param.11) | copy-start | bytes 28
  68.2 120.8 %all-gather.5.cloned.1.call-start = ((), (), s32[]{:S(2)}) async-start(), calls=%async_computation.1 | async-start | bytes 4456448 | tf_op jit(solution)/shard_map/all_gather | solution.py:99
  88.2 100.9 %copy-start.6 = (f32[1024]{0:T(1024)S(1)}, f32[1024]{0:T(1024)}, u32[]{:S(2)}) copy-start(f32[1024]{0:T(1024)} %param.13) | copy-start | bytes 12292
Sparse Core Ops, SparseCore 0:
  68.3 40.1 all-gather.2
  110.6 78.3 all-gather.4

commit v2 on v1

--- a/solution.py
+++ b/solution.py
@@ -4,6 +4,7 @@
 import jax.numpy as jnp
 from jax import lax
 from jax.sharding import Mesh, PartitionSpec as P
+
 
 DH = 128
 ROT = 32
@@ -69,9 +70,18 @@
     return mixed.astype(jnp.bfloat16)
 
 
-def local(query_proj, key_proj, value_proj, lengths, page_table, out_weight, out_bias):
+def local_body(query_proj, key_proj, value_proj, lengths, page_table, out_weight, out_bias):
     local_heads = query_proj.shape[1] // DH
     device_rank = lax.axis_index(REQ)
+    core_rank = lax.axis_index("core")
+    half = out_weight.shape[1] // 2
+    weight_pair = lax.all_gather(out_weight, "core", axis=0, tiled=True)
+    weight_rows = lax.dynamic_slice_in_dim(weight_pair, core_rank * half, half, 1)
+    weight_rows = lax.all_gather(weight_rows, "x", axis=0, tiled=True)
+    weight_rows, query_proj, key_proj = lax.optimization_barrier(
+        (weight_rows, query_proj, key_proj)
+    )
+    weight_rows = lax.all_gather(weight_rows, "z", axis=0, tiled=True)
     first_token = device_rank * TOK_DEV
     own_tokens = first_token + jnp.arange(TOK_DEV, dtype=jnp.int32)
     request_id, position = request_info(lengths, own_tokens)
@@ -79,27 +89,28 @@
     key_flat = rotate_heads(key_proj.reshape(TOK_DEV, local_heads, DH), position).reshape(
         TOK_DEV, local_heads * DH
     )
-    key_list = [key_flat]
-    value_list = [value_proj]
+    halo = jnp.stack([key_flat, value_proj], axis=0)
+    halo_list = [halo]
     for distance in range(1, REACH + 1):
-        far_key, far_value = passed_along((key_flat, value_proj), REQ, distance)
-        key_list.append(far_key)
-        value_list.append(far_value)
-    key_stack = jnp.stack(key_list[::-1], axis=0)
-    value_stack = jnp.stack(value_list[::-1], axis=0)
+        halo_list.append(passed_along(halo, REQ, distance))
+    halo_stack = jnp.stack(halo_list[::-1], axis=1)
+    key_stack = halo_stack[0]
+    value_stack = halo_stack[1]
     key_rows = (REACH + 1) * TOK_DEV
     key_all = key_stack.reshape(key_rows, local_heads, DH)
     value_all = value_stack.reshape(key_rows, local_heads, DH)
     key_tokens = first_token - REACH * TOK_DEV + jnp.arange(key_rows, dtype=jnp.int32)
-    key_id, key_position = request_info(lengths, key_tokens)
+    key_id, _ = request_info(lengths, key_tokens)
     mixed = attend_block(query_rot, key_all, value_all, request_id, own_tokens, key_id, key_tokens)
     heads_out = mixed.reshape(TOK_DEV, local_heads * DH)
-    weight_rows = lax.all_gather(out_weight, "core", axis=0, tiled=True)
-    weight_rows = lax.all_gather(weight_rows, "x", axis=0, tiled=True)
-    weight_rows = lax.all_gather(weight_rows, "z", axis=0, tiled=True)
     heads_all = lax.all_gather(heads_out, "head", axis=1, tiled=True)
-    summed = jnp.dot(heads_all, weight_rows, preferred_element_type=jnp.float32)
-    attended = (summed + out_bias).astype(jnp.bfloat16)
+    heads_pair = lax.all_gather(heads_all, "core", axis=0, tiled=True)
+    summed = jnp.dot(heads_pair, weight_rows, preferred_element_type=jnp.float32)
+    bias_half = lax.dynamic_slice_in_dim(out_bias, core_rank * half, half, 0)
+    pair_out = (summed + bias_half).astype(jnp.bfloat16)
+    attended = lax.all_to_all(
+        pair_out.reshape(2, TOK_DEV, half), "core", 0, 2, tiled=True
+    ).reshape(TOK_DEV, 2 * half)
     local_page = page_table - device_rank * BLK_DEV
     picker = (local_page[:, None] == jnp.arange(BLK_DEV, dtype=jnp.int32)[None, :]).astype(
         jnp.bfloat16
@@ -136,7 +147,7 @@
         P("head"),
     )
     return jax.shard_map(
-        local,
+        local_body,
         mesh=split,
         in_specs=placed,
         out_specs=(P(REQ, "head"), P(REQ, None, None, "head")),

time: 201 us -> 235 us (1.17)
  the two profiles are of different devices: /device:TPU:2 before, /device:TPU:1 now
where the time goes in v2:
time: 235 us
  waiting for transfers between devices  153 us (65%)
  blocking collectives  22.4 us (10%)
  local copies, waits for them, and re-layouts  17 us (7%)
  between operations  14.1 us (6%)
  starting transfers between devices  12.2 us (5%)
  matrix products  12.1 us (5%)
  other arithmetic  3.8 us (2%)
    all_gather x1, waiting for transfers between devices, local_body(): weight_rows = lax.all_gather(weight_rows, 'z', axis=0, tiled=True)  65.6 us
    all_gather x1, waiting for transfers between devices, local_body(): heads_all = lax.all_gather(heads_out, 'head', axis=1, tiled=True)  30.6 us
    all_gather x1, waiting for transfers between devices, local_body(): heads_pair = lax.all_gather(heads_all, 'core', axis=0, tiled=True)  30.2 us
    ppermute x4, waiting for transfers between devices, passed_along(): return lax.ppermute(array, axis, pairs)  26 us
    ppermute x4, starting transfers between devices, passed_along(): return lax.ppermute(array, axis, pairs)  11.9 us
    all_gather x1, blocking collectives, local_body(): weight_rows = lax.all_gather(weight_rows, 'x', axis=0, tiled=True)  9.83 us
    all_gather x1, blocking collectives, local_body(): weight_pair = lax.all_gather(out_weight, 'core', axis=0, tiled=True)  8.55 us
    dot_general x1, matrix products, attend_block(): jnp.einsum('hqk,khd->qhd', probs, value_rows, preferred_element_type=jnp....  4.78 us
  transfers between devices with their start and end apart: 7, of which 6 were waited for; matrix products, arithmetic and copies ran while one was open for 3% of the time, Pallas kernels for 0%

profile of v2, /device:TPU:1, one launch (start us, length us, event | category | flops | bytes accessed | tf_op | source)
XLA Modules:
  0.0 234.8 jit_solution(14269620803667977578)
XLA Ops:
  7.2 8.6 %all_gather.15 = bf16[32,1024]{1,0:T(8,128)(2,1)S(1)} all-gather(bf16[16,1024]{1,0:T(8,128)(2,1)} %param.12), channel_id=1, replica_groups=mesh['z'=16,'x'=4,'core'=2,'head'=4] {'core'}, dimensions={0}, use_global_device_ids=true | all-gather | bytes 98304 | tf_op jit(solution)/shard_map/all_gather | solution.py:78
  15.8 9.8 %all_gather.16 = bf16[128,512]{1,0:T(8,128)(2,1)} all-gather(bf16[32,512]{1,0:T(8,128)(2,1)S(1)} %constant_dynamic-slice_fusion), channel_id=1, replica_groups=mesh['z'=16,'x'=4,'core'=2,'head'=4] {'x'}, dimensions={0}, use_global_device_ids=true | all-gather | bytes 163840 | tf_op jit(solution)/shard_map/all_gather | solution.py:80
  25.6 1.1 copy.51
  26.8 0.7 copy.53
  27.8 0.7 multiply_subtract_fusion.1
  29.9 3.9 %collective-permute-start = (bf16[2,256,512]{1,2,0:T(8,128)(2,1)S(1)}, bf16[2,256,512]{1,2,0:T(8,128)(2,1)}, u32[]{:S(2)}, u32[]{:S(2)}) collective-permute-start(bf16[2,256,512]{1,2,0:T(8,128)(2,1)S(1)} %pad_maximum_fusion), channel_id=1, source_target_pairs={{0,16},{4,20},{8,24},{12,28},{16,32},{20,36},{24,40},{28,44},{32,4... | collective-permute-start | bytes 1572872 | tf_op jit(solution)/shard_map/ppermute | solution.py:26
  33.8 4.3 %collective-permute-start.1 = (bf16[2,256,512]{1,2,0:T(8,128)(2,1)S(1)}, bf16[2,256,512]{1,2,0:T(8,128)(2,1)S(1)}, u32[]{:S(2)}, u32[]{:S(2)}) collective-permute-start(bf16[2,256,512]{1,2,0:T(8,128)(2,1)S(1)} %pad_maximum_fusion), channel_id=1, source_target_pairs={{0,12},{4,16},{8,20},{12,24},{16,28},{20,32},{24,36},{28,40},{32,4... | collective-permute-start | bytes 1572872 | tf_op jit(solution)/shard_map/ppermute | solution.py:26
  38.1 1.3 collective-permute-start.2
  39.5 2.4 %collective-permute-start.3 = (bf16[2,256,512]{1,2,0:T(8,128)(2,1)S(1)}, bf16[2,256,512]{1,2,0:T(8,128)(2,1)S(1)}, u32[]{:S(2)}, u32[]{:S(2)}) collective-permute-start(bf16[2,256,512]{1,2,0:T(8,128)(2,1)S(1)} %pad_maximum_fusion), channel_id=1, source_target_pairs={{0,4},{4,8},{8,12},{12,16},{16,20},{20,24},{24,28},{28,32},{32,36}... | collective-permute-start | bytes 1572872 | tf_op jit(solution)/shard_map/ppermute | solution.py:26
  42.0 1.1 compare_and_fusion
  43.1 1.1 copy.61
  44.8 1.0 pad_maximum_fusion.3
  45.8 1.1 bitcast_dynamic-update-slice_fusion.4
  46.8 5.5 %collective-permute-done.1 = bf16[2,256,512]{1,2,0:T(8,128)(2,1)S(1)} collective-permute-done((bf16[2,256,512]{1,2,0:T(8,128)(2,1)S(1)}, bf16[2,256,512]{1,2,0:T(8,128)(2,1)S(1)}, u32[]{:S(2)}, u32[]{:S(2)}) %collective-permute-start.1) | collective-permute-done | bytes 524320 | tf_op jit(solution)/shard_map/ppermute | solution.py:26
  52.4 11.2 %collective-permute-done.2 = bf16[2,256,512]{1,2,0:T(8,128)(2,1)S(1)} collective-permute-done((bf16[2,256,512]{1,2,0:T(8,128)(2,1)S(1)}, bf16[2,256,512]{1,2,0:T(8,128)(2,1)S(1)}, u32[]{:S(2)}, u32[]{:S(2)}) %collective-permute-start.2) | collective-permute-done | bytes 524320 | tf_op jit(solution)/shard_map/ppermute | solution.py:26
  63.6 9.3 %collective-permute-done.3 = bf16[2,256,512]{1,2,0:T(8,128)(2,1)S(1)} collective-permute-done((bf16[2,256,512]{1,2,0:T(8,128)(2,1)S(1)}, bf16[2,256,512]{1,2,0:T(8,128)(2,1)S(1)}, u32[]{:S(2)}, u32[]{:S(2)}) %collective-permute-start.3) | collective-permute-done | bytes 524320 | tf_op jit(solution)/shard_map/ppermute | solution.py:26
  73.2 1.6 copy.64
  74.8 3.6 %reshape_squeeze.7 = bf16[1280,4,128]{2,1,0:T(4,128)(2,1)} reshape(bf16[1,5,256,512]{3,2,1,0:T(8,128)(2,1)} %copy.64) | data formatting | bytes 2621440 | tf_op jit(solution)/shard_map/reshape;squeeze | solution.py:100
  78.3 0.8 copy.73
  79.2 2.3 reshape.210
  81.5 3.2 %exponential_reduce_fusion = f32[4,256]{1,0:T(4,128)S(1)} fusion(bf16[256,4,128]{2,0,1:T(8,128)(2,1)} %pad_maximum_fusion.3, pred[256,1280]{1,0:T(8,128)(4,1)} %compare_and_fusion, bf16[1280,4,128]{2,1,0:T(4,128)(2,1)S(1)} %copy-done.2), kind=kOutput, calls=%fused_computation.4 | convolution fusion | flops 340788480 | bytes 1904640 | tf_op jit(solution)/shard_map/sub | solution.py:67
  84.7 4.8 %fusion.5 = bf16[4,128,256]{2,1,0:T(8,128)(2,1)} fusion(bf16[1280,4,128]{0,2,1:T(8,128)(2,1)} %reshape.210, f32[4,256]{1,0:T(4,128)S(1)} %exponential_reduce_fusion, bf16[256,4,128]{2,0,1:T(8,128)(2,1)} %pad_maximum_fusion.3, pred[256,1280]{1,0:T(8,128)(4,1)} %compare_and_fusion, bf16[1280,4,128]{2,1,0:T(4,128)(2,1)S(1)} %copy-done.3), kind=kOutput, calls=%fused_computation.11 | convolution fusion | flops 677775616 | bytes 3477504 | tf_op jit(solution)/shard_map/hqk,khd->qhd/dot_general | solution.py:69
  89.6 0.7 all-gather.8.cloned.1.call-update
  90.5 30.6 %all-gather.4.cloned.1.call-done = bf16[256,2048]{0,1:T(8,128)(2,1)} async-done(((bf16[256,512]{0,1:T(8,128)(2,1)}), bf16[256,2048]{0,1:T(8,128)(2,1)}) %all-gather.4.cloned.1.call-update) | async-done | bytes 1048592 | tf_op jit(solution)/shard_map/all_gather | solution.py:106
  122.0 0.7 convolution_convert_fusion
  122.6 0.9 copy.71
  123.5 65.6 %all-gather.8.cloned.1.call-done = bf16[2048,512]{1,0:T(8,128)(2,1)} async-done(((bf16[128,512]{1,0:T(8,128)(2,1)}), bf16[2048,512]{1,0:T(8,128)(2,1)}) %all-gather.8.cloned.1.call-update) | async-done | bytes 2097168 | tf_op jit(solution)/shard_map/all_gather | solution.py:84
  189.1 30.2 %all-gather.6.cloned.1.call-done = bf16[512,2048]{0,1:T(8,128)(2,1)} async-done(((bf16[256,2048]{0,1:T(8,128)(2,1)}), bf16[512,2048]{0,1:T(8,128)(2,1)}) %all-gather.6.cloned.1.call-update) | async-done | bytes 2097168 | tf_op jit(solution)/shard_map/all_gather | solution.py:107
  219.3 3.5 %fusion.4 = bf16[512,512]{1,0:T(8,128)(2,1)S(1)} fusion(bf16[512,2048]{0,1:T(8,128)(2,1)} %all-gather.6.cloned.1.call-done, bf16[2048,512]{1,0:T(8,128)(2,1)} %all-gather.8.cloned.1.call-done, f32[512]{0:T(512)S(1)} %dynamic_slice.7), kind=kOutput, calls=%fused_computation.10 | convolution fusion | flops 1074266112 | bytes 4720640 | tf_op jit(solution)/shard_map/dot_general | solution.py:108
  222.8 4.0 %all_to_all.15 = bf16[2,256,512]{2,1,0:T(8,128)(2,1)S(1)} all-to-all(bf16[2,256,512]{2,1,0:T(8,128)(2,1)S(1)} %bitcast.47), channel_id=1, replica_groups=mesh['z'=16,'x'=4,'core'=2,'head'=4] {'core'}, dimensions={0} | all-to-all | bytes 1048576 | tf_op jit(solution)/shard_map/all_to_all | solution.py:111
  226.8 0.5 copy.67
  227.4 0.9 copy.79
  (59 shorter events, 3.9 us)
Async XLA Ops:
  7.2 113.9 %all-gather.4.cloned.1.call-start = ((), (), s32[]{:S(2)}) async-start(), calls=%async_computation.1 | async-start | bytes 1310720 | tf_op jit(solution)/shard_map/all_gather | solution.py:106
  25.6 4.1 %copy-start.4 = (bf16[256,512]{1,0:T(8,128)(2,1)S(1)}, bf16[256,512]{1,0:T(8,128)(2,1)}, u32[]{:S(2)}) copy-start(bf16[256,512]{1,0:T(8,128)(2,1)} %param.9) | copy-start | bytes 786436
  29.9 43.1 %copy-start = (bf16[256,4,128]{0,2,1:T(8,128)(2,1)}, bf16[256,4,128]{0,2,1:T(8,128)(2,1)S(1)}, u32[]{:S(2)}) copy-start(bf16[256,4,128]{0,2,1:T(8,128)(2,1)S(1)} %maximum_convert_fusion) | copy-start | bytes 786436
  29.9 15.8 %collective-permute-start = (bf16[2,256,512]{1,2,0:T(8,128)(2,1)S(1)}, bf16[2,256,512]{1,2,0:T(8,128)(2,1)}, u32[]{:S(2)}, u32[]{:S(2)}) collective-permute-start(bf16[2,256,512]{1,2,0:T(8,128)(2,1)S(1)} %pad_maximum_fusion), channel_id=1, source_target_pairs={{0,16},{4,20},{8,24},{12,28},{16,32},{20,36},{24,40},{28,44},{32,4... | collective-permute-start | bytes 1572872 | tf_op jit(solution)/shard_map/ppermute | solution.py:26
  33.8 18.5 %collective-permute-start.1 = (bf16[2,256,512]{1,2,0:T(8,128)(2,1)S(1)}, bf16[2,256,512]{1,2,0:T(8,128)(2,1)S(1)}, u32[]{:S(2)}, u32[]{:S(2)}) collective-permute-start(bf16[2,256,512]{1,2,0:T(8,128)(2,1)S(1)} %pad_maximum_fusion), channel_id=1, source_target_pairs={{0,12},{4,16},{8,20},{12,24},{16,28},{20,32},{24,36},{28,40},{32,4... | collective-permute-start | bytes 1572872 | tf_op jit(solution)/shard_map/ppermute | solution.py:26
  38.1 25.4 %collective-permute-start.2 = (bf16[2,256,512]{1,2,0:T(8,128)(2,1)S(1)}, bf16[2,256,512]{1,2,0:T(8,128)(2,1)S(1)}, u32[]{:S(2)}, u32[]{:S(2)}) collective-permute-start(bf16[2,256,512]{1,2,0:T(8,128)(2,1)S(1)} %pad_maximum_fusion), channel_id=1, source_target_pairs={{0,8},{4,12},{8,16},{12,20},{16,24},{20,28},{24,32},{28,36},{32,40... | collective-permute-start | bytes 1572872 | tf_op jit(solution)/shard_map/ppermute | solution.py:26
  39.5 33.4 %collective-permute-start.3 = (bf16[2,256,512]{1,2,0:T(8,128)(2,1)S(1)}, bf16[2,256,512]{1,2,0:T(8,128)(2,1)S(1)}, u32[]{:S(2)}, u32[]{:S(2)}) collective-permute-start(bf16[2,256,512]{1,2,0:T(8,128)(2,1)S(1)} %pad_maximum_fusion), channel_id=1, source_target_pairs={{0,4},{4,8},{8,12},{12,16},{16,20},{20,24},{24,28},{28,32},{32,36}... | collective-permute-start | bytes 1572872 | tf_op jit(solution)/shard_map/ppermute | solution.py:26
  79.2 2.3 copy-start.2
  81.5 3.2 %copy-start.3 = (bf16[1280,4,128]{2,1,0:T(4,128)(2,1)S(1)}, bf16[1280,4,128]{2,1,0:T(4,128)(2,1)}, u32[]{:S(2)}) copy-start(bf16[1280,4,128]{2,1,0:T(4,128)(2,1)} %reshape_squeeze.7) | copy-start | bytes 3932164
  84.7 36.4 %copy-start.1 = (bf16[256,4,128]{0,2,1:T(8,128)(2,1)S(1)}, bf16[256,4,128]{0,2,1:T(8,128)(2,1)}, u32[]{:S(2)}) copy-start(bf16[256,4,128]{0,2,1:T(8,128)(2,1)} %copy-done) | copy-start | bytes 786436
  84.7 36.5 %copy-start.6 = (f32[1024]{0:T(1024)S(1)}, f32[1024]{0:T(1024)}, u32[]{:S(2)}) copy-start(f32[1024]{0:T(1024)} %param.13) | copy-start | bytes 12292
  89.5 32.2 %copy-start.5 = (bf16[256,512]{1,0:T(8,128)(2,1)S(1)}, bf16[256,512]{1,0:T(8,128)(2,1)}, u32[]{:S(2)}) copy-start(bf16[256,512]{1,0:T(8,128)(2,1)} %param.9) | copy-start | bytes 786436
  89.5 32.4 %copy-start.7 = (s32[2]{0:T(128)S(1)}, s32[2]{0:T(128)}, u32[]{:S(2)}) copy-start(s32[2]{0:T(128)} %param.11) | copy-start | bytes 28
  89.5 99.6 %all-gather.8.cloned.1.call-start = ((), (), s32[]{:S(2)}) async-start(), calls=%async_computation.3 | async-start | bytes 2228224 | tf_op jit(solution)/shard_map/all_gather | solution.py:84
  90.3 129.0 %all-gather.6.cloned.1.call-start = ((), (), s32[]{:S(2)}) async-start(), calls=%async_computation.2 | async-start | bytes 3145728 | tf_op jit(solution)/shard_map/all_gather | solution.py:107
Sparse Core Ops, SparseCore 0:
  89.6 31.3 all-gather.3
  123.1 65.8 all-gather.7
  191.2 28.1 all-gather.5

commit v3 on v2

--- a/solution.py
+++ b/solution.py
@@ -24,6 +24,30 @@
     count = lax.axis_size(axis)
     pairs = [(i, i + by) for i in range(count) if 0 <= i + by < count]
     return lax.ppermute(array, axis, pairs)
+
+
+def swapped(array, axis):
+    return lax.ppermute(array, axis, [(0, 1), (1, 0)])
+
+
+def ring_gather(piece, axis):
+    count = lax.axis_size(axis)
+    forward = [(i, (i + 1) % count) for i in range(count)]
+    backward = [(i, (i - 1) % count) for i in range(count)]
+    ahead = [piece]
+    behind = []
+    sent_ahead = piece
+    sent_behind = piece
+    for step in range(1, count // 2 + 1):
+        sent_ahead = lax.ppermute(sent_ahead, axis, forward)
+        behind.append(sent_ahead)
+        if step < count - count // 2:
+            sent_behind = lax.ppermute(sent_behind, axis, backward)
+            ahead.append(sent_behind)
+    relative = jnp.stack(ahead + behind[::-1], axis=0)
+    rank = lax.axis_index(axis)
+    placed = jnp.roll(relative, rank, axis=0)
+    return placed.reshape((count * piece.shape[0],) + piece.shape[1:])
 
 
 def request_info(lengths, token_index):
@@ -77,11 +101,9 @@
     half = out_weight.shape[1] // 2
     weight_pair = lax.all_gather(out_weight, "core", axis=0, tiled=True)
     weight_rows = lax.dynamic_slice_in_dim(weight_pair, core_rank * half, half, 1)
-    weight_rows = lax.all_gather(weight_rows, "x", axis=0, tiled=True)
-    weight_rows, query_proj, key_proj = lax.optimization_barrier(
-        (weight_rows, query_proj, key_proj)
-    )
-    weight_rows = lax.all_gather(weight_rows, "z", axis=0, tiled=True)
+    weight_rows = ring_gather(weight_rows, "x")
+    weight_rows = ring_gather(weight_rows, "z")
+    weight_other = swapped(weight_rows, "core")
     first_token = device_rank * TOK_DEV
     own_tokens = first_token + jnp.arange(TOK_DEV, dtype=jnp.int32)
     request_id, position = request_info(lengths, own_tokens)
@@ -101,16 +123,24 @@
     value_all = value_stack.reshape(key_rows, local_heads, DH)
     key_tokens = first_token - REACH * TOK_DEV + jnp.arange(key_rows, dtype=jnp.int32)
     key_id, _ = request_info(lengths, key_tokens)
+    weight_rows, weight_other, query_rot = lax.optimization_barrier(
+        (weight_rows, weight_other, query_rot)
+    )
     mixed = attend_block(query_rot, key_all, value_all, request_id, own_tokens, key_id, key_tokens)
     heads_out = mixed.reshape(TOK_DEV, local_heads * DH)
-    heads_all = lax.all_gather(heads_out, "head", axis=1, tiled=True)
-    heads_pair = lax.all_gather(heads_all, "core", axis=0, tiled=True)
-    summed = jnp.dot(heads_pair, weight_rows, preferred_element_type=jnp.float32)
-    bias_half = lax.dynamic_slice_in_dim(out_bias, core_rank * half, half, 0)
-    pair_out = (summed + bias_half).astype(jnp.bfloat16)
-    attended = lax.all_to_all(
-        pair_out.reshape(2, TOK_DEV, half), "core", 0, 2, tiled=True
-    ).reshape(TOK_DEV, 2 * half)
+    heads_all = ring_gather(heads_out.T, "head").T
+    other_rank = 1 - core_rank
+    bias_own = lax.dynamic_slice_in_dim(out_bias, core_rank * half, half, 0)
+    bias_other = lax.dynamic_slice_in_dim(out_bias, other_rank * half, half, 0)
+    own_cols = jnp.dot(heads_all, weight_rows, preferred_element_type=jnp.float32) + bias_own
+    other_cols = jnp.dot(heads_all, weight_other, preferred_element_type=jnp.float32) + bias_other
+    own_cols = own_cols.astype(jnp.bfloat16)
+    other_cols = other_cols.astype(jnp.bfloat16)
+    attended = jnp.where(
+        core_rank == 0,
+        jnp.concatenate([own_cols, other_cols], axis=1),
+        jnp.concatenate([other_cols, own_cols], axis=1),
+    )
     local_page = page_table - device_rank * BLK_DEV
     picker = (local_page[:, None] == jnp.arange(BLK_DEV, dtype=jnp.int32)[None, :]).astype(
         jnp.bfloat16

time: 235 us -> 188 us (0.80)
  waiting for transfers between devices: 153 us -> 45.6 us
  starting transfers between devices: 12.2 us -> 98.8 us
  blocking collectives: 22.4 us -> 8.68 us
  between operations: 14.1 us -> 1.65 us
  local copies, waits for them, and re-layouts: 17 us -> 13.8 us
    all_gather x3 -> x0, waiting for transfers between devices: 126 us -> none  [the longest x1 65.6 us: local_body(): weight_rows = lax.all_gather(weight_rows, 'z', axis=0, tiled=True)]
    ppermute x0 -> x22, starting transfers between devices: none -> 80.7 us  [the longest x9 49.6 us: ring_gather(): sent_behind = lax.ppermute(sent_behind, axis, backward)]
    ppermute x0 -> x22, waiting for transfers between devices: none -> 45.5 us  [the longest x12 44.4 us: ring_gather(): sent_ahead = lax.ppermute(sent_ahead, axis, forward)]
    ppermute x4, waiting for transfers between devices: 26 us -> 0.01 us  [passed_along(): return lax.ppermute(array, axis, pairs)]
    all_gather x1 -> x0, blocking collectives: 9.83 us -> none  [local_body(): weight_rows = lax.all_gather(weight_rows, 'x', axis=0, tiled=True)]
    ppermute x4, starting transfers between devices: 11.9 us -> 18.1 us  [passed_along(): return lax.ppermute(array, axis, pairs)]
    all_to_all x1 -> x0, blocking collectives: 4.03 us -> none  [local_body(): lax.all_to_all(pair_out.reshape(2, TOK_DEV, half), 'core', 0, 2, tiled=True)]
    another operation x2 -> x1, local copies, waits for them, and re-layouts: 3.14 us -> 0.33 us  [local_body(): value_all = value_stack.reshape(key_rows, local_heads, DH)]
  transfers between devices with their start and end apart: 7 -> 26, of which waited for: 6 -> 7; matrix products, arithmetic and copies ran while one was open for 3% -> 11% of each run, Pallas kernels for 0% -> 0%
where the time goes in v3:
time: 188 us; the launch traced here: 187 us
  starting transfers between devices  98.8 us (53%)
  waiting for transfers between devices  45.6 us (24%)
  local copies, waits for them, and re-layouts  13.8 us (7%)
  matrix products  12.5 us (7%)
  blocking collectives  8.68 us (5%)
  other arithmetic  5.49 us (3%)
    ppermute x9, starting transfers between devices, ring_gather(): sent_behind = lax.ppermute(sent_behind, axis, backward)  49.6 us
    ppermute x12, waiting for transfers between devices, ring_gather(): sent_ahead = lax.ppermute(sent_ahead, axis, forward)  44.4 us
    ppermute x12, starting transfers between devices, ring_gather(): sent_ahead = lax.ppermute(sent_ahead, axis, forward)  24.4 us
    ppermute x4, starting transfers between devices, passed_along(): return lax.ppermute(array, axis, pairs)  18.1 us
    all_gather x1, blocking collectives, local_body(): weight_pair = lax.all_gather(out_weight, 'core', axis=0, tiled=True)  8.68 us
    ppermute x1, starting transfers between devices, swapped(): return lax.ppermute(array, axis, [(0, 1), (1, 0)])  6.63 us
    unnamed x60, local copies, waits for them, and re-layouts  4.65 us
  transfers between devices with their start and end apart: 26, of which 7 were waited for; matrix products, arithmetic and copies ran while one was open for 11% of the time, Pallas kernels for 0%

profile of v3, /device:TPU:1, one launch (start us, length us, event | category | flops | bytes accessed | tf_op | source)
XLA Modules:
  0.0 186.5 jit_solution(6712904160581017049)
XLA Ops:
  0.6 8.7 %all_gather.3 = bf16[32,1024]{1,0:T(8,128)(2,1)S(1)} all-gather(bf16[16,1024]{1,0:T(8,128)(2,1)} %param.12), channel_id=1, replica_groups=mesh['z'=16,'x'=4,'core'=2,'head'=4] {'core'}, dimensions={0}, use_global_device_ids=true | all-gather | bytes 98304 | tf_op jit(solution)/shard_map/all_gather | solution.py:102
  9.3 1.9 %collective-permute-start.4 = (bf16[32,512]{1,0:T(8,128)(2,1)S(1)}, bf16[32,512]{1,0:T(8,128)(2,1)S(1)}, u32[]{:S(2)}, u32[]{:S(2)}) collective-permute-start(bf16[32,512]{1,0:T(8,128)(2,1)S(1)} %get-tuple-element.19), channel_id=1, source_target_pairs={{0,24},{8,0},{16,8},{24,16},{1,25},{9,1},{17,9},{25,17},{2,26},{10... | collective-permute-start | bytes 98312 | tf_op jit(solution)/shard_map/ppermute | solution.py:45
  11.3 3.4 %collective-permute-start.5 = (bf16[32,512]{1,0:T(8,128)(2,1)S(1)}, bf16[32,512]{1,0:T(8,128)(2,1)S(1)}, u32[]{:S(2)}, u32[]{:S(2)}) collective-permute-start(bf16[32,512]{1,0:T(8,128)(2,1)S(1)} %get-tuple-element.19), channel_id=1, source_target_pairs={{0,8},{8,16},{16,24},{24,0},{1,9},{9,17},{17,25},{25,1},{2,10},{10... | collective-permute-start | bytes 98312 | tf_op jit(solution)/shard_map/ppermute | solution.py:42
  19.3 2.1 %collective-permute-start = (bf16[2,256,512]{2,1,0:T(8,128)(2,1)S(1)}, bf16[2,256,512]{2,1,0:T(8,128)(2,1)}, u32[]{:S(2)}, u32[]{:S(2)}) collective-permute-start(bf16[2,256,512]{2,1,0:T(8,128)(2,1)S(1)} %pad_maximum_fusion), channel_id=1, source_target_pairs={{0,16},{4,20},{8,24},{12,28},{16,32},{20,36},{24,40},{28,44},{32,4... | collective-permute-start | bytes 1572872 | tf_op jit(solution)/shard_map/ppermute | solution.py:26
  21.4 3.3 %collective-permute-start.1 = (bf16[2,256,512]{2,1,0:T(8,128)(2,1)S(1)}, bf16[2,256,512]{2,1,0:T(8,128)(2,1)}, u32[]{:S(2)}, u32[]{:S(2)}) collective-permute-start(bf16[2,256,512]{2,1,0:T(8,128)(2,1)S(1)} %pad_maximum_fusion), channel_id=1, source_target_pairs={{0,12},{4,16},{8,20},{12,24},{16,28},{20,32},{24,36},{28,40},{32,4... | collective-permute-start | bytes 1572872 | tf_op jit(solution)/shard_map/ppermute | solution.py:26
  24.8 2.9 %collective-permute-start.2 = (bf16[2,256,512]{2,1,0:T(8,128)(2,1)S(1)}, bf16[2,256,512]{2,1,0:T(8,128)(2,1)S(1)}, u32[]{:S(2)}, u32[]{:S(2)}) collective-permute-start(bf16[2,256,512]{2,1,0:T(8,128)(2,1)S(1)} %pad_maximum_fusion), channel_id=1, source_target_pairs={{0,8},{4,12},{8,16},{12,20},{16,24},{20,28},{24,32},{28,36},{32,40... | collective-permute-start | bytes 1572872 | tf_op jit(solution)/shard_map/ppermute | solution.py:26
  27.9 1.9 %collective-permute-start.6 = (bf16[32,512]{1,0:T(8,128)(2,1)S(1)}, bf16[32,512]{1,0:T(8,128)(2,1)S(1)}, u32[]{:S(2)}, u32[]{:S(2)}) collective-permute-start(bf16[32,512]{1,0:T(8,128)(2,1)S(1)} %collective-permute-done.5), channel_id=1, source_target_pairs={{0,8},{8,16},{16,24},{24,0},{1,9},{9,17},{17,25},{25,1},{2,10},{10... | collective-permute-start | bytes 98312 | tf_op jit(solution)/shard_map/ppermute | solution.py:42
  29.8 24.6 %collective-permute-done.6 = bf16[32,512]{1,0:T(8,128)(2,1)S(1)} collective-permute-done((bf16[32,512]{1,0:T(8,128)(2,1)S(1)}, bf16[32,512]{1,0:T(8,128)(2,1)S(1)}, u32[]{:S(2)}, u32[]{:S(2)}) %collective-permute-start.6) | collective-permute-done | bytes 32800 | tf_op jit(solution)/shard_map/ppermute | solution.py:42
  54.5 13.1 %collective-permute-start.7 = (bf16[128,512]{1,0:T(8,128)(2,1)S(1)}, bf16[128,512]{1,0:T(8,128)(2,1)S(1)}, u32[]{:S(2)}, u32[]{:S(2)}) collective-permute-start(bf16[128,512]{1,0:T(8,128)(2,1)S(1)} %bitcast.118), channel_id=1, source_target_pairs={{0,480},{32,0},{64,32},{96,64},{128,96},{160,128},{192,160},{224,1... | collective-permute-start | bytes 393224 | tf_op jit(solution)/shard_map/ppermute | solution.py:45
  67.6 1.9 %collective-permute-start.14 = (bf16[128,512]{1,0:T(8,128)(2,1)S(1)}, bf16[128,512]{1,0:T(8,128)(2,1)S(1)}, u32[]{:S(2)}, u32[]{:S(2)}) collective-permute-start(bf16[128,512]{1,0:T(8,128)(2,1)S(1)} %bitcast.119), channel_id=1, source_target_pairs={{0,32},{32,64},{64,96},{96,128},{128,160},{160,192},{192,224},{224... | collective-permute-start | bytes 393224 | tf_op jit(solution)/shard_map/ppermute | solution.py:42
  70.0 5.3 %collective-permute-start.8 = (bf16[128,512]{1,0:T(8,128)(2,1)S(1)}, bf16[128,512]{1,0:T(8,128)(2,1)S(1)}, u32[]{:S(2)}, u32[]{:S(2)}) collective-permute-start(bf16[128,512]{1,0:T(8,128)(2,1)S(1)} %collective-permute-done.7), channel_id=1, source_target_pairs={{0,480},{32,0},{64,32},{96,64},{128,96},{160,128},{192,160},{224,1... | collective-permute-start | bytes 393224 | tf_op jit(solution)/shard_map/ppermute | solution.py:45
  75.3 1.9 %collective-permute-start.15 = (bf16[128,512]{1,0:T(8,128)(2,1)S(1)}, bf16[128,512]{1,0:T(8,128)(2,1)S(1)}, u32[]{:S(2)}, u32[]{:S(2)}) collective-permute-start(bf16[128,512]{1,0:T(8,128)(2,1)S(1)} %collective-permute-done.14), channel_id=1, source_target_pairs={{0,32},{32,64},{64,96},{96,128},{128,160},{160,192},{192,224},{224... | collective-permute-start | bytes 393224 | tf_op jit(solution)/shard_map/ppermute | solution.py:42
  77.2 4.9 %collective-permute-start.9 = (bf16[128,512]{1,0:T(8,128)(2,1)S(1)}, bf16[128,512]{1,0:T(8,128)(2,1)S(1)}, u32[]{:S(2)}, u32[]{:S(2)}) collective-permute-start(bf16[128,512]{1,0:T(8,128)(2,1)S(1)} %collective-permute-done.8), channel_id=1, source_target_pairs={{0,480},{32,0},{64,32},{96,64},{128,96},{160,128},{192,160},{224,1... | collective-permute-start | bytes 393224 | tf_op jit(solution)/shard_map/ppermute | solution.py:45
  82.2 1.9 %collective-permute-start.16 = (bf16[128,512]{1,0:T(8,128)(2,1)S(1)}, bf16[128,512]{1,0:T(8,128)(2,1)S(1)}, u32[]{:S(2)}, u32[]{:S(2)}) collective-permute-start(bf16[128,512]{1,0:T(8,128)(2,1)S(1)} %collective-permute-done.15), channel_id=1, source_target_pairs={{0,32},{32,64},{64,96},{96,128},{128,160},{160,192},{192,224},{224... | collective-permute-start | bytes 393224 | tf_op jit(solution)/shard_map/ppermute | solution.py:42
  84.2 4.9 %collective-permute-start.10 = (bf16[128,512]{1,0:T(8,128)(2,1)S(1)}, bf16[128,512]{1,0:T(8,128)(2,1)S(1)}, u32[]{:S(2)}, u32[]{:S(2)}) collective-permute-start(bf16[128,512]{1,0:T(8,128)(2,1)S(1)} %collective-permute-done.9), channel_id=1, source_target_pairs={{0,480},{32,0},{64,32},{96,64},{128,96},{160,128},{192,160},{224,1... | collective-permute-start | bytes 393224 | tf_op jit(solution)/shard_map/ppermute | solution.py:45
  89.1 1.9 %collective-permute-start.17 = (bf16[128,512]{1,0:T(8,128)(2,1)S(1)}, bf16[128,512]{1,0:T(8,128)(2,1)S(1)}, u32[]{:S(2)}, u32[]{:S(2)}) collective-permute-start(bf16[128,512]{1,0:T(8,128)(2,1)S(1)} %collective-permute-done.16), channel_id=1, source_target_pairs={{0,32},{32,64},{64,96},{96,128},{128,160},{160,192},{192,224},{224... | collective-permute-start | bytes 393224 | tf_op jit(solution)/shard_map/ppermute | solution.py:42
  91.1 4.9 %collective-permute-start.11 = (bf16[128,512]{1,0:T(8,128)(2,1)S(1)}, bf16[128,512]{1,0:T(8,128)(2,1)S(1)}, u32[]{:S(2)}, u32[]{:S(2)}) collective-permute-start(bf16[128,512]{1,0:T(8,128)(2,1)S(1)} %collective-permute-done.10), channel_id=1, source_target_pairs={{0,480},{32,0},{64,32},{96,64},{128,96},{160,128},{192,160},{224,1... | collective-permute-start | bytes 393224 | tf_op jit(solution)/shard_map/ppermute | solution.py:45
  96.0 1.9 %collective-permute-start.18 = (bf16[128,512]{1,0:T(8,128)(2,1)S(1)}, bf16[128,512]{1,0:T(8,128)(2,1)S(1)}, u32[]{:S(2)}, u32[]{:S(2)}) collective-permute-start(bf16[128,512]{1,0:T(8,128)(2,1)S(1)} %collective-permute-done.17), channel_id=1, source_target_pairs={{0,32},{32,64},{64,96},{96,128},{128,160},{160,192},{192,224},{224... | collective-permute-start | bytes 393224 | tf_op jit(solution)/shard_map/ppermute | solution.py:42
  98.0 4.9 %collective-permute-start.12 = (bf16[128,512]{1,0:T(8,128)(2,1)S(1)}, bf16[128,512]{1,0:T(8,128)(2,1)S(1)}, u32[]{:S(2)}, u32[]{:S(2)}) collective-permute-start(bf16[128,512]{1,0:T(8,128)(2,1)S(1)} %collective-permute-done.11), channel_id=1, source_target_pairs={{0,480},{32,0},{64,32},{96,64},{128,96},{160,128},{192,160},{224,1... | collective-permute-start | bytes 393224 | tf_op jit(solution)/shard_map/ppermute | solution.py:45
  104.9 4.9 %collective-permute-start.13 = (bf16[128,512]{1,0:T(8,128)(2,1)S(1)}, bf16[128,512]{1,0:T(8,128)(2,1)S(1)}, u32[]{:S(2)}, u32[]{:S(2)}) collective-permute-start(bf16[128,512]{1,0:T(8,128)(2,1)S(1)} %collective-permute-done.12), channel_id=1, source_target_pairs={{0,480},{32,0},{64,32},{96,64},{128,96},{160,128},{192,160},{224,1... | collective-permute-start | bytes 393224 | tf_op jit(solution)/shard_map/ppermute | solution.py:45
  112.6 9.7 %collective-permute-start.3 = (bf16[2,256,512]{2,1,0:T(8,128)(2,1)S(1)}, bf16[2,256,512]{2,1,0:T(8,128)(2,1)}, u32[]{:S(2)}, u32[]{:S(2)}) collective-permute-start(bf16[2,256,512]{2,1,0:T(8,128)(2,1)S(1)} %pad_maximum_fusion), channel_id=1, source_target_pairs={{0,4},{4,8},{8,12},{12,16},{16,20},{20,24},{24,28},{28,32},{32,36}... | collective-permute-start | bytes 1572872 | tf_op jit(solution)/shard_map/ppermute | solution.py:26
  122.4 1.9 %collective-permute-start.21 = (bf16[128,512]{1,0:T(8,128)(2,1)S(1)}, bf16[128,512]{1,0:T(8,128)(2,1)S(1)}, u32[]{:S(2)}, u32[]{:S(2)}) collective-permute-start(bf16[128,512]{1,0:T(8,128)(2,1)S(1)} %collective-permute-done.20), channel_id=1, source_target_pairs={{0,32},{32,64},{64,96},{96,128},{128,160},{160,192},{192,224},{224... | collective-permute-start | bytes 393224 | tf_op jit(solution)/shard_map/ppermute | solution.py:42
  124.3 5.7 %collective-permute-done.21 = bf16[128,512]{1,0:T(8,128)(2,1)S(1)} collective-permute-done((bf16[128,512]{1,0:T(8,128)(2,1)S(1)}, bf16[128,512]{1,0:T(8,128)(2,1)S(1)}, u32[]{:S(2)}, u32[]{:S(2)}) %collective-permute-start.21) | collective-permute-done | bytes 131104 | tf_op jit(solution)/shard_map/ppermute | solution.py:42
  132.0 6.6 %collective-permute-start.22 = (bf16[2048,512]{1,0:T(8,128)(2,1)}, bf16[2048,512]{1,0:T(8,128)(2,1)}, u32[]{:S(2)}, u32[]{:S(2)}) collective-permute-start(bf16[2048,512]{1,0:T(8,128)(2,1)} %bitcast.28), channel_id=1, source_target_pairs={{0,4},{4,0},{1,5},{5,1},{2,6},{6,2},{3,7},{7,3},{8,12},{12,8},{9,1... | collective-permute-start | bytes 6291464 | tf_op jit(solution)/shard_map/ppermute | solution.py:30
  149.3 3.4 %exponential_reduce_fusion = f32[4,256]{1,0:T(4,128)S(1)} fusion(pred[256,1280]{1,0:T(8,128)(4,1)S(1)} %compare_and_fusion, bf16[1280,4,128]{2,1,0:T(4,128)(2,1)} %reshape_squeeze.7, bf16[256,4,128]{2,1,0:T(4,128)(2,1)S(1)} %copy-done.2), kind=kOutput, calls=%fused_computation.4 | convolution fusion | flops 340788480 | bytes 1904640 | tf_op jit(solution)/shard_map/sub | solution.py:91
  152.7 2.8 %fusion.7 = bf16[4,128,256]{2,1,0:T(8,128)(2,1)S(1)} fusion(f32[4,256]{1,0:T(4,128)S(1)} %exponential_reduce_fusion, bf16[1280,4,128]{2,1,0:T(4,128)(2,1)S(1)} %reshape_squeeze.6, pred[256,1280]{1,0:T(8,128)(4,1)S(1)} %compare_and_fusion, bf16[1280,4,128]{2,1,0:T(4,128)(2,1)S(1)} %copy-done.1, bf16[256,4,128]{2,1,0:T(4,128)(2,1)S(1)} %copy-done.2), kind=kOutput, calls=%fused_computation.14 | convolution fusion | flops 677775616 | bytes 3477504 | tf_op jit(solution)/shard_map/hqk,khd->qhd/dot_general | solution.py:93
  155.6 4.7 %collective-permute-start.23 = (bf16[512,256]{1,0:T(8,128)(2,1)S(1)}, bf16[512,256]{1,0:T(8,128)(2,1)S(1)}, u32[]{:S(2)}, u32[]{:S(2)}) collective-permute-start(bf16[512,256]{1,0:T(8,128)(2,1)S(1)} %bitcast.124), channel_id=1, source_target_pairs={{0,3},{1,0},{2,1},{3,2},{4,7},{5,4},{6,5},{7,6},{8,11},{9,8},{10,9... | collective-permute-start | bytes 786440 | tf_op jit(solution)/shard_map/ppermute | solution.py:45
  160.2 1.9 %collective-permute-start.24 = (bf16[512,256]{1,0:T(8,128)(2,1)S(1)}, bf16[512,256]{1,0:T(8,128)(2,1)S(1)}, u32[]{:S(2)}, u32[]{:S(2)}) collective-permute-start(bf16[512,256]{1,0:T(8,128)(2,1)S(1)} %bitcast.125), channel_id=1, source_target_pairs={{0,1},{1,2},{2,3},{3,0},{4,5},{5,6},{6,7},{7,4},{8,9},{9,10},{10,1... | collective-permute-start | bytes 786440 | tf_op jit(solution)/shard_map/ppermute | solution.py:42
  164.8 6.1 %collective-permute-done.24 = bf16[512,256]{1,0:T(8,128)(2,1)S(1)} collective-permute-done((bf16[512,256]{1,0:T(8,128)(2,1)S(1)}, bf16[512,256]{1,0:T(8,128)(2,1)S(1)}, u32[]{:S(2)}, u32[]{:S(2)}) %collective-permute-start.24) | collective-permute-done | bytes 262176 | tf_op jit(solution)/shard_map/ppermute | solution.py:42
  172.9 7.8 %collective-permute-done.25 = bf16[512,256]{1,0:T(8,128)(2,1)S(1)} collective-permute-done((bf16[512,256]{1,0:T(8,128)(2,1)S(1)}, bf16[512,256]{1,0:T(8,128)(2,1)S(1)}, u32[]{:S(2)}, u32[]{:S(2)}) %collective-permute-start.25) | collective-permute-done | bytes 262176 | tf_op jit(solution)/shard_map/ppermute | solution.py:42
  180.9 2.3 %fusion.5 = bf16[256,512]{1,0:T(8,128)(2,1)S(1)} fusion(bf16[2048,256]{1,0:T(8,128)(2,1)S(1)} %bitcast.122, bf16[2048,512]{1,0:T(8,128)(2,1)} %bitcast.28, f32[512]{0:T(512)S(1)} %get-tuple-element.26), kind=kOutput, calls=%fused_computation.12 | convolution fusion | flops 537133056 | bytes 3409920 | tf_op jit(solution)/shard_map/dot_general | solution.py:135
  183.3 2.3 %fusion.6 = bf16[256,512]{1,0:T(8,128)(2,1)S(1)} fusion(bf16[2048,256]{1,0:T(8,128)(2,1)S(1)} %bitcast.123, bf16[2048,512]{1,0:T(8,128)(2,1)} %collective-permute-done.22, f32[512]{0:T(512)S(1)} %get-tuple-element.27), kind=kOutput, calls=%fused_computation.13 | convolution fusion | flops 537133056 | bytes 3409920 | tf_op jit(solution)/shard_map/dot_general | solution.py:136
  (129 shorter events, 28.1 us)
Async XLA Ops:
  0.6 18.6 %copy-start = (bf16[256,512]{1,0:T(8,128)(2,1)S(1)}, bf16[256,512]{1,0:T(8,128)(2,1)}, u32[]{:S(2)}) copy-start(bf16[256,512]{1,0:T(8,128)(2,1)} %param.9) | copy-start | bytes 786436
  9.3 20.5 %collective-permute-start.4 = (bf16[32,512]{1,0:T(8,128)(2,1)S(1)}, bf16[32,512]{1,0:T(8,128)(2,1)S(1)}, u32[]{:S(2)}, u32[]{:S(2)}) collective-permute-start(bf16[32,512]{1,0:T(8,128)(2,1)S(1)} %get-tuple-element.19), channel_id=1, source_target_pairs={{0,24},{8,0},{16,8},{24,16},{1,25},{9,1},{17,9},{25,17},{2,26},{10... | collective-permute-start | bytes 98312 | tf_op jit(solution)/shard_map/ppermute | solution.py:45
  11.3 16.6 %collective-permute-start.5 = (bf16[32,512]{1,0:T(8,128)(2,1)S(1)}, bf16[32,512]{1,0:T(8,128)(2,1)S(1)}, u32[]{:S(2)}, u32[]{:S(2)}) collective-permute-start(bf16[32,512]{1,0:T(8,128)(2,1)S(1)} %get-tuple-element.19), channel_id=1, source_target_pairs={{0,8},{8,16},{16,24},{24,0},{1,9},{9,17},{17,25},{25,1},{2,10},{10... | collective-permute-start | bytes 98312 | tf_op jit(solution)/shard_map/ppermute | solution.py:42
  19.3 124.8 %collective-permute-start = (bf16[2,256,512]{2,1,0:T(8,128)(2,1)S(1)}, bf16[2,256,512]{2,1,0:T(8,128)(2,1)}, u32[]{:S(2)}, u32[]{:S(2)}) collective-permute-start(bf16[2,256,512]{2,1,0:T(8,128)(2,1)S(1)} %pad_maximum_fusion), channel_id=1, source_target_pairs={{0,16},{4,20},{8,24},{12,28},{16,32},{20,36},{24,40},{28,44},{32,4... | collective-permute-start | bytes 1572872 | tf_op jit(solution)/shard_map/ppermute | solution.py:26
  21.4 123.8 %collective-permute-start.1 = (bf16[2,256,512]{2,1,0:T(8,128)(2,1)S(1)}, bf16[2,256,512]{2,1,0:T(8,128)(2,1)}, u32[]{:S(2)}, u32[]{:S(2)}) collective-permute-start(bf16[2,256,512]{2,1,0:T(8,128)(2,1)S(1)} %pad_maximum_fusion), channel_id=1, source_target_pairs={{0,12},{4,16},{8,20},{12,24},{16,28},{20,32},{24,36},{28,40},{32,4... | collective-permute-start | bytes 1572872 | tf_op jit(solution)/shard_map/ppermute | solution.py:26
  24.8 121.6 %collective-permute-start.2 = (bf16[2,256,512]{2,1,0:T(8,128)(2,1)S(1)}, bf16[2,256,512]{2,1,0:T(8,128)(2,1)S(1)}, u32[]{:S(2)}, u32[]{:S(2)}) collective-permute-start(bf16[2,256,512]{2,1,0:T(8,128)(2,1)S(1)} %pad_maximum_fusion), channel_id=1, source_target_pairs={{0,8},{4,12},{8,16},{12,20},{16,24},{20,28},{24,32},{28,36},{32,40... | collective-permute-start | bytes 1572872 | tf_op jit(solution)/shard_map/ppermute | solution.py:26
  27.9 26.6 %collective-permute-start.6 = (bf16[32,512]{1,0:T(8,128)(2,1)S(1)}, bf16[32,512]{1,0:T(8,128)(2,1)S(1)}, u32[]{:S(2)}, u32[]{:S(2)}) collective-permute-start(bf16[32,512]{1,0:T(8,128)(2,1)S(1)} %collective-permute-done.5), channel_id=1, source_target_pairs={{0,8},{8,16},{16,24},{24,0},{1,9},{9,17},{17,25},{25,1},{2,10},{10... | collective-permute-start | bytes 98312 | tf_op jit(solution)/shard_map/ppermute | solution.py:42
  54.5 15.4 %collective-permute-start.7 = (bf16[128,512]{1,0:T(8,128)(2,1)S(1)}, bf16[128,512]{1,0:T(8,128)(2,1)S(1)}, u32[]{:S(2)}, u32[]{:S(2)}) collective-permute-start(bf16[128,512]{1,0:T(8,128)(2,1)S(1)} %bitcast.118), channel_id=1, source_target_pairs={{0,480},{32,0},{64,32},{96,64},{128,96},{160,128},{192,160},{224,1... | collective-permute-start | bytes 393224 | tf_op jit(solution)/shard_map/ppermute | solution.py:45
  67.6 7.7 %collective-permute-start.14 = (bf16[128,512]{1,0:T(8,128)(2,1)S(1)}, bf16[128,512]{1,0:T(8,128)(2,1)S(1)}, u32[]{:S(2)}, u32[]{:S(2)}) collective-permute-start(bf16[128,512]{1,0:T(8,128)(2,1)S(1)} %bitcast.119), channel_id=1, source_target_pairs={{0,32},{32,64},{64,96},{96,128},{128,160},{160,192},{192,224},{224... | collective-permute-start | bytes 393224 | tf_op jit(solution)/shard_map/ppermute | solution.py:42
  70.0 7.3 %collective-permute-start.8 = (bf16[128,512]{1,0:T(8,128)(2,1)S(1)}, bf16[128,512]{1,0:T(8,128)(2,1)S(1)}, u32[]{:S(2)}, u32[]{:S(2)}) collective-permute-start(bf16[128,512]{1,0:T(8,128)(2,1)S(1)} %collective-permute-done.7), channel_id=1, source_target_pairs={{0,480},{32,0},{64,32},{96,64},{128,96},{160,128},{192,160},{224,1... | collective-permute-start | bytes 393224 | tf_op jit(solution)/shard_map/ppermute | solution.py:45
  75.3 6.9 %collective-permute-start.15 = (bf16[128,512]{1,0:T(8,128)(2,1)S(1)}, bf16[128,512]{1,0:T(8,128)(2,1)S(1)}, u32[]{:S(2)}, u32[]{:S(2)}) collective-permute-start(bf16[128,512]{1,0:T(8,128)(2,1)S(1)} %collective-permute-done.14), channel_id=1, source_target_pairs={{0,32},{32,64},{64,96},{96,128},{128,160},{160,192},{192,224},{224... | collective-permute-start | bytes 393224 | tf_op jit(solution)/shard_map/ppermute | solution.py:42
  77.2 6.9 %collective-permute-start.9 = (bf16[128,512]{1,0:T(8,128)(2,1)S(1)}, bf16[128,512]{1,0:T(8,128)(2,1)S(1)}, u32[]{:S(2)}, u32[]{:S(2)}) collective-permute-start(bf16[128,512]{1,0:T(8,128)(2,1)S(1)} %collective-permute-done.8), channel_id=1, source_target_pairs={{0,480},{32,0},{64,32},{96,64},{128,96},{160,128},{192,160},{224,1... | collective-permute-start | bytes 393224 | tf_op jit(solution)/shard_map/ppermute | solution.py:45
  82.2 6.9 %collective-permute-start.16 = (bf16[128,512]{1,0:T(8,128)(2,1)S(1)}, bf16[128,512]{1,0:T(8,128)(2,1)S(1)}, u32[]{:S(2)}, u32[]{:S(2)}) collective-permute-start(bf16[128,512]{1,0:T(8,128)(2,1)S(1)} %collective-permute-done.15), channel_id=1, source_target_pairs={{0,32},{32,64},{64,96},{96,128},{128,160},{160,192},{192,224},{224... | collective-permute-start | bytes 393224 | tf_op jit(solution)/shard_map/ppermute | solution.py:42
  84.2 6.9 %collective-permute-start.10 = (bf16[128,512]{1,0:T(8,128)(2,1)S(1)}, bf16[128,512]{1,0:T(8,128)(2,1)S(1)}, u32[]{:S(2)}, u32[]{:S(2)}) collective-permute-start(bf16[128,512]{1,0:T(8,128)(2,1)S(1)} %collective-permute-done.9), channel_id=1, source_target_pairs={{0,480},{32,0},{64,32},{96,64},{128,96},{160,128},{192,160},{224,1... | collective-permute-start | bytes 393224 | tf_op jit(solution)/shard_map/ppermute | solution.py:45
  89.1 6.9 %collective-permute-start.17 = (bf16[128,512]{1,0:T(8,128)(2,1)S(1)}, bf16[128,512]{1,0:T(8,128)(2,1)S(1)}, u32[]{:S(2)}, u32[]{:S(2)}) collective-permute-start(bf16[128,512]{1,0:T(8,128)(2,1)S(1)} %collective-permute-done.16), channel_id=1, source_target_pairs={{0,32},{32,64},{64,96},{96,128},{128,160},{160,192},{192,224},{224... | collective-permute-start | bytes 393224 | tf_op jit(solution)/shard_map/ppermute | solution.py:42
  91.1 6.9 %collective-permute-start.11 = (bf16[128,512]{1,0:T(8,128)(2,1)S(1)}, bf16[128,512]{1,0:T(8,128)(2,1)S(1)}, u32[]{:S(2)}, u32[]{:S(2)}) collective-permute-start(bf16[128,512]{1,0:T(8,128)(2,1)S(1)} %collective-permute-done.10), channel_id=1, source_target_pairs={{0,480},{32,0},{64,32},{96,64},{128,96},{160,128},{192,160},{224,1... | collective-permute-start | bytes 393224 | tf_op jit(solution)/shard_map/ppermute | solution.py:45
  96.0 6.9 %collective-permute-start.18 = (bf16[128,512]{1,0:T(8,128)(2,1)S(1)}, bf16[128,512]{1,0:T(8,128)(2,1)S(1)}, u32[]{:S(2)}, u32[]{:S(2)}) collective-permute-start(bf16[128,512]{1,0:T(8,128)(2,1)S(1)} %collective-permute-done.17), channel_id=1, source_target_pairs={{0,32},{32,64},{64,96},{96,128},{128,160},{160,192},{192,224},{224... | collective-permute-start | bytes 393224 | tf_op jit(solution)/shard_map/ppermute | solution.py:42
  98.0 6.9 %collective-permute-start.12 = (bf16[128,512]{1,0:T(8,128)(2,1)S(1)}, bf16[128,512]{1,0:T(8,128)(2,1)S(1)}, u32[]{:S(2)}, u32[]{:S(2)}) collective-permute-start(bf16[128,512]{1,0:T(8,128)(2,1)S(1)} %collective-permute-done.11), channel_id=1, source_target_pairs={{0,480},{32,0},{64,32},{96,64},{128,96},{160,128},{192,160},{224,1... | collective-permute-start | bytes 393224 | tf_op jit(solution)/shard_map/ppermute | solution.py:45
  102.9 6.9 %collective-permute-start.19 = (bf16[128,512]{1,0:T(8,128)(2,1)S(1)}, bf16[128,512]{1,0:T(8,128)(2,1)S(1)}, u32[]{:S(2)}, u32[]{:S(2)}) collective-permute-start(bf16[128,512]{1,0:T(8,128)(2,1)S(1)} %collective-permute-done.18), channel_id=1, source_target_pairs={{0,32},{32,64},{64,96},{96,128},{128,160},{160,192},{192,224},{224... | collective-permute-start | bytes 393224 | tf_op jit(solution)/shard_map/ppermute | solution.py:42
  104.9 7.7 %collective-permute-start.13 = (bf16[128,512]{1,0:T(8,128)(2,1)S(1)}, bf16[128,512]{1,0:T(8,128)(2,1)S(1)}, u32[]{:S(2)}, u32[]{:S(2)}) collective-permute-start(bf16[128,512]{1,0:T(8,128)(2,1)S(1)} %collective-permute-done.12), channel_id=1, source_target_pairs={{0,480},{32,0},{64,32},{96,64},{128,96},{160,128},{192,160},{224,1... | collective-permute-start | bytes 393224 | tf_op jit(solution)/shard_map/ppermute | solution.py:45
  109.9 12.5 %collective-permute-start.20 = (bf16[128,512]{1,0:T(8,128)(2,1)S(1)}, bf16[128,512]{1,0:T(8,128)(2,1)S(1)}, u32[]{:S(2)}, u32[]{:S(2)}) collective-permute-start(bf16[128,512]{1,0:T(8,128)(2,1)S(1)} %collective-permute-done.19), channel_id=1, source_target_pairs={{0,32},{32,64},{64,96},{96,128},{128,160},{160,192},{192,224},{224... | collective-permute-start | bytes 393224 | tf_op jit(solution)/shard_map/ppermute | solution.py:42
  112.6 33.8 %collective-permute-start.3 = (bf16[2,256,512]{2,1,0:T(8,128)(2,1)S(1)}, bf16[2,256,512]{2,1,0:T(8,128)(2,1)}, u32[]{:S(2)}, u32[]{:S(2)}) collective-permute-start(bf16[2,256,512]{2,1,0:T(8,128)(2,1)S(1)} %pad_maximum_fusion), channel_id=1, source_target_pairs={{0,4},{4,8},{8,12},{12,16},{16,20},{20,24},{24,28},{28,32},{32,36}... | collective-permute-start | bytes 1572872 | tf_op jit(solution)/shard_map/ppermute | solution.py:26
  122.4 7.6 %collective-permute-start.21 = (bf16[128,512]{1,0:T(8,128)(2,1)S(1)}, bf16[128,512]{1,0:T(8,128)(2,1)S(1)}, u32[]{:S(2)}, u32[]{:S(2)}) collective-permute-start(bf16[128,512]{1,0:T(8,128)(2,1)S(1)} %collective-permute-done.20), channel_id=1, source_target_pairs={{0,32},{32,64},{64,96},{96,128},{128,160},{160,192},{192,224},{224... | collective-permute-start | bytes 393224 | tf_op jit(solution)/shard_map/ppermute | solution.py:42
  130.4 10.3 %copy-start.4 = (s32[2]{0:T(128)S(1)}, s32[2]{0:T(128)}, u32[]{:S(2)}) copy-start(s32[2]{0:T(128)} %param.11) | copy-start | bytes 28
  132.0 17.3 %collective-permute-start.22 = (bf16[2048,512]{1,0:T(8,128)(2,1)}, bf16[2048,512]{1,0:T(8,128)(2,1)}, u32[]{:S(2)}, u32[]{:S(2)}) collective-permute-start(bf16[2048,512]{1,0:T(8,128)(2,1)} %bitcast.28), channel_id=1, source_target_pairs={{0,4},{4,0},{1,5},{5,1},{2,6},{6,2},{3,7},{7,3},{8,12},{12,8},{9,1... | collective-permute-start | bytes 6291464 | tf_op jit(solution)/shard_map/ppermute | solution.py:30
  147.5 1.8 copy-start.2
  149.3 3.4 %copy-start.1 = (bf16[1280,4,128]{2,1,0:T(4,128)(2,1)S(1)}, bf16[1280,4,128]{2,1,0:T(4,128)(2,1)}, u32[]{:S(2)}) copy-start(bf16[1280,4,128]{2,1,0:T(4,128)(2,1)} %reshape_squeeze.7) | copy-start | bytes 3932164
  155.5 9.2 %copy-start.3 = (f32[1024]{0:T(1024)S(1)}, f32[1024]{0:T(1024)}, u32[]{:S(2)}) copy-start(f32[1024]{0:T(1024)} %param.13) | copy-start | bytes 12292
  155.6 17.3 %collective-permute-start.23 = (bf16[512,256]{1,0:T(8,128)(2,1)S(1)}, bf16[512,256]{1,0:T(8,128)(2,1)S(1)}, u32[]{:S(2)}, u32[]{:S(2)}) collective-permute-start(bf16[512,256]{1,0:T(8,128)(2,1)S(1)} %bitcast.124), channel_id=1, source_target_pairs={{0,3},{1,0},{2,1},{3,2},{4,7},{5,4},{6,5},{7,6},{8,11},{9,8},{10,9... | collective-permute-start | bytes 786440 | tf_op jit(solution)/shard_map/ppermute | solution.py:45
  160.2 10.7 %collective-permute-start.24 = (bf16[512,256]{1,0:T(8,128)(2,1)S(1)}, bf16[512,256]{1,0:T(8,128)(2,1)S(1)}, u32[]{:S(2)}, u32[]{:S(2)}) collective-permute-start(bf16[512,256]{1,0:T(8,128)(2,1)S(1)} %bitcast.125), channel_id=1, source_target_pairs={{0,1},{1,2},{2,3},{3,0},{4,5},{5,6},{6,7},{7,4},{8,9},{9,10},{10,1... | collective-permute-start | bytes 786440 | tf_op jit(solution)/shard_map/ppermute | solution.py:42
  170.9 9.8 %collective-permute-start.25 = (bf16[512,256]{1,0:T(8,128)(2,1)S(1)}, bf16[512,256]{1,0:T(8,128)(2,1)S(1)}, u32[]{:S(2)}, u32[]{:S(2)}) collective-permute-start(bf16[512,256]{1,0:T(8,128)(2,1)S(1)} %collective-permute-done.24), channel_id=1, source_target_pairs={{0,1},{1,2},{2,3},{3,0},{4,5},{5,6},{6,7},{7,4},{8,9},{9,10},{10,1... | collective-permute-start | bytes 786440 | tf_op jit(solution)/shard_map/ppermute | solution.py:42

commit v4 on v2

--- a/solution.py
+++ b/solution.py
@@ -82,6 +82,7 @@
         (weight_rows, query_proj, key_proj)
     )
     weight_rows = lax.all_gather(weight_rows, "z", axis=0, tiled=True)
+    weight_other = lax.ppermute(weight_rows, "core", [(0, 1), (1, 0)])
     first_token = device_rank * TOK_DEV
     own_tokens = first_token + jnp.arange(TOK_DEV, dtype=jnp.int32)
     request_id, position = request_info(lengths, own_tokens)
@@ -104,13 +105,18 @@
     mixed = attend_block(query_rot, key_all, value_all, request_id, own_tokens, key_id, key_tokens)
     heads_out = mixed.reshape(TOK_DEV, local_heads * DH)
     heads_all = lax.all_gather(heads_out, "head", axis=1, tiled=True)
-    heads_pair = lax.all_gather(heads_all, "core", axis=0, tiled=True)
-    summed = jnp.dot(heads_pair, weight_rows, preferred_element_type=jnp.float32)
-    bias_half = lax.dynamic_slice_in_dim(out_bias, core_rank * half, half, 0)
-    pair_out = (summed + bias_half).astype(jnp.bfloat16)
-    attended = lax.all_to_all(
-        pair_out.reshape(2, TOK_DEV, half), "core", 0, 2, tiled=True
-    ).reshape(TOK_DEV, 2 * half)
+    other_rank = 1 - core_rank
+    bias_own = lax.dynamic_slice_in_dim(out_bias, core_rank * half, half, 0)
+    bias_other = lax.dynamic_slice_in_dim(out_bias, other_rank * half, half, 0)
+    own_cols = jnp.dot(heads_all, weight_rows, preferred_element_type=jnp.float32) + bias_own
+    other_cols = jnp.dot(heads_all, weight_other, preferred_element_type=jnp.float32) + bias_other
+    own_cols = own_cols.astype(jnp.bfloat16)
+    other_cols = other_cols.astype(jnp.bfloat16)
+    attended = jnp.where(
+        core_rank == 0,
+        jnp.concatenate([own_cols, other_cols], axis=1),
+        jnp.concatenate([other_cols, own_cols], axis=1),
+    )
     local_page = page_table - device_rank * BLK_DEV
     picker = (local_page[:, None] == jnp.arange(BLK_DEV, dtype=jnp.int32)[None, :]).astype(
         jnp.bfloat16

time: 235 us -> 159 us (0.68)
  waiting for transfers between devices: 153 us -> 66.1 us
  starting transfers between devices: 12.2 us -> 23.6 us
  blocking collectives: 22.4 us -> 18.4 us
    all_gather x1, waiting for transfers between devices: 65.6 us -> 6.27 us  [local_body(): weight_rows = lax.all_gather(weight_rows, 'z', axis=0, tiled=True)]
    all_gather x1 -> x0, waiting for transfers between devices: 30.2 us -> none  [local_body(): heads_pair = lax.all_gather(heads_all, 'core', axis=0, tiled=True)]
    ppermute x0 -> x1, starting transfers between devices: none -> 11.6 us  [local_body(): weight_other = lax.ppermute(weight_rows, 'core', [(0, 1), (1, 0)])]
    all_to_all x1 -> x0, blocking collectives: 4.03 us -> none  [local_body(): lax.all_to_all(pair_out.reshape(2, TOK_DEV, half), 'core', 0, 2, tiled=True)]
    all_gather x1, waiting for transfers between devices: 30.6 us -> 33.8 us  [local_body(): heads_all = lax.all_gather(heads_out, 'head', axis=1, tiled=True)]
  transfers between devices with their start and end apart: 7 -> 7, of which waited for: 6 -> 5; matrix products, arithmetic and copies ran while one was open for 3% -> 19% of each run, Pallas kernels for 0% -> 0%
where the time goes in v4:
time: 159 us; the launch traced here: 157 us
  waiting for transfers between devices  66.1 us (42%)
  starting transfers between devices  23.6 us (15%)
  blocking collectives  18.4 us (12%)
  between operations  15.9 us (10%)
  local copies, waits for them, and re-layouts  15.6 us (10%)
  matrix products  12.9 us (8%)
  other arithmetic  4.74 us (3%)
    all_gather x1, waiting for transfers between devices, local_body(): heads_all = lax.all_gather(heads_out, 'head', axis=1, tiled=True)  33.8 us
    ppermute x4, waiting for transfers between devices, passed_along(): return lax.ppermute(array, axis, pairs)  26 us
    ppermute x4, starting transfers between devices, passed_along(): return lax.ppermute(array, axis, pairs)  11.9 us
    ppermute x1, starting transfers between devices, local_body(): weight_other = lax.ppermute(weight_rows, 'core', [(0, 1), (1, 0)])  11.6 us
    all_gather x1, blocking collectives, local_body(): weight_rows = lax.all_gather(weight_rows, 'x', axis=0, tiled=True)  9.83 us
    all_gather x1, blocking collectives, local_body(): weight_pair = lax.all_gather(out_weight, 'core', axis=0, tiled=True)  8.55 us
    all_gather x1, waiting for transfers between devices, local_body(): weight_rows = lax.all_gather(weight_rows, 'z', axis=0, tiled=True)  6.27 us
    dot_general x1, matrix products, attend_block(): jnp.einsum('hqk,khd->qhd', probs, value_rows, preferred_element_type=jnp....  4.74 us
  transfers between devices with their start and end apart: 7, of which 5 were waited for; matrix products, arithmetic and copies ran while one was open for 19% of the time, Pallas kernels for 0%

profile of v4, /device:TPU:1, one launch (start us, length us, event | category | flops | bytes accessed | tf_op | source)
XLA Modules:
  0.0 157.2 jit_solution(16035876064572360545)
XLA Ops:
  8.0 8.6 %all_gather.12 = bf16[32,1024]{1,0:T(8,128)(2,1)S(1)} all-gather(bf16[16,1024]{1,0:T(8,128)(2,1)} %param.12), channel_id=1, replica_groups=mesh['z'=16,'x'=4,'core'=2,'head'=4] {'core'}, dimensions={0}, use_global_device_ids=true | all-gather | bytes 98304 | tf_op jit(solution)/shard_map/all_gather | solution.py:78
  16.6 9.8 %all_gather.13 = bf16[128,512]{1,0:T(8,128)(2,1)} all-gather(bf16[32,512]{1,0:T(8,128)(2,1)S(1)} %constant_dynamic-slice_fusion), channel_id=1, replica_groups=mesh['z'=16,'x'=4,'core'=2,'head'=4] {'x'}, dimensions={0}, use_global_device_ids=true | all-gather | bytes 163840 | tf_op jit(solution)/shard_map/all_gather | solution.py:80
  26.6 0.7 copy.50
  27.5 0.7 multiply_subtract_fusion.1
  28.6 1.1 copy.48
  30.8 3.9 %collective-permute-start = (bf16[2,256,512]{1,2,0:T(8,128)(2,1)S(1)}, bf16[2,256,512]{1,2,0:T(8,128)(2,1)}, u32[]{:S(2)}, u32[]{:S(2)}) collective-permute-start(bf16[2,256,512]{1,2,0:T(8,128)(2,1)S(1)} %pad_maximum_fusion), channel_id=1, source_target_pairs={{0,16},{4,20},{8,24},{12,28},{16,32},{20,36},{24,40},{28,44},{32,4... | collective-permute-start | bytes 1572872 | tf_op jit(solution)/shard_map/ppermute | solution.py:26
  34.7 4.3 %collective-permute-start.1 = (bf16[2,256,512]{1,2,0:T(8,128)(2,1)S(1)}, bf16[2,256,512]{1,2,0:T(8,128)(2,1)S(1)}, u32[]{:S(2)}, u32[]{:S(2)}) collective-permute-start(bf16[2,256,512]{1,2,0:T(8,128)(2,1)S(1)} %pad_maximum_fusion), channel_id=1, source_target_pairs={{0,12},{4,16},{8,20},{12,24},{16,28},{20,32},{24,36},{28,40},{32,4... | collective-permute-start | bytes 1572872 | tf_op jit(solution)/shard_map/ppermute | solution.py:26
  39.0 1.3 collective-permute-start.2
  40.3 2.4 %collective-permute-start.3 = (bf16[2,256,512]{1,2,0:T(8,128)(2,1)S(1)}, bf16[2,256,512]{1,2,0:T(8,128)(2,1)S(1)}, u32[]{:S(2)}, u32[]{:S(2)}) collective-permute-start(bf16[2,256,512]{1,2,0:T(8,128)(2,1)S(1)} %pad_maximum_fusion), channel_id=1, source_target_pairs={{0,4},{4,8},{8,12},{12,16},{16,20},{20,24},{24,28},{28,32},{32,36}... | collective-permute-start | bytes 1572872 | tf_op jit(solution)/shard_map/ppermute | solution.py:26
  42.9 1.1 compare_and_fusion
  44.0 1.1 copy.58
  45.7 1.0 pad_maximum_fusion.3
  46.6 1.1 bitcast_dynamic-update-slice_fusion.4
  47.7 5.5 %collective-permute-done.1 = bf16[2,256,512]{1,2,0:T(8,128)(2,1)S(1)} collective-permute-done((bf16[2,256,512]{1,2,0:T(8,128)(2,1)S(1)}, bf16[2,256,512]{1,2,0:T(8,128)(2,1)S(1)}, u32[]{:S(2)}, u32[]{:S(2)}) %collective-permute-start.1) | collective-permute-done | bytes 524320 | tf_op jit(solution)/shard_map/ppermute | solution.py:26
  53.2 11.2 %collective-permute-done.2 = bf16[2,256,512]{1,2,0:T(8,128)(2,1)S(1)} collective-permute-done((bf16[2,256,512]{1,2,0:T(8,128)(2,1)S(1)}, bf16[2,256,512]{1,2,0:T(8,128)(2,1)S(1)}, u32[]{:S(2)}, u32[]{:S(2)}) %collective-permute-start.2) | collective-permute-done | bytes 524320 | tf_op jit(solution)/shard_map/ppermute | solution.py:26
  64.5 9.3 %collective-permute-done.3 = bf16[2,256,512]{1,2,0:T(8,128)(2,1)S(1)} collective-permute-done((bf16[2,256,512]{1,2,0:T(8,128)(2,1)S(1)}, bf16[2,256,512]{1,2,0:T(8,128)(2,1)S(1)}, u32[]{:S(2)}, u32[]{:S(2)}) %collective-permute-start.3) | collective-permute-done | bytes 524320 | tf_op jit(solution)/shard_map/ppermute | solution.py:26
  74.0 1.6 %copy.61 = bf16[1,5,256,512]{3,2,1,0:T(8,128)(2,1)} copy(bf16[1,5,256,512]{2,3,0,1:T(8,128)(2,1)S(1)} %get-tuple-element.18) | data formatting | bytes 2621440 | tf_op jit(solution)/shard_map/slice | solution.py:98
  75.7 3.6 %reshape_squeeze.7 = bf16[1280,4,128]{2,1,0:T(4,128)(2,1)} reshape(bf16[1,5,256,512]{3,2,1,0:T(8,128)(2,1)} %copy.61) | data formatting | bytes 2621440 | tf_op jit(solution)/shard_map/reshape;squeeze | solution.py:101
  79.2 0.8 copy.69
  80.1 2.3 %reshape.202 = bf16[1280,4,128]{0,2,1:T(8,128)(2,1)} reshape(bf16[1,5,256,512]{2,1,3,0:T(8,128)(2,1)S(1)} %copy.69) | data formatting | bytes 2621440 | tf_op jit(solution)/shard_map/reshape;squeeze | solution.py:102
  82.4 3.2 %exponential_reduce_fusion = f32[4,256]{1,0:T(4,128)S(1)} fusion(bf16[256,4,128]{2,0,1:T(8,128)(2,1)} %pad_maximum_fusion.3, pred[256,1280]{1,0:T(8,128)(4,1)} %compare_and_fusion, bf16[1280,4,128]{2,1,0:T(4,128)(2,1)S(1)} %copy-done.2), kind=kOutput, calls=%fused_computation.4 | convolution fusion | flops 340788480 | bytes 1904640 | tf_op jit(solution)/shard_map/sub | solution.py:67
  85.6 6.3 %all-gather.5.cloned.1.call-done = bf16[2048,512]{1,0:T(8,128)(2,1)} async-done(((bf16[128,512]{1,0:T(8,128)(2,1)}), bf16[2048,512]{1,0:T(8,128)(2,1)}) %all-gather.5.cloned.1.call-update) | async-done | bytes 2097168 | tf_op jit(solution)/shard_map/all_gather | solution.py:84
  91.9 11.6 %collective-permute-start.4 = (bf16[2048,512]{1,0:T(8,128)(2,1)}, bf16[2048,512]{1,0:T(8,128)(2,1)}, u32[]{:S(2)}, u32[]{:S(2)}) collective-permute-start(bf16[2048,512]{1,0:T(8,128)(2,1)} %all-gather.5.cloned.1.call-done), channel_id=1, source_target_pairs={{0,4},{4,0},{1,5},{5,1},{2,6},{6,2},{3,7},{7,3},{8,12},{12,8},{9,1... | collective-permute-start | bytes 6291464 | tf_op jit(solution)/shard_map/ppermute | solution.py:85
  103.5 4.7 %fusion.6 = bf16[4,128,256]{2,1,0:T(8,128)(2,1)} fusion(bf16[1280,4,128]{0,2,1:T(8,128)(2,1)} %reshape.202, f32[4,256]{1,0:T(4,128)S(1)} %exponential_reduce_fusion, bf16[256,4,128]{2,0,1:T(8,128)(2,1)} %pad_maximum_fusion.3, pred[256,1280]{1,0:T(8,128)(4,1)} %compare_and_fusion, bf16[1280,4,128]{2,1,0:T(4,128)(2,1)S(1)} %copy-done.3), kind=kOutput, calls=%fused_computation.13 | convolution fusion | flops 677775616 | bytes 3477504 | tf_op jit(solution)/shard_map/hqk,khd->qhd/dot_general | solution.py:69
  108.3 0.4 copy.65
  108.8 0.3 copy.66
  109.1 0.7 convolution_convert_fusion
  109.8 0.9 copy.67
  110.7 33.8 %all-gather.3.cloned.1.call-done = bf16[256,2048]{0,1:T(8,128)(2,1)} async-done(((bf16[256,512]{0,1:T(8,128)(2,1)}), bf16[256,2048]{0,1:T(8,128)(2,1)}) %all-gather.3.cloned.1.call-update) | async-done | bytes 1048592 | tf_op jit(solution)/shard_map/all_gather | solution.py:107
  144.5 2.0 %fusion.4 = bf16[256,512]{1,0:T(8,128)(2,1)S(1)} fusion(bf16[256,2048]{0,1:T(8,128)(2,1)} %all-gather.3.cloned.1.call-done, bf16[2048,512]{1,0:T(8,128)(2,1)S(1)} %copy-done.7, f32[512]{0:T(512)S(1)} %get-tuple-element.26), kind=kOutput, calls=%fused_computation.11 | convolution fusion | flops 537133056 | bytes 3409920 | tf_op jit(solution)/shard_map/dot_general | solution.py:111
  146.5 2.3 %fusion.5 = bf16[256,512]{1,0:T(8,128)(2,1)S(1)} fusion(bf16[256,2048]{0,1:T(8,128)(2,1)S(1)} %copy-done.8, bf16[2048,512]{1,0:T(8,128)(2,1)} %collective-permute-done.4, f32[512]{0:T(512)S(1)} %get-tuple-element.27), kind=kOutput, calls=%fused_computation.12 | convolution fusion | flops 537133056 | bytes 3409920 | tf_op jit(solution)/shard_map/dot_general | solution.py:112
  148.9 0.9 maximum_select_fusion
  (61 shorter events, 3.0 us)
Async XLA Ops:
  8.0 83.9 %all-gather.5.cloned.1.call-start = ((), (), s32[]{:S(2)}) async-start(), calls=%async_computation.1 | async-start | bytes 2228224 | tf_op jit(solution)/shard_map/all_gather | solution.py:84
  26.5 118.0 %all-gather.3.cloned.1.call-start = ((), (), s32[]{:S(2)}) async-start(), calls=%async_computation | async-start | bytes 1310720 | tf_op jit(solution)/shard_map/all_gather | solution.py:107
  27.3 3.3 %copy-start.4 = (bf16[256,512]{1,0:T(8,128)(2,1)S(1)}, bf16[256,512]{1,0:T(8,128)(2,1)}, u32[]{:S(2)}) copy-start(bf16[256,512]{1,0:T(8,128)(2,1)} %param.9) | copy-start | bytes 786436
  30.7 43.1 %copy-start = (bf16[256,4,128]{0,2,1:T(8,128)(2,1)}, bf16[256,4,128]{0,2,1:T(8,128)(2,1)S(1)}, u32[]{:S(2)}) copy-start(bf16[256,4,128]{0,2,1:T(8,128)(2,1)S(1)} %maximum_convert_fusion) | copy-start | bytes 786436
  30.8 15.8 %collective-permute-start = (bf16[2,256,512]{1,2,0:T(8,128)(2,1)S(1)}, bf16[2,256,512]{1,2,0:T(8,128)(2,1)}, u32[]{:S(2)}, u32[]{:S(2)}) collective-permute-start(bf16[2,256,512]{1,2,0:T(8,128)(2,1)S(1)} %pad_maximum_fusion), channel_id=1, source_target_pairs={{0,16},{4,20},{8,24},{12,28},{16,32},{20,36},{24,40},{28,44},{32,4... | collective-permute-start | bytes 1572872 | tf_op jit(solution)/shard_map/ppermute | solution.py:26
  34.7 18.5 %collective-permute-start.1 = (bf16[2,256,512]{1,2,0:T(8,128)(2,1)S(1)}, bf16[2,256,512]{1,2,0:T(8,128)(2,1)S(1)}, u32[]{:S(2)}, u32[]{:S(2)}) collective-permute-start(bf16[2,256,512]{1,2,0:T(8,128)(2,1)S(1)} %pad_maximum_fusion), channel_id=1, source_target_pairs={{0,12},{4,16},{8,20},{12,24},{16,28},{20,32},{24,36},{28,40},{32,4... | collective-permute-start | bytes 1572872 | tf_op jit(solution)/shard_map/ppermute | solution.py:26
  39.0 25.4 %collective-permute-start.2 = (bf16[2,256,512]{1,2,0:T(8,128)(2,1)S(1)}, bf16[2,256,512]{1,2,0:T(8,128)(2,1)S(1)}, u32[]{:S(2)}, u32[]{:S(2)}) collective-permute-start(bf16[2,256,512]{1,2,0:T(8,128)(2,1)S(1)} %pad_maximum_fusion), channel_id=1, source_target_pairs={{0,8},{4,12},{8,16},{12,20},{16,24},{20,28},{24,32},{28,36},{32,40... | collective-permute-start | bytes 1572872 | tf_op jit(solution)/shard_map/ppermute | solution.py:26
  40.3 33.4 %collective-permute-start.3 = (bf16[2,256,512]{1,2,0:T(8,128)(2,1)S(1)}, bf16[2,256,512]{1,2,0:T(8,128)(2,1)S(1)}, u32[]{:S(2)}, u32[]{:S(2)}) collective-permute-start(bf16[2,256,512]{1,2,0:T(8,128)(2,1)S(1)} %pad_maximum_fusion), channel_id=1, source_target_pairs={{0,4},{4,8},{8,12},{12,16},{16,20},{20,24},{24,28},{28,32},{32,36}... | collective-permute-start | bytes 1572872 | tf_op jit(solution)/shard_map/ppermute | solution.py:26
  80.1 2.3 %copy-start.2 = (bf16[1280,4,128]{2,1,0:T(4,128)(2,1)S(1)}, bf16[1280,4,128]{2,1,0:T(4,128)(2,1)}, u32[]{:S(2)}) copy-start(bf16[1280,4,128]{2,1,0:T(4,128)(2,1)} %reshape_squeeze.7) | copy-start | bytes 3932164
  82.4 21.1 %copy-start.3 = (bf16[1280,4,128]{2,1,0:T(4,128)(2,1)S(1)}, bf16[1280,4,128]{2,1,0:T(4,128)(2,1)}, u32[]{:S(2)}) copy-start(bf16[1280,4,128]{2,1,0:T(4,128)(2,1)} %reshape_squeeze.7) | copy-start | bytes 3932164
  85.5 22.7 %copy-start.1 = (bf16[256,4,128]{0,2,1:T(8,128)(2,1)S(1)}, bf16[256,4,128]{0,2,1:T(8,128)(2,1)}, u32[]{:S(2)}) copy-start(bf16[256,4,128]{0,2,1:T(8,128)(2,1)} %copy-done) | copy-start | bytes 786436
  85.6 23.2 %copy-start.5 = (bf16[256,512]{1,0:T(8,128)(2,1)S(1)}, bf16[256,512]{1,0:T(8,128)(2,1)}, u32[]{:S(2)}) copy-start(bf16[256,512]{1,0:T(8,128)(2,1)} %param.9) | copy-start | bytes 786436
  85.6 23.5 %copy-start.9 = (s32[2]{0:T(128)S(1)}, s32[2]{0:T(128)}, u32[]{:S(2)}) copy-start(s32[2]{0:T(128)} %param.11) | copy-start | bytes 28
  91.9 54.7 %collective-permute-start.4 = (bf16[2048,512]{1,0:T(8,128)(2,1)}, bf16[2048,512]{1,0:T(8,128)(2,1)}, u32[]{:S(2)}, u32[]{:S(2)}) collective-permute-start(bf16[2048,512]{1,0:T(8,128)(2,1)} %all-gather.5.cloned.1.call-done), channel_id=1, source_target_pairs={{0,4},{4,0},{1,5},{5,1},{2,6},{6,2},{3,7},{7,3},{8,12},{12,8},{9,1... | collective-permute-start | bytes 6291464 | tf_op jit(solution)/shard_map/ppermute | solution.py:85
  108.7 1.9 %copy-start.6 = (f32[1024]{0:T(1024)S(1)}, f32[1024]{0:T(1024)}, u32[]{:S(2)}) copy-start(f32[1024]{0:T(1024)} %param.13) | copy-start | bytes 12292
  108.7 35.7 %copy-start.7 = (bf16[2048,512]{1,0:T(8,128)(2,1)S(1)}, bf16[2048,512]{1,0:T(8,128)(2,1)}, u32[]{:S(2)}) copy-start(bf16[2048,512]{1,0:T(8,128)(2,1)} %all-gather.5.cloned.1.call-done) | copy-start | bytes 6291460
  144.5 2.1 %copy-start.8 = (bf16[256,2048]{0,1:T(8,128)(2,1)S(1)}, bf16[256,2048]{0,1:T(8,128)(2,1)}, u32[]{:S(2)}) copy-start(bf16[256,2048]{0,1:T(8,128)(2,1)} %all-gather.3.cloned.1.call-done) | copy-start | bytes 3145732
Sparse Core Ops, SparseCore 0:
  26.6 65.2 all-gather.4
Sparse Core Ops, SparseCore 1:
  108.3 36.1 all-gather.2

commit v5 on v4

--- a/solution.py
+++ b/solution.py
@@ -77,11 +77,9 @@
     half = out_weight.shape[1] // 2
     weight_pair = lax.all_gather(out_weight, "core", axis=0, tiled=True)
     weight_rows = lax.dynamic_slice_in_dim(weight_pair, core_rank * half, half, 1)
-    weight_rows = lax.all_gather(weight_rows, "x", axis=0, tiled=True)
-    weight_rows, query_proj, key_proj = lax.optimization_barrier(
-        (weight_rows, query_proj, key_proj)
-    )
-    weight_rows = lax.all_gather(weight_rows, "z", axis=0, tiled=True)
+    weight_rows = lax.all_gather(weight_rows, "z", axis=0, tiled=False)
+    weight_rows = lax.all_gather(weight_rows, "x", axis=1, tiled=False)
+    weight_rows = weight_rows.reshape(-1, half)
     weight_other = lax.ppermute(weight_rows, "core", [(0, 1), (1, 0)])
     first_token = device_rank * TOK_DEV
     own_tokens = first_token + jnp.arange(TOK_DEV, dtype=jnp.int32)

time: 159 us -> 175 us (1.10)
  blocking collectives: 18.4 us -> 34.3 us
  waiting for transfers between devices: 66.1 us -> 73 us
  starting transfers between devices: 23.6 us -> 18 us
    all_gather x1, waiting for transfers between devices: 6.27 us -> 46.1 us  [local_body(): weight_rows = lax.all_gather(weight_rows, 'x', axis=1, tiled=False)]
    ppermute x4, waiting for transfers between devices: 26 us -> 0.01 us  [passed_along(): return lax.ppermute(array, axis, pairs)]
    all_gather x1, blocking collectives: 9.83 us -> 32.3 us  [local_body(): weight_rows = lax.all_gather(weight_rows, 'z', axis=0, tiled=False)]
    ppermute x1, starting transfers between devices: 11.6 us -> 3.05 us  [local_body(): weight_other = lax.ppermute(weight_rows, 'core', [(0, 1), (1, 0)])]
    all_gather x1, waiting for transfers between devices: 33.8 us -> 26.9 us  [local_body(): heads_all = lax.all_gather(heads_out, 'head', axis=1, tiled=True)]
    all_gather x1, blocking collectives: 8.55 us -> 2.03 us  [local_body(): weight_pair = lax.all_gather(out_weight, 'core', axis=0, tiled=True)]
    ppermute x4, starting transfers between devices: 11.9 us -> 14.9 us  [passed_along(): return lax.ppermute(array, axis, pairs)]
    optimization_barrier x2 -> x0, local copies, waits for them, and re-layouts: 2.18 us -> none  [local_body(): lax.optimization_barrier((weight_rows, query_proj, key_proj))]
  transfers between devices with their start and end apart: 7 -> 7, of which waited for: 5 -> 2; matrix products, arithmetic and copies ran while one was open for 19% -> 14% of each run, Pallas kernels for 0% -> 0%
where the time goes in v5:
time: 175 us; the launch traced here: 174 us
  waiting for transfers between devices  73 us (42%)
  blocking collectives  34.3 us (20%)
  starting transfers between devices  18 us (10%)
  between operations  15.9 us (9%)
  local copies, waits for them, and re-layouts  14.7 us (8%)
  matrix products  12.9 us (7%)
  other arithmetic  4.74 us (3%)
    all_gather x1, waiting for transfers between devices, local_body(): weight_rows = lax.all_gather(weight_rows, 'x', axis=1, tiled=False)  46.1 us
    all_gather x1, blocking collectives, local_body(): weight_rows = lax.all_gather(weight_rows, 'z', axis=0, tiled=False)  32.3 us
    all_gather x1, waiting for transfers between devices, local_body(): heads_all = lax.all_gather(heads_out, 'head', axis=1, tiled=True)  26.9 us
    ppermute x4, starting transfers between devices, passed_along(): return lax.ppermute(array, axis, pairs)  14.9 us
    dot_general x1, matrix products, attend_block(): jnp.einsum('hqk,khd->qhd', probs, value_rows, preferred_element_type=jnp....  4.73 us
    unnamed x34, local copies, waits for them, and re-layouts  3.88 us
    another operation x1, local copies, waits for them, and re-layouts, local_body(): key_all = key_stack.reshape(key_rows, local_heads, DH)  3.57 us
  transfers between devices with their start and end apart: 7, of which 2 were waited for; matrix products, arithmetic and copies ran while one was open for 14% of the time, Pallas kernels for 0%

profile of v5, /device:TPU:1, one launch (start us, length us, event | category | flops | bytes accessed | tf_op | source)
XLA Modules:
  0.0 173.6 jit_solution(15941049881234449146)
XLA Ops:
  8.1 1.1 copy.48
  9.3 0.7 copy.50
  10.2 0.7 multiply_subtract_fusion.1
  11.3 0.2 copy.73
  11.6 0.2 copy.74
  12.4 6.3 %collective-permute-start = (bf16[2,256,512]{1,2,0:T(8,128)(2,1)S(1)}, bf16[2,256,512]{1,2,0:T(8,128)(2,1)}, u32[]{:S(2)}, u32[]{:S(2)}) collective-permute-start(bf16[2,256,512]{1,2,0:T(8,128)(2,1)S(1)} %pad_maximum_fusion), channel_id=1, source_target_pairs={{0,16},{4,20},{8,24},{12,28},{16,32},{20,36},{24,40},{28,44},{32,4... | collective-permute-start | bytes 1572872 | tf_op jit(solution)/shard_map/ppermute | solution.py:26
  18.7 3.6 %collective-permute-start.1 = (bf16[2,256,512]{1,2,0:T(8,128)(2,1)S(1)}, bf16[2,256,512]{1,2,0:T(8,128)(2,1)S(1)}, u32[]{:S(2)}, u32[]{:S(2)}) collective-permute-start(bf16[2,256,512]{1,2,0:T(8,128)(2,1)S(1)} %pad_maximum_fusion), channel_id=1, source_target_pairs={{0,12},{4,16},{8,20},{12,24},{16,28},{20,32},{24,36},{28,40},{32,4... | collective-permute-start | bytes 1572872 | tf_op jit(solution)/shard_map/ppermute | solution.py:26
  22.3 3.1 %collective-permute-start.2 = (bf16[2,256,512]{1,2,0:T(8,128)(2,1)S(1)}, bf16[2,256,512]{1,2,0:T(8,128)(2,1)S(1)}, u32[]{:S(2)}, u32[]{:S(2)}) collective-permute-start(bf16[2,256,512]{1,2,0:T(8,128)(2,1)S(1)} %pad_maximum_fusion), channel_id=1, source_target_pairs={{0,8},{4,12},{8,16},{12,20},{16,24},{20,28},{24,32},{28,36},{32,40... | collective-permute-start | bytes 1572872 | tf_op jit(solution)/shard_map/ppermute | solution.py:26
  25.4 1.9 %collective-permute-start.3 = (bf16[2,256,512]{1,2,0:T(8,128)(2,1)S(1)}, bf16[2,256,512]{1,2,0:T(8,128)(2,1)S(1)}, u32[]{:S(2)}, u32[]{:S(2)}) collective-permute-start(bf16[2,256,512]{1,2,0:T(8,128)(2,1)S(1)} %pad_maximum_fusion), channel_id=1, source_target_pairs={{0,4},{4,8},{8,12},{12,16},{16,20},{20,24},{24,28},{28,32},{32,36}... | collective-permute-start | bytes 1572872 | tf_op jit(solution)/shard_map/ppermute | solution.py:26
  27.3 2.0 %all_gather.19 = bf16[32,1024]{1,0:T(8,128)(2,1)S(1)} all-gather(bf16[16,1024]{1,0:T(8,128)(2,1)S(1)} %copy-done.7), channel_id=1, replica_groups=mesh['z'=16,'x'=4,'core'=2,'head'=4] {'core'}, dimensions={0}, use_global_device_ids=true | all-gather | bytes 98304 | tf_op jit(solution)/shard_map/all_gather | solution.py:78
  29.4 32.3 %all-gather = bf16[512,512]{1,0:T(8,128)(2,1)} all-gather(bf16[32,512]{1,0:T(8,128)(2,1)S(1)} %constant_dynamic-slice_fusion), channel_id=2, replica_groups=mesh['z'=16,'x'=4,'core'=2,'head'=4] {'z'}, dimensions={0}, use_global_device_ids=true | all-gather | bytes 557056 | tf_op jit(solution)/shard_map/all_gather | solution.py:80
  61.9 1.1 compare_and_fusion
  63.4 0.3 subtract_convert_fusion
  63.7 1.0 pad_maximum_fusion.3
  64.7 1.1 bitcast_dynamic-update-slice_fusion.4
  66.0 0.2 fusion.28
  66.1 1.6 copy.61
  67.7 3.6 %reshape_squeeze.7 = bf16[1280,4,128]{2,1,0:T(4,128)(2,1)} reshape(bf16[1,5,256,512]{3,2,1,0:T(8,128)(2,1)} %copy.61) | data formatting | bytes 2621440 | tf_op jit(solution)/shard_map/reshape;squeeze | solution.py:99
  71.3 0.8 copy.69
  72.2 2.3 %reshape.209 = bf16[1280,4,128]{0,2,1:T(8,128)(2,1)} reshape(bf16[1,5,256,512]{2,1,3,0:T(8,128)(2,1)S(1)} %copy.69) | data formatting | bytes 2621440 | tf_op jit(solution)/shard_map/reshape;squeeze | solution.py:100
  74.5 3.2 %exponential_reduce_fusion = f32[4,256]{1,0:T(4,128)S(1)} fusion(bf16[256,4,128]{2,0,1:T(8,128)(2,1)} %pad_maximum_fusion.3, pred[256,1280]{1,0:T(8,128)(4,1)} %compare_and_fusion, bf16[1280,4,128]{2,1,0:T(4,128)(2,1)S(1)} %copy-done.2), kind=kOutput, calls=%fused_computation.4 | convolution fusion | flops 340788480 | bytes 1904640 | tf_op jit(solution)/shard_map/sub | solution.py:67
  77.6 46.1 %all-gather.7.cloned.1.call-done = bf16[16,128,512]{2,1,0:T(8,128)(2,1)} async-done(((bf16[16,32,512]{2,1,0:T(8,128)(2,1)}), bf16[16,128,512]{2,1,0:T(8,128)(2,1)}) %all-gather.7.cloned.1.call-update) | async-done | bytes 2097168 | tf_op jit(solution)/shard_map/all_gather | solution.py:81
  123.7 3.0 %collective-permute-start.4 = (bf16[2048,512]{1,0:T(8,128)(2,1)}, bf16[2048,512]{1,0:T(8,128)(2,1)}, u32[]{:S(2)}, u32[]{:S(2)}) collective-permute-start(bf16[2048,512]{1,0:T(8,128)(2,1)} %bitcast.51), channel_id=1, source_target_pairs={{0,4},{4,0},{1,5},{5,1},{2,6},{6,2},{3,7},{7,3},{8,12},{12,8},{9,1... | collective-permute-start | bytes 6291464 | tf_op jit(solution)/shard_map/ppermute | solution.py:83
  126.8 4.7 %fusion.6 = bf16[4,128,256]{2,1,0:T(8,128)(2,1)} fusion(bf16[1280,4,128]{0,2,1:T(8,128)(2,1)} %reshape.209, f32[4,256]{1,0:T(4,128)S(1)} %exponential_reduce_fusion, bf16[256,4,128]{2,0,1:T(8,128)(2,1)} %pad_maximum_fusion.3, pred[256,1280]{1,0:T(8,128)(4,1)} %compare_and_fusion, bf16[1280,4,128]{2,1,0:T(4,128)(2,1)S(1)} %copy-done.3), kind=kOutput, calls=%fused_computation.13 | convolution fusion | flops 677775616 | bytes 3477504 | tf_op jit(solution)/shard_map/hqk,khd->qhd/dot_general | solution.py:69
  131.6 0.4 copy.65
  132.1 0.3 copy.66
  132.4 0.7 convolution_convert_fusion
  133.1 0.9 copy.67
  134.0 26.9 %all-gather.5.cloned.1.call-done = bf16[256,2048]{0,1:T(8,128)(2,1)} async-done(((bf16[256,512]{0,1:T(8,128)(2,1)}), bf16[256,2048]{0,1:T(8,128)(2,1)}) %all-gather.5.cloned.1.call-update) | async-done | bytes 1048592 | tf_op jit(solution)/shard_map/all_gather | solution.py:105
  160.9 2.0 %fusion.4 = bf16[256,512]{1,0:T(8,128)(2,1)S(1)} fusion(bf16[256,2048]{0,1:T(8,128)(2,1)} %all-gather.5.cloned.1.call-done, bf16[2048,512]{1,0:T(8,128)(2,1)S(1)} %bitcast.52, f32[512]{0:T(512)S(1)} %get-tuple-element.20), kind=kOutput, calls=%fused_computation.11 | convolution fusion | flops 537133056 | bytes 3409920 | tf_op jit(solution)/shard_map/dot_general | solution.py:109
  162.9 2.3 %fusion.5 = bf16[256,512]{1,0:T(8,128)(2,1)S(1)} fusion(bf16[256,2048]{0,1:T(8,128)(2,1)S(1)} %copy-done.10, bf16[2048,512]{1,0:T(8,128)(2,1)} %collective-permute-done.4, f32[512]{0:T(512)S(1)} %get-tuple-element.21), kind=kOutput, calls=%fused_computation.12 | convolution fusion | flops 537133056 | bytes 3409920 | tf_op jit(solution)/shard_map/dot_general | solution.py:110
  165.3 0.9 maximum_select_fusion
  (65 shorter events, 2.3 us)
Async XLA Ops:
  8.0 115.7 %all-gather.7.cloned.1.call-start = ((), (), s32[]{:S(2)}) async-start(), calls=%async_computation.1 | async-start | bytes 2621440 | tf_op jit(solution)/shard_map/all_gather | solution.py:81
  8.1 4.1 %copy-start.4 = (bf16[256,512]{1,0:T(8,128)(2,1)S(1)}, bf16[256,512]{1,0:T(8,128)(2,1)}, u32[]{:S(2)}) copy-start(bf16[256,512]{1,0:T(8,128)(2,1)} %param.9) | copy-start | bytes 786436
  11.6 15.8 %copy-start.7 = (bf16[16,1024]{1,0:T(8,128)(2,1)S(1)}, bf16[16,1024]{1,0:T(8,128)(2,1)}, u32[]{:S(2)}) copy-start(bf16[16,1024]{1,0:T(8,128)(2,1)} %param.12) | copy-start | bytes 98308
  11.9 51.0 %copy-start.6 = (bf16[256,512]{1,0:T(8,128)(2,1)S(1)}, bf16[256,512]{1,0:T(8,128)(2,1)}, u32[]{:S(2)}) copy-start(bf16[256,512]{1,0:T(8,128)(2,1)} %param.7) | copy-start | bytes 786436
  12.3 53.6 %copy-start = (bf16[256,4,128]{0,2,1:T(8,128)(2,1)}, bf16[256,4,128]{0,2,1:T(8,128)(2,1)S(1)}, u32[]{:S(2)}) copy-start(bf16[256,4,128]{0,2,1:T(8,128)(2,1)S(1)} %maximum_convert_fusion) | copy-start | bytes 786436
  12.4 52.2 %collective-permute-start = (bf16[2,256,512]{1,2,0:T(8,128)(2,1)S(1)}, bf16[2,256,512]{1,2,0:T(8,128)(2,1)}, u32[]{:S(2)}, u32[]{:S(2)}) collective-permute-start(bf16[2,256,512]{1,2,0:T(8,128)(2,1)S(1)} %pad_maximum_fusion), channel_id=1, source_target_pairs={{0,16},{4,20},{8,24},{12,28},{16,32},{20,36},{24,40},{28,44},{32,4... | collective-permute-start | bytes 1572872 | tf_op jit(solution)/shard_map/ppermute | solution.py:26
  18.7 47.1 %collective-permute-start.1 = (bf16[2,256,512]{1,2,0:T(8,128)(2,1)S(1)}, bf16[2,256,512]{1,2,0:T(8,128)(2,1)S(1)}, u32[]{:S(2)}, u32[]{:S(2)}) collective-permute-start(bf16[2,256,512]{1,2,0:T(8,128)(2,1)S(1)} %pad_maximum_fusion), channel_id=1, source_target_pairs={{0,12},{4,16},{8,20},{12,24},{16,28},{20,32},{24,36},{28,40},{32,4... | collective-permute-start | bytes 1572872 | tf_op jit(solution)/shard_map/ppermute | solution.py:26
  22.3 43.5 %collective-permute-start.2 = (bf16[2,256,512]{1,2,0:T(8,128)(2,1)S(1)}, bf16[2,256,512]{1,2,0:T(8,128)(2,1)S(1)}, u32[]{:S(2)}, u32[]{:S(2)}) collective-permute-start(bf16[2,256,512]{1,2,0:T(8,128)(2,1)S(1)} %pad_maximum_fusion), channel_id=1, source_target_pairs={{0,8},{4,12},{8,16},{12,20},{16,24},{20,28},{24,32},{28,36},{32,40... | collective-permute-start | bytes 1572872 | tf_op jit(solution)/shard_map/ppermute | solution.py:26
  25.4 40.5 %collective-permute-start.3 = (bf16[2,256,512]{1,2,0:T(8,128)(2,1)S(1)}, bf16[2,256,512]{1,2,0:T(8,128)(2,1)S(1)}, u32[]{:S(2)}, u32[]{:S(2)}) collective-permute-start(bf16[2,256,512]{1,2,0:T(8,128)(2,1)S(1)} %pad_maximum_fusion), channel_id=1, source_target_pairs={{0,4},{4,8},{8,12},{12,16},{16,20},{20,24},{24,28},{28,32},{32,36}... | collective-permute-start | bytes 1572872 | tf_op jit(solution)/shard_map/ppermute | solution.py:26
  61.7 99.2 %all-gather.5.cloned.1.call-start = ((), (), s32[]{:S(2)}) async-start(), calls=%async_computation | async-start | bytes 1310720 | tf_op jit(solution)/shard_map/all_gather | solution.py:105
  72.1 2.3 %copy-start.2 = (bf16[1280,4,128]{2,1,0:T(4,128)(2,1)S(1)}, bf16[1280,4,128]{2,1,0:T(4,128)(2,1)}, u32[]{:S(2)}) copy-start(bf16[1280,4,128]{2,1,0:T(4,128)(2,1)} %reshape_squeeze.7) | copy-start | bytes 3932164
  74.5 52.3 %copy-start.3 = (bf16[1280,4,128]{2,1,0:T(4,128)(2,1)S(1)}, bf16[1280,4,128]{2,1,0:T(4,128)(2,1)}, u32[]{:S(2)}) copy-start(bf16[1280,4,128]{2,1,0:T(4,128)(2,1)} %reshape_squeeze.7) | copy-start | bytes 3932164
  123.7 7.8 %copy-start.1 = (bf16[256,4,128]{0,2,1:T(8,128)(2,1)S(1)}, bf16[256,4,128]{0,2,1:T(8,128)(2,1)}, u32[]{:S(2)}) copy-start(bf16[256,4,128]{0,2,1:T(8,128)(2,1)} %copy-done) | copy-start | bytes 786436
  123.7 8.3 %copy-start.5 = (bf16[256,512]{1,0:T(8,128)(2,1)S(1)}, bf16[256,512]{1,0:T(8,128)(2,1)}, u32[]{:S(2)}) copy-start(bf16[256,512]{1,0:T(8,128)(2,1)} %param.9) | copy-start | bytes 786436
  123.7 8.6 %copy-start.11 = (s32[2]{0:T(128)S(1)}, s32[2]{0:T(128)}, u32[]{:S(2)}) copy-start(s32[2]{0:T(128)} %param.11) | copy-start | bytes 28
  123.7 39.2 %collective-permute-start.4 = (bf16[2048,512]{1,0:T(8,128)(2,1)}, bf16[2048,512]{1,0:T(8,128)(2,1)}, u32[]{:S(2)}, u32[]{:S(2)}) collective-permute-start(bf16[2048,512]{1,0:T(8,128)(2,1)} %bitcast.51), channel_id=1, source_target_pairs={{0,4},{4,0},{1,5},{5,1},{2,6},{6,2},{3,7},{7,3},{8,12},{12,8},{9,1... | collective-permute-start | bytes 6291464 | tf_op jit(solution)/shard_map/ppermute | solution.py:83
  132.0 1.9 %copy-start.8 = (f32[1024]{0:T(1024)S(1)}, f32[1024]{0:T(1024)}, u32[]{:S(2)}) copy-start(f32[1024]{0:T(1024)} %param.13) | copy-start | bytes 12292
  132.1 28.8 %copy-start.9 = (bf16[16,128,512]{2,1,0:T(8,128)(2,1)S(1)}, bf16[16,128,512]{2,1,0:T(8,128)(2,1)}, u32[]{:S(2)}) copy-start(bf16[16,128,512]{2,1,0:T(8,128)(2,1)} %all-gather.7.cloned.1.call-done) | copy-start | bytes 6291460
  160.9 2.1 %copy-start.10 = (bf16[256,2048]{0,1:T(8,128)(2,1)S(1)}, bf16[256,2048]{0,1:T(8,128)(2,1)}, u32[]{:S(2)}) copy-start(bf16[256,2048]{0,1:T(8,128)(2,1)} %all-gather.5.cloned.1.call-done) | copy-start | bytes 3145732
Sparse Core Ops, SparseCore 0:
  61.8 61.8 all-gather.6
Sparse Core Ops, SparseCore 1:
  131.6 29.2 all-gather.4

commit v6 on v4

--- a/solution.py
+++ b/solution.py
@@ -24,6 +24,15 @@
     count = lax.axis_size(axis)
     pairs = [(i, i + by) for i in range(count) if 0 <= i + by < count]
     return lax.ppermute(array, axis, pairs)
+
+
+def ring_gather(piece, axis):
+    count = lax.axis_size(axis)
+    relative = [piece]
+    for distance in range(1, count):
+        pairs = [(i, (i - distance) % count) for i in range(count)]
+        relative.append(lax.ppermute(piece, axis, pairs))
+    return jnp.roll(jnp.stack(relative, axis=0), lax.axis_index(axis), axis=0)
 
 
 def request_info(lengths, token_index):
@@ -104,12 +113,19 @@
     key_id, _ = request_info(lengths, key_tokens)
     mixed = attend_block(query_rot, key_all, value_all, request_id, own_tokens, key_id, key_tokens)
     heads_out = mixed.reshape(TOK_DEV, local_heads * DH)
-    heads_all = lax.all_gather(heads_out, "head", axis=1, tiled=True)
+    heads_all = ring_gather(heads_out, "head")
+    groups = heads_all.shape[0]
+    weight_rows = weight_rows.reshape(groups, -1, half)
+    weight_other = weight_other.reshape(groups, -1, half)
     other_rank = 1 - core_rank
     bias_own = lax.dynamic_slice_in_dim(out_bias, core_rank * half, half, 0)
     bias_other = lax.dynamic_slice_in_dim(out_bias, other_rank * half, half, 0)
-    own_cols = jnp.dot(heads_all, weight_rows, preferred_element_type=jnp.float32) + bias_own
-    other_cols = jnp.dot(heads_all, weight_other, preferred_element_type=jnp.float32) + bias_other
+    own_cols = jnp.einsum(
+        "gtk,gkc->tc", heads_all, weight_rows, preferred_element_type=jnp.float32
+    ) + bias_own
+    other_cols = jnp.einsum(
+        "gtk,gkc->tc", heads_all, weight_other, preferred_element_type=jnp.float32
+    ) + bias_other
     own_cols = own_cols.astype(jnp.bfloat16)
     other_cols = other_cols.astype(jnp.bfloat16)
     attended = jnp.where(

time: 159 us -> 146 us (0.918)
  the two profiles are of different devices: /device:TPU:1 before, /device:TPU:257 now
where the time goes in v6:
time: 146 us; the launch traced here: 145 us
  waiting for transfers between devices  43.9 us (30%)
  starting transfers between devices  40.3 us (28%)
  local copies, waits for them, and re-layouts  18.6 us (13%)
  between operations  14.6 us (10%)
  blocking collectives  12.7 us (9%)
  matrix products  10.5 us (7%)
  other arithmetic  4.74 us (3%)
    ppermute x4, waiting for transfers between devices, passed_along(): return lax.ppermute(array, axis, pairs)  31.6 us
    ppermute x1, starting transfers between devices, local_body(): weight_other = lax.ppermute(weight_rows, 'core', [(0, 1), (1, 0)])  15.4 us
    ppermute x4, starting transfers between devices, passed_along(): return lax.ppermute(array, axis, pairs)  15.3 us
    ppermute x3, waiting for transfers between devices, ring_gather(): relative.append(lax.ppermute(piece, axis, pairs))  12.2 us
    all_gather x1, blocking collectives, local_body(): weight_rows = lax.all_gather(weight_rows, 'x', axis=0, tiled=True)  10.3 us
    ppermute x3, starting transfers between devices, ring_gather(): relative.append(lax.ppermute(piece, axis, pairs))  9.51 us
    unnamed x33, local copies, waits for them, and re-layouts  4.92 us
    dot_general x1, matrix products, attend_block(): jnp.einsum('hqk,khd->qhd', probs, value_rows, preferred_element_type=jnp....  3.69 us
  transfers between devices with their start and end apart: 9, of which 4 were waited for; matrix products, arithmetic and copies ran while one was open for 21% of the time, Pallas kernels for 0%

profile of v6, /device:TPU:257, one launch (start us, length us, event | category | flops | bytes accessed | tf_op | source)
XLA Modules:
  0.0 145.3 jit_solution(7711372386845847596)
XLA Ops:
  7.2 2.4 %all_gather.9 = bf16[32,1024]{1,0:T(8,128)(2,1)S(1)} all-gather(bf16[16,1024]{1,0:T(8,128)(2,1)} %param.12), channel_id=1, replica_groups=mesh['z'=16,'x'=4,'core'=2,'head'=4] {'core'}, dimensions={0}, use_global_device_ids=true | all-gather | bytes 98304 | tf_op jit(solution)/shard_map/all_gather | solution.py:87
  9.6 10.3 %all_gather.10 = bf16[128,512]{1,0:T(8,128)(2,1)} all-gather(bf16[32,512]{1,0:T(8,128)(2,1)S(1)} %constant_dynamic-slice_fusion), channel_id=1, replica_groups=mesh['z'=16,'x'=4,'core'=2,'head'=4] {'x'}, dimensions={0}, use_global_device_ids=true | all-gather | bytes 163840 | tf_op jit(solution)/shard_map/all_gather | solution.py:89
  20.0 0.7 copy.65
  22.1 1.1 copy.63
  24.3 3.1 %collective-permute-start = (bf16[2,256,512]{1,2,0:T(8,128)(2,1)S(1)}, bf16[2,256,512]{1,2,0:T(8,128)(2,1)}, u32[]{:S(2)}, u32[]{:S(2)}) collective-permute-start(bf16[2,256,512]{1,2,0:T(8,128)(2,1)S(1)} %pad_maximum_fusion), channel_id=1, source_target_pairs={{0,16},{4,20},{8,24},{12,28},{16,32},{20,36},{24,40},{28,44},{32,4... | collective-permute-start | bytes 1572872 | tf_op jit(solution)/shard_map/ppermute | solution.py:26
  27.4 7.4 %collective-permute-start.1 = (bf16[2,256,512]{1,2,0:T(8,128)(2,1)S(1)}, bf16[2,256,512]{1,2,0:T(8,128)(2,1)}, u32[]{:S(2)}, u32[]{:S(2)}) collective-permute-start(bf16[2,256,512]{1,2,0:T(8,128)(2,1)S(1)} %pad_maximum_fusion), channel_id=1, source_target_pairs={{0,12},{4,16},{8,20},{12,24},{16,28},{20,32},{24,36},{28,40},{32,4... | collective-permute-start | bytes 1572872 | tf_op jit(solution)/shard_map/ppermute | solution.py:26
  34.9 2.8 %collective-permute-start.2 = (bf16[2,256,512]{1,2,0:T(8,128)(2,1)S(1)}, bf16[2,256,512]{1,2,0:T(8,128)(2,1)}, u32[]{:S(2)}, u32[]{:S(2)}) collective-permute-start(bf16[2,256,512]{1,2,0:T(8,128)(2,1)S(1)} %pad_maximum_fusion), channel_id=1, source_target_pairs={{0,8},{4,12},{8,16},{12,20},{16,24},{20,28},{24,32},{28,36},{32,40... | collective-permute-start | bytes 1572872 | tf_op jit(solution)/shard_map/ppermute | solution.py:26
  37.7 1.9 %collective-permute-start.3 = (bf16[2,256,512]{1,2,0:T(8,128)(2,1)S(1)}, bf16[2,256,512]{1,2,0:T(8,128)(2,1)S(1)}, u32[]{:S(2)}, u32[]{:S(2)}) collective-permute-start(bf16[2,256,512]{1,2,0:T(8,128)(2,1)S(1)} %pad_maximum_fusion), channel_id=1, source_target_pairs={{0,4},{4,8},{8,12},{12,16},{16,20},{20,24},{24,28},{28,32},{32,36}... | collective-permute-start | bytes 1572872 | tf_op jit(solution)/shard_map/ppermute | solution.py:26
  40.3 1.1 compare_and_fusion
  41.6 1.0 pad_maximum_fusion.3
  42.7 1.0 copy.85
  43.7 1.0 copy.86
  44.7 1.1 bitcast_dynamic-update-slice_fusion.4
  45.7 25.3 %collective-permute-done.1 = bf16[2,256,512]{1,2,0:T(8,128)(2,1)} collective-permute-done((bf16[2,256,512]{1,2,0:T(8,128)(2,1)S(1)}, bf16[2,256,512]{1,2,0:T(8,128)(2,1)}, u32[]{:S(2)}, u32[]{:S(2)}) %collective-permute-start.1) | collective-permute-done | bytes 524320 | tf_op jit(solution)/shard_map/ppermute | solution.py:26
  71.0 1.1 bitcast_dynamic-update-slice_fusion.3
  72.1 6.3 %collective-permute-done.2 = bf16[2,256,512]{1,2,0:T(8,128)(2,1)} collective-permute-done((bf16[2,256,512]{1,2,0:T(8,128)(2,1)S(1)}, bf16[2,256,512]{1,2,0:T(8,128)(2,1)}, u32[]{:S(2)}, u32[]{:S(2)}) %collective-permute-start.2) | collective-permute-done | bytes 524320 | tf_op jit(solution)/shard_map/ppermute | solution.py:26
  78.4 1.1 bitcast_dynamic-update-slice_fusion.2
  79.8 1.6 %copy.76 = bf16[1,5,256,512]{3,2,1,0:T(8,128)(2,1)} copy(bf16[1,5,256,512]{2,3,0,1:T(8,128)(2,1)S(1)} %get-tuple-element.18) | data formatting | bytes 2621440 | tf_op jit(solution)/shard_map/slice | solution.py:107
  81.4 3.6 %reshape_squeeze.7 = bf16[1280,4,128]{2,1,0:T(4,128)(2,1)} reshape(bf16[1,5,256,512]{3,2,1,0:T(8,128)(2,1)} %copy.76) | data formatting | bytes 2621440 | tf_op jit(solution)/shard_map/reshape;squeeze | solution.py:110
  85.0 0.8 copy.89
  85.8 2.3 %reshape.212 = bf16[1280,4,128]{0,2,1:T(8,128)(2,1)} reshape(bf16[1,5,256,512]{2,1,3,0:T(8,128)(2,1)S(1)} %copy.89) | data formatting | bytes 2621440 | tf_op jit(solution)/shard_map/reshape;squeeze | solution.py:111
  88.2 3.2 %exponential_reduce_fusion = f32[4,256]{1,0:T(4,128)S(1)} fusion(bf16[256,4,128]{2,0,1:T(8,128)(2,1)} %pad_maximum_fusion.3, pred[256,1280]{1,0:T(8,128)(4,1)} %compare_and_fusion, bf16[1280,4,128]{2,1,0:T(4,128)(2,1)S(1)} %copy-done), kind=kOutput, calls=%fused_computation.4 | convolution fusion | flops 340788480 | bytes 1904640 | tf_op jit(solution)/shard_map/sub | solution.py:76
  91.4 3.7 %fusion.8 = bf16[4,128,256]{2,1,0:T(8,128)(2,1)S(1)} fusion(bf16[1280,4,128]{0,2,1:T(8,128)(2,1)S(1)} %copy-done.1, f32[4,256]{1,0:T(4,128)S(1)} %exponential_reduce_fusion, bf16[256,4,128]{2,0,1:T(8,128)(2,1)} %pad_maximum_fusion.3, pred[256,1280]{1,0:T(8,128)(4,1)} %compare_and_fusion, bf16[1280,4,128]{2,1,0:T(4,128)(2,1)S(1)} %copy-done), kind=kOutput, calls=%fused_computation.15 | convolution fusion | flops 677775616 | bytes 3477504 | tf_op jit(solution)/shard_map/hqk,khd->qhd/dot_general | solution.py:78
  95.2 4.7 %collective-permute-start.4 = (bf16[256,512]{1,0:T(8,128)(2,1)S(1)}, bf16[256,512]{1,0:T(8,128)(2,1)S(1)}, u32[]{:S(2)}, u32[]{:S(2)}) collective-permute-start(bf16[256,512]{1,0:T(8,128)(2,1)S(1)} %copy.79), channel_id=1, source_target_pairs={{0,3},{1,0},{2,1},{3,2},{4,7},{5,4},{6,5},{7,6},{8,11},{9,8},{10,9... | collective-permute-start | bytes 786440 | tf_op jit(solution)/shard_map/ppermute | solution.py:34
  100.0 15.4 %collective-permute-start.7 = (bf16[2048,512]{1,0:T(8,128)(2,1)}, bf16[2048,512]{1,0:T(8,128)(2,1)}, u32[]{:S(2)}, u32[]{:S(2)}) collective-permute-start(bf16[2048,512]{1,0:T(8,128)(2,1)} %all-gather.2.cloned.1.call-done), channel_id=1, source_target_pairs={{0,4},{4,0},{1,5},{5,1},{2,6},{6,2},{3,7},{7,3},{8,12},{12,8},{9,1... | collective-permute-start | bytes 6291464 | tf_op jit(solution)/shard_map/ppermute | solution.py:94
  116.1 0.9 copy.87
  117.1 2.1 %collective-permute-start.5 = (bf16[256,512]{1,0:T(8,128)(2,1)S(1)}, bf16[256,512]{1,0:T(8,128)(2,1)S(1)}, u32[]{:S(2)}, u32[]{:S(2)}) collective-permute-start(bf16[256,512]{1,0:T(8,128)(2,1)S(1)} %copy.79), channel_id=1, source_target_pairs={{0,2},{1,3},{2,0},{3,1},{4,6},{5,7},{6,4},{7,5},{8,10},{9,11},{10,... | collective-permute-start | bytes 786440 | tf_op jit(solution)/shard_map/ppermute | solution.py:34
  119.2 2.7 %collective-permute-start.6 = (bf16[256,512]{1,0:T(8,128)(2,1)S(1)}, bf16[256,512]{1,0:T(8,128)(2,1)S(1)}, u32[]{:S(2)}, u32[]{:S(2)}) collective-permute-start(bf16[256,512]{1,0:T(8,128)(2,1)S(1)} %copy.79), channel_id=1, source_target_pairs={{0,1},{1,2},{2,3},{3,0},{4,5},{5,6},{6,7},{7,4},{8,9},{9,10},{10,1... | collective-permute-start | bytes 786440 | tf_op jit(solution)/shard_map/ppermute | solution.py:34
  122.1 6.2 %collective-permute-done.5 = bf16[256,512]{1,0:T(8,128)(2,1)S(1)} collective-permute-done((bf16[256,512]{1,0:T(8,128)(2,1)S(1)}, bf16[256,512]{1,0:T(8,128)(2,1)S(1)}, u32[]{:S(2)}, u32[]{:S(2)}) %collective-permute-start.5) | collective-permute-done | bytes 262176 | tf_op jit(solution)/shard_map/ppermute | solution.py:34
  128.4 6.0 %collective-permute-done.6 = bf16[256,512]{1,0:T(8,128)(2,1)S(1)} collective-permute-done((bf16[256,512]{1,0:T(8,128)(2,1)S(1)}, bf16[256,512]{1,0:T(8,128)(2,1)S(1)}, u32[]{:S(2)}, u32[]{:S(2)}) %collective-permute-start.6) | collective-permute-done | bytes 262176 | tf_op jit(solution)/shard_map/ppermute | solution.py:34
  135.2 2.3 %fusion.6 = bf16[256,512]{1,0:T(8,128)(2,1)S(1)} fusion(bf16[4,512,512]{2,1,0:T(8,128)(2,1)} %bitcast.21, bf16[8,256,512]{2,1,0:T(8,128)(2,1)S(1)} %bitcast_dynamic-update-slice_fusion.6, s32[]{:T(128)S(6)} %select_n.41, f32[512]{0:T(512)S(1)} %get-tuple-element.27), kind=kOutput, calls=%fused_computation.13 | convolution fusion | flops 537133056 | bytes 3409924 | tf_op jit(solution)/shard_map/gtk,gkc->tc/dot_general | solution.py:126
  137.5 0.9 maximum_select_fusion
  (72 shorter events, 5.6 us)
Async XLA Ops:
  7.2 92.8 %all-gather.2.cloned.1.call-start = ((), (), s32[]{:S(2)}) async-start(), calls=%async_computation | async-start | bytes 2228224 | tf_op jit(solution)/shard_map/all_gather | solution.py:93
  23.2 1.0 copy-start.2
  23.7 15.9 %copy-start.3 = (bf16[256,512]{1,0:T(8,128)(2,1)S(1)}, bf16[256,512]{1,0:T(8,128)(2,1)}, u32[]{:S(2)}) copy-start(bf16[256,512]{1,0:T(8,128)(2,1)} %param.7) | copy-start | bytes 786436
  24.3 20.3 %collective-permute-start = (bf16[2,256,512]{1,2,0:T(8,128)(2,1)S(1)}, bf16[2,256,512]{1,2,0:T(8,128)(2,1)}, u32[]{:S(2)}, u32[]{:S(2)}) collective-permute-start(bf16[2,256,512]{1,2,0:T(8,128)(2,1)S(1)} %pad_maximum_fusion), channel_id=1, source_target_pairs={{0,16},{4,20},{8,24},{12,28},{16,32},{20,36},{24,40},{28,44},{32,4... | collective-permute-start | bytes 1572872 | tf_op jit(solution)/shard_map/ppermute | solution.py:26
  27.4 43.6 %collective-permute-start.1 = (bf16[2,256,512]{1,2,0:T(8,128)(2,1)S(1)}, bf16[2,256,512]{1,2,0:T(8,128)(2,1)}, u32[]{:S(2)}, u32[]{:S(2)}) collective-permute-start(bf16[2,256,512]{1,2,0:T(8,128)(2,1)S(1)} %pad_maximum_fusion), channel_id=1, source_target_pairs={{0,12},{4,16},{8,20},{12,24},{16,28},{20,32},{24,36},{28,40},{32,4... | collective-permute-start | bytes 1572872 | tf_op jit(solution)/shard_map/ppermute | solution.py:26
  34.9 43.6 %collective-permute-start.2 = (bf16[2,256,512]{1,2,0:T(8,128)(2,1)S(1)}, bf16[2,256,512]{1,2,0:T(8,128)(2,1)}, u32[]{:S(2)}, u32[]{:S(2)}) collective-permute-start(bf16[2,256,512]{1,2,0:T(8,128)(2,1)S(1)} %pad_maximum_fusion), channel_id=1, source_target_pairs={{0,8},{4,12},{8,16},{12,20},{16,24},{20,28},{24,32},{28,36},{32,40... | collective-permute-start | bytes 1572872 | tf_op jit(solution)/shard_map/ppermute | solution.py:26
  37.7 41.8 %collective-permute-start.3 = (bf16[2,256,512]{1,2,0:T(8,128)(2,1)S(1)}, bf16[2,256,512]{1,2,0:T(8,128)(2,1)S(1)}, u32[]{:S(2)}, u32[]{:S(2)}) collective-permute-start(bf16[2,256,512]{1,2,0:T(8,128)(2,1)S(1)} %pad_maximum_fusion), channel_id=1, source_target_pairs={{0,4},{4,8},{8,12},{12,16},{16,20},{20,24},{24,28},{28,32},{32,36}... | collective-permute-start | bytes 1572872 | tf_op jit(solution)/shard_map/ppermute | solution.py:26
  39.8 1.8 %copy-start.8 = (s32[2]{0:T(128)S(1)}, s32[2]{0:T(128)}, u32[]{:S(2)}) copy-start(s32[2]{0:T(128)} %param.11) | copy-start | bytes 28
  85.8 2.3 %copy-start = (bf16[1280,4,128]{2,1,0:T(4,128)(2,1)S(1)}, bf16[1280,4,128]{2,1,0:T(4,128)(2,1)}, u32[]{:S(2)}) copy-start(bf16[1280,4,128]{2,1,0:T(4,128)(2,1)} %reshape_squeeze.7) | copy-start | bytes 3932164
  88.2 3.2 %copy-start.1 = (bf16[1280,4,128]{0,2,1:T(8,128)(2,1)S(1)}, bf16[1280,4,128]{0,2,1:T(8,128)(2,1)}, u32[]{:S(2)}) copy-start(bf16[1280,4,128]{0,2,1:T(8,128)(2,1)} %reshape.212) | copy-start | bytes 3932164
  91.3 24.1 %copy-start.4 = (bf16[2,1,128,512]{3,0,2,1:T(2,128)(2,1)S(1)}, bf16[2,1,128,512]{3,0,2,1:T(2,128)(2,1)}, u32[]{:S(2)}) copy-start(bf16[2,1,128,512]{3,0,2,1:T(2,128)(2,1)} %copy.85) | copy-start | bytes 786436
  91.3 24.1 %copy-start.5 = (bf16[2,1,128,512]{3,0,2,1:T(2,128)(2,1)S(1)}, bf16[2,1,128,512]{3,0,2,1:T(2,128)(2,1)}, u32[]{:S(2)}) copy-start(bf16[2,1,128,512]{3,0,2,1:T(2,128)(2,1)} %copy.86) | copy-start | bytes 786436
  95.2 21.8 %copy-start.6 = (f32[1024]{0:T(1024)S(1)}, f32[1024]{0:T(1024)}, u32[]{:S(2)}) copy-start(f32[1024]{0:T(1024)} %param.13) | copy-start | bytes 12292
  95.2 26.9 %collective-permute-start.4 = (bf16[256,512]{1,0:T(8,128)(2,1)S(1)}, bf16[256,512]{1,0:T(8,128)(2,1)S(1)}, u32[]{:S(2)}, u32[]{:S(2)}) collective-permute-start(bf16[256,512]{1,0:T(8,128)(2,1)S(1)} %copy.79), channel_id=1, source_target_pairs={{0,3},{1,0},{2,1},{3,2},{4,7},{5,4},{6,5},{7,6},{8,11},{9,8},{10,9... | collective-permute-start | bytes 786440 | tf_op jit(solution)/shard_map/ppermute | solution.py:34
  100.0 35.2 %collective-permute-start.7 = (bf16[2048,512]{1,0:T(8,128)(2,1)}, bf16[2048,512]{1,0:T(8,128)(2,1)}, u32[]{:S(2)}, u32[]{:S(2)}) collective-permute-start(bf16[2048,512]{1,0:T(8,128)(2,1)} %all-gather.2.cloned.1.call-done), channel_id=1, source_target_pairs={{0,4},{4,0},{1,5},{5,1},{2,6},{6,2},{3,7},{7,3},{8,12},{12,8},{9,1... | collective-permute-start | bytes 6291464 | tf_op jit(solution)/shard_map/ppermute | solution.py:94
  117.1 11.3 %collective-permute-start.5 = (bf16[256,512]{1,0:T(8,128)(2,1)S(1)}, bf16[256,512]{1,0:T(8,128)(2,1)S(1)}, u32[]{:S(2)}, u32[]{:S(2)}) collective-permute-start(bf16[256,512]{1,0:T(8,128)(2,1)S(1)} %copy.79), channel_id=1, source_target_pairs={{0,2},{1,3},{2,0},{3,1},{4,6},{5,7},{6,4},{7,5},{8,10},{9,11},{10,... | collective-permute-start | bytes 786440 | tf_op jit(solution)/shard_map/ppermute | solution.py:34
  119.2 15.1 %collective-permute-start.6 = (bf16[256,512]{1,0:T(8,128)(2,1)S(1)}, bf16[256,512]{1,0:T(8,128)(2,1)S(1)}, u32[]{:S(2)}, u32[]{:S(2)}) collective-permute-start(bf16[256,512]{1,0:T(8,128)(2,1)S(1)} %copy.79), channel_id=1, source_target_pairs={{0,1},{1,2},{2,3},{3,0},{4,5},{5,6},{6,7},{7,4},{8,9},{9,10},{10,1... | collective-permute-start | bytes 786440 | tf_op jit(solution)/shard_map/ppermute | solution.py:34
  122.1 12.4 %copy-start.7 = (bf16[2048,512]{1,0:T(8,128)(2,1)S(1)}, bf16[2048,512]{1,0:T(8,128)(2,1)}, u32[]{:S(2)}) copy-start(bf16[2048,512]{1,0:T(8,128)(2,1)} %all-gather.2.cloned.1.call-done) | copy-start | bytes 6291460
Sparse Core Ops, SparseCore 0:
  20.1 62.7 all-gather.1

commit v7 on v6

--- a/solution.py
+++ b/solution.py
@@ -28,11 +28,20 @@
 
 def ring_gather(piece, axis):
     count = lax.axis_size(axis)
-    relative = [piece]
-    for distance in range(1, count):
-        pairs = [(i, (i - distance) % count) for i in range(count)]
-        relative.append(lax.ppermute(piece, axis, pairs))
-    return jnp.roll(jnp.stack(relative, axis=0), lax.axis_index(axis), axis=0)
+    forward = [(i, (i + 1) % count) for i in range(count)]
+    backward = [(i, (i - 1) % count) for i in range(count)]
+    ahead = [piece]
+    behind = []
+    sent_ahead = piece
+    sent_behind = piece
+    for step in range(1, count // 2 + 1):
+        sent_ahead = lax.ppermute(sent_ahead, axis, forward)
+        behind.append(sent_ahead)
+        if step < count - count // 2:
+            sent_behind = lax.ppermute(sent_behind, axis, backward)
+            ahead.append(sent_behind)
+    relative = jnp.stack(ahead + behind[::-1], axis=0)
+    return jnp.roll(relative, lax.axis_index(axis), axis=0)
 
 
 def request_info(lengths, token_index):
@@ -86,7 +95,8 @@
     half = out_weight.shape[1] // 2
     weight_pair = lax.all_gather(out_weight, "core", axis=0, tiled=True)
     weight_rows = lax.dynamic_slice_in_dim(weight_pair, core_rank * half, half, 1)
-    weight_rows = lax.all_gather(weight_rows, "x", axis=0, tiled=True)
+    weight_rows = ring_gather(weight_rows, "x")
+    weight_rows = weight_rows.reshape(-1, half)
     weight_rows, query_proj, key_proj = lax.optimization_barrier(
         (weight_rows, query_proj, key_proj)
     )

time: 146 us -> 145 us (level)
  the two profiles are of different devices: /device:TPU:257 before, /device:TPU:256 now
where the time goes in v7:
time: 145 us; the launch traced here: 144 us
  waiting for transfers between devices  63.4 us (44%)
  starting transfers between devices  31.7 us (22%)
  local copies, waits for them, and re-layouts  16.8 us (12%)
  between operations  14.7 us (10%)
  matrix products  10.9 us (8%)
  other arithmetic  4.74 us (3%)
  blocking collectives  2.2 us (2%)
    ppermute x4, waiting for transfers between devices, passed_along(): return lax.ppermute(array, axis, pairs)  47.1 us
    ppermute x4, waiting for transfers between devices, ring_gather(): sent_ahead = lax.ppermute(sent_ahead, axis, forward)  16.2 us
    ppermute x4, starting transfers between devices, passed_along(): return lax.ppermute(array, axis, pairs)  11.7 us
    ppermute x4, starting transfers between devices, ring_gather(): sent_ahead = lax.ppermute(sent_ahead, axis, forward)  9.79 us
    ppermute x2, starting transfers between devices, ring_gather(): sent_behind = lax.ppermute(sent_behind, axis, backward)  8.2 us
    unnamed x42, local copies, waits for them, and re-layouts  4.78 us
    dot_general x1, matrix products, attend_block(): jnp.einsum('hqk,khd->qhd', probs, value_rows, preferred_element_type=jnp....  4.08 us
    another operation x1, local copies, waits for them, and re-layouts, local_body(): key_all = key_stack.reshape(key_rows, local_heads, DH)  3.56 us
  transfers between devices with their start and end apart: 12, of which 7 were waited for; matrix products, arithmetic and copies ran while one was open for 20% of the time, Pallas kernels for 0%

profile of v7, /device:TPU:256, one launch (start us, length us, event | category | flops | bytes accessed | tf_op | source)
XLA Modules:
  0.0 144.5 jit_solution(297387844600835207)
XLA Ops:
  7.2 2.2 %all_gather.6 = bf16[32,1024]{1,0:T(8,128)(2,1)S(1)} all-gather(bf16[16,1024]{1,0:T(8,128)(2,1)} %param.12), channel_id=1, replica_groups=mesh['z'=16,'x'=4,'core'=2,'head'=4] {'core'}, dimensions={0}, use_global_device_ids=true | all-gather | bytes 98304 | tf_op jit(solution)/shard_map/all_gather | solution.py:96
  9.4 4.7 %collective-permute-start = (bf16[32,512]{1,0:T(8,128)(2,1)S(1)}, bf16[32,512]{1,0:T(8,128)(2,1)S(1)}, u32[]{:S(2)}, u32[]{:S(2)}) collective-permute-start(bf16[32,512]{1,0:T(8,128)(2,1)S(1)} %get-tuple-element.19), channel_id=1, source_target_pairs={{0,24},{8,0},{16,8},{24,16},{1,25},{9,1},{17,9},{25,17},{2,26},{10... | collective-permute-start | bytes 98312 | tf_op jit(solution)/shard_map/ppermute | solution.py:41
  14.1 1.9 %collective-permute-start.1 = (bf16[32,512]{1,0:T(8,128)(2,1)S(1)}, bf16[32,512]{1,0:T(8,128)(2,1)S(1)}, u32[]{:S(2)}, u32[]{:S(2)}) collective-permute-start(bf16[32,512]{1,0:T(8,128)(2,1)S(1)} %get-tuple-element.19), channel_id=1, source_target_pairs={{0,8},{8,16},{16,24},{24,0},{1,9},{9,17},{17,25},{25,1},{2,10},{10... | collective-permute-start | bytes 98312 | tf_op jit(solution)/shard_map/ppermute | solution.py:38
  18.3 1.1 copy.68
  19.4 1.7 %collective-permute-done.1 = bf16[32,512]{1,0:T(8,128)(2,1)S(1)} collective-permute-done((bf16[32,512]{1,0:T(8,128)(2,1)S(1)}, bf16[32,512]{1,0:T(8,128)(2,1)S(1)}, u32[]{:S(2)}, u32[]{:S(2)}) %collective-permute-start.1) | collective-permute-done | bytes 32800 | tf_op jit(solution)/shard_map/ppermute | solution.py:38
  21.1 1.9 %collective-permute-start.2 = (bf16[32,512]{1,0:T(8,128)(2,1)S(1)}, bf16[32,512]{1,0:T(8,128)(2,1)S(1)}, u32[]{:S(2)}, u32[]{:S(2)}) collective-permute-start(bf16[32,512]{1,0:T(8,128)(2,1)S(1)} %collective-permute-done.1), channel_id=1, source_target_pairs={{0,8},{8,16},{16,24},{24,0},{1,9},{9,17},{17,25},{25,1},{2,10},{10... | collective-permute-start | bytes 98312 | tf_op jit(solution)/shard_map/ppermute | solution.py:38
  23.1 5.1 %collective-permute-done.2 = bf16[32,512]{1,0:T(8,128)(2,1)S(1)} collective-permute-done((bf16[32,512]{1,0:T(8,128)(2,1)S(1)}, bf16[32,512]{1,0:T(8,128)(2,1)S(1)}, u32[]{:S(2)}, u32[]{:S(2)}) %collective-permute-start.2) | collective-permute-done | bytes 32800 | tf_op jit(solution)/shard_map/ppermute | solution.py:38
  28.9 1.1 compare_and_fusion
  31.0 1.9 %collective-permute-start.3 = (bf16[2,256,512]{1,2,0:T(8,128)(2,1)S(1)}, bf16[2,256,512]{1,2,0:T(8,128)(2,1)}, u32[]{:S(2)}, u32[]{:S(2)}) collective-permute-start(bf16[2,256,512]{1,2,0:T(8,128)(2,1)S(1)} %pad_maximum_fusion), channel_id=1, source_target_pairs={{0,16},{4,20},{8,24},{12,28},{16,32},{20,36},{24,40},{28,44},{32,4... | collective-permute-start | bytes 1572872 | tf_op jit(solution)/shard_map/ppermute | solution.py:26
  33.0 1.9 %collective-permute-start.4 = (bf16[2,256,512]{1,2,0:T(8,128)(2,1)S(1)}, bf16[2,256,512]{1,2,0:T(8,128)(2,1)}, u32[]{:S(2)}, u32[]{:S(2)}) collective-permute-start(bf16[2,256,512]{1,2,0:T(8,128)(2,1)S(1)} %pad_maximum_fusion), channel_id=1, source_target_pairs={{0,12},{4,16},{8,20},{12,24},{16,28},{20,32},{24,36},{28,40},{32,4... | collective-permute-start | bytes 1572872 | tf_op jit(solution)/shard_map/ppermute | solution.py:26
  34.9 3.1 %collective-permute-start.5 = (bf16[2,256,512]{1,2,0:T(8,128)(2,1)S(1)}, bf16[2,256,512]{1,2,0:T(8,128)(2,1)S(1)}, u32[]{:S(2)}, u32[]{:S(2)}) collective-permute-start(bf16[2,256,512]{1,2,0:T(8,128)(2,1)S(1)} %pad_maximum_fusion), channel_id=1, source_target_pairs={{0,8},{4,12},{8,16},{12,20},{16,24},{20,28},{24,32},{28,36},{32,40... | collective-permute-start | bytes 1572872 | tf_op jit(solution)/shard_map/ppermute | solution.py:26
  38.0 4.8 %collective-permute-start.6 = (bf16[2,256,512]{1,2,0:T(8,128)(2,1)S(1)}, bf16[2,256,512]{1,2,0:T(8,128)(2,1)S(1)}, u32[]{:S(2)}, u32[]{:S(2)}) collective-permute-start(bf16[2,256,512]{1,2,0:T(8,128)(2,1)S(1)} %pad_maximum_fusion), channel_id=1, source_target_pairs={{0,4},{4,8},{8,12},{12,16},{16,20},{20,24},{24,28},{28,32},{32,36}... | collective-permute-start | bytes 1572872 | tf_op jit(solution)/shard_map/ppermute | solution.py:26
  43.6 1.0 pad_maximum_fusion.3
  44.5 9.6 %collective-permute-done.3 = bf16[2,256,512]{1,2,0:T(8,128)(2,1)} collective-permute-done((bf16[2,256,512]{1,2,0:T(8,128)(2,1)S(1)}, bf16[2,256,512]{1,2,0:T(8,128)(2,1)}, u32[]{:S(2)}, u32[]{:S(2)}) %collective-permute-start.3) | collective-permute-done | bytes 524320 | tf_op jit(solution)/shard_map/ppermute | solution.py:26
  54.2 1.1 bitcast_dynamic-update-slice_fusion.4
  55.3 3.4 %collective-permute-done.4 = bf16[2,256,512]{1,2,0:T(8,128)(2,1)} collective-permute-done((bf16[2,256,512]{1,2,0:T(8,128)(2,1)S(1)}, bf16[2,256,512]{1,2,0:T(8,128)(2,1)}, u32[]{:S(2)}, u32[]{:S(2)}) %collective-permute-start.4) | collective-permute-done | bytes 524320 | tf_op jit(solution)/shard_map/ppermute | solution.py:26
  58.7 1.1 bitcast_dynamic-update-slice_fusion.3
  59.7 30.6 %collective-permute-done.5 = bf16[2,256,512]{1,2,0:T(8,128)(2,1)S(1)} collective-permute-done((bf16[2,256,512]{1,2,0:T(8,128)(2,1)S(1)}, bf16[2,256,512]{1,2,0:T(8,128)(2,1)S(1)}, u32[]{:S(2)}, u32[]{:S(2)}) %collective-permute-start.5) | collective-permute-done | bytes 524320 | tf_op jit(solution)/shard_map/ppermute | solution.py:26
  90.4 3.5 %collective-permute-done.6 = bf16[2,256,512]{1,2,0:T(8,128)(2,1)S(1)} collective-permute-done((bf16[2,256,512]{1,2,0:T(8,128)(2,1)S(1)}, bf16[2,256,512]{1,2,0:T(8,128)(2,1)S(1)}, u32[]{:S(2)}, u32[]{:S(2)}) %collective-permute-start.6) | collective-permute-done | bytes 524320 | tf_op jit(solution)/shard_map/ppermute | solution.py:26
  94.2 1.6 %copy.73 = bf16[1,5,256,512]{3,2,1,0:T(8,128)(2,1)} copy(bf16[1,5,256,512]{2,3,0,1:T(8,128)(2,1)S(1)} %get-tuple-element.20) | data formatting | bytes 2621440 | tf_op jit(solution)/shard_map/slice | solution.py:117
  95.8 3.6 %reshape_squeeze.7 = bf16[1280,4,128]{2,1,0:T(4,128)(2,1)} reshape(bf16[1,5,256,512]{3,2,1,0:T(8,128)(2,1)} %copy.73) | data formatting | bytes 2621440 | tf_op jit(solution)/shard_map/reshape;squeeze | solution.py:120
  100.2 2.3 %reshape.216 = bf16[1280,4,128]{0,2,1:T(8,128)(2,1)} reshape(bf16[1,5,256,512]{2,1,3,0:T(8,128)(2,1)S(1)} %copy.85) | data formatting | bytes 2621440 | tf_op jit(solution)/shard_map/reshape;squeeze | solution.py:121
  102.5 3.2 %exponential_reduce_fusion = f32[4,256]{1,0:T(4,128)S(1)} fusion(bf16[256,4,128]{2,0,1:T(8,128)(2,1)} %pad_maximum_fusion.3, pred[256,1280]{1,0:T(8,128)(4,1)} %compare_and_fusion, bf16[1280,4,128]{2,1,0:T(4,128)(2,1)S(1)} %copy-done.2), kind=kOutput, calls=%fused_computation.4 | convolution fusion | flops 340788480 | bytes 1904640 | tf_op jit(solution)/shard_map/sub | solution.py:85
  105.7 4.1 %fusion.8 = bf16[4,128,256]{2,1,0:T(8,128)(2,1)S(1)} fusion(bf16[1280,4,128]{0,2,1:T(8,128)(2,1)} %reshape.216, f32[4,256]{1,0:T(4,128)S(1)} %exponential_reduce_fusion, bf16[256,4,128]{2,0,1:T(8,128)(2,1)} %pad_maximum_fusion.3, pred[256,1280]{1,0:T(8,128)(4,1)} %compare_and_fusion, bf16[1280,4,128]{2,1,0:T(4,128)(2,1)S(1)} %copy-done.3), kind=kOutput, calls=%fused_computation.15 | convolution fusion | flops 677775616 | bytes 3477504 | tf_op jit(solution)/shard_map/hqk,khd->qhd/dot_general | solution.py:87
  109.9 3.5 %collective-permute-start.8 = (bf16[256,512]{1,0:T(8,128)(2,1)S(1)}, bf16[256,512]{1,0:T(8,128)(2,1)S(1)}, u32[]{:S(2)}, u32[]{:S(2)}) collective-permute-start(bf16[256,512]{1,0:T(8,128)(2,1)S(1)} %copy.76), channel_id=1, source_target_pairs={{0,1},{1,2},{2,3},{3,0},{4,5},{5,6},{6,7},{7,4},{8,9},{9,10},{10,1... | collective-permute-start | bytes 786440 | tf_op jit(solution)/shard_map/ppermute | solution.py:38
  114.3 3.5 %collective-permute-start.7 = (bf16[256,512]{1,0:T(8,128)(2,1)S(1)}, bf16[256,512]{1,0:T(8,128)(2,1)S(1)}, u32[]{:S(2)}, u32[]{:S(2)}) collective-permute-start(bf16[256,512]{1,0:T(8,128)(2,1)S(1)} %copy.76), channel_id=1, source_target_pairs={{0,3},{1,0},{2,1},{3,2},{4,7},{5,4},{6,5},{7,6},{8,11},{9,8},{10,9... | collective-permute-start | bytes 786440 | tf_op jit(solution)/shard_map/ppermute | solution.py:41
  117.9 1.9 %collective-permute-start.10 = (bf16[2048,512]{1,0:T(8,128)(2,1)}, bf16[2048,512]{1,0:T(8,128)(2,1)}, u32[]{:S(2)}, u32[]{:S(2)}) collective-permute-start(bf16[2048,512]{1,0:T(8,128)(2,1)} %all-gather.2.cloned.1.call-done), channel_id=1, source_target_pairs={{0,4},{4,0},{1,5},{5,1},{2,6},{6,2},{3,7},{7,3},{8,12},{12,8},{9,1... | collective-permute-start | bytes 6291464 | tf_op jit(solution)/shard_map/ppermute | solution.py:104
  120.5 0.9 copy.83
  121.5 2.4 %collective-permute-start.9 = (bf16[256,512]{1,0:T(8,128)(2,1)S(1)}, bf16[256,512]{1,0:T(8,128)(2,1)S(1)}, u32[]{:S(2)}, u32[]{:S(2)}) collective-permute-start(bf16[256,512]{1,0:T(8,128)(2,1)S(1)} %collective-permute-done.8), channel_id=1, source_target_pairs={{0,1},{1,2},{2,3},{3,0},{4,5},{5,6},{6,7},{7,4},{8,9},{9,10},{10,1... | collective-permute-start | bytes 786440 | tf_op jit(solution)/shard_map/ppermute | solution.py:38
  124.1 9.4 %collective-permute-done.9 = bf16[256,512]{1,0:T(8,128)(2,1)S(1)} collective-permute-done((bf16[256,512]{1,0:T(8,128)(2,1)S(1)}, bf16[256,512]{1,0:T(8,128)(2,1)S(1)}, u32[]{:S(2)}, u32[]{:S(2)}) %collective-permute-start.9) | collective-permute-done | bytes 262176 | tf_op jit(solution)/shard_map/ppermute | solution.py:38
  134.4 2.3 %fusion.6 = bf16[256,512]{1,0:T(8,128)(2,1)S(1)} fusion(bf16[4,512,512]{2,1,0:T(8,128)(2,1)} %bitcast.26, bf16[8,256,512]{2,1,0:T(8,128)(2,1)S(1)} %bitcast_dynamic-update-slice_fusion.6, s32[]{:T(128)S(6)} %select_n.53, f32[512]{0:T(512)S(1)} %get-tuple-element.29), kind=kOutput, calls=%fused_computation.13 | convolution fusion | flops 537133056 | bytes 3409924 | tf_op jit(solution)/shard_map/gtk,gkc->tc/dot_general | solution.py:136
  136.7 0.9 maximum_select_fusion
  (87 shorter events, 8.5 us)
Async XLA Ops:
  7.2 22.8 %copy-start.5 = (bf16[256,512]{1,0:T(8,128)(2,1)S(1)}, bf16[256,512]{1,0:T(8,128)(2,1)}, u32[]{:S(2)}) copy-start(bf16[256,512]{1,0:T(8,128)(2,1)} %param.8) | copy-start | bytes 786436
  7.2 110.7 %all-gather.2.cloned.1.call-start = ((), (), s32[]{:S(2)}) async-start(), calls=%async_computation | async-start | bytes 2228224 | tf_op jit(solution)/shard_map/all_gather | solution.py:103
  9.4 13.6 %collective-permute-start = (bf16[32,512]{1,0:T(8,128)(2,1)S(1)}, bf16[32,512]{1,0:T(8,128)(2,1)S(1)}, u32[]{:S(2)}, u32[]{:S(2)}) collective-permute-start(bf16[32,512]{1,0:T(8,128)(2,1)S(1)} %get-tuple-element.19), channel_id=1, source_target_pairs={{0,24},{8,0},{16,8},{24,16},{1,25},{9,1},{17,9},{25,17},{2,26},{10... | collective-permute-start | bytes 98312 | tf_op jit(solution)/shard_map/ppermute | solution.py:41
  14.1 7.0 %collective-permute-start.1 = (bf16[32,512]{1,0:T(8,128)(2,1)S(1)}, bf16[32,512]{1,0:T(8,128)(2,1)S(1)}, u32[]{:S(2)}, u32[]{:S(2)}) collective-permute-start(bf16[32,512]{1,0:T(8,128)(2,1)S(1)} %get-tuple-element.19), channel_id=1, source_target_pairs={{0,8},{8,16},{16,24},{24,0},{1,9},{9,17},{17,25},{25,1},{2,10},{10... | collective-permute-start | bytes 98312 | tf_op jit(solution)/shard_map/ppermute | solution.py:38
  21.1 7.0 %collective-permute-start.2 = (bf16[32,512]{1,0:T(8,128)(2,1)S(1)}, bf16[32,512]{1,0:T(8,128)(2,1)S(1)}, u32[]{:S(2)}, u32[]{:S(2)}) collective-permute-start(bf16[32,512]{1,0:T(8,128)(2,1)S(1)} %collective-permute-done.1), channel_id=1, source_target_pairs={{0,8},{8,16},{16,24},{24,0},{1,9},{9,17},{17,25},{25,1},{2,10},{10... | collective-permute-start | bytes 98312 | tf_op jit(solution)/shard_map/ppermute | solution.py:38
  30.5 2.4 %copy-start.9 = (s32[2]{0:T(128)S(1)}, s32[2]{0:T(128)}, u32[]{:S(2)}) copy-start(s32[2]{0:T(128)} %param.11) | copy-start | bytes 28
  30.5 12.3 %copy-start.6 = (bf16[256,512]{1,0:T(8,128)(2,1)S(1)}, bf16[256,512]{1,0:T(8,128)(2,1)}, u32[]{:S(2)}) copy-start(bf16[256,512]{1,0:T(8,128)(2,1)} %param.7) | copy-start | bytes 786436
  30.9 63.0 %copy-start = (bf16[256,4,128]{0,2,1:T(8,128)(2,1)}, bf16[256,4,128]{0,2,1:T(8,128)(2,1)S(1)}, u32[]{:S(2)}) copy-start(bf16[256,4,128]{0,2,1:T(8,128)(2,1)S(1)} %maximum_convert_fusion) | copy-start | bytes 786436
  31.0 23.2 %collective-permute-start.3 = (bf16[2,256,512]{1,2,0:T(8,128)(2,1)S(1)}, bf16[2,256,512]{1,2,0:T(8,128)(2,1)}, u32[]{:S(2)}, u32[]{:S(2)}) collective-permute-start(bf16[2,256,512]{1,2,0:T(8,128)(2,1)S(1)} %pad_maximum_fusion), channel_id=1, source_target_pairs={{0,16},{4,20},{8,24},{12,28},{16,32},{20,36},{24,40},{28,44},{32,4... | collective-permute-start | bytes 1572872 | tf_op jit(solution)/shard_map/ppermute | solution.py:26
  33.0 25.7 %collective-permute-start.4 = (bf16[2,256,512]{1,2,0:T(8,128)(2,1)S(1)}, bf16[2,256,512]{1,2,0:T(8,128)(2,1)}, u32[]{:S(2)}, u32[]{:S(2)}) collective-permute-start(bf16[2,256,512]{1,2,0:T(8,128)(2,1)S(1)} %pad_maximum_fusion), channel_id=1, source_target_pairs={{0,12},{4,16},{8,20},{12,24},{16,28},{20,32},{24,36},{28,40},{32,4... | collective-permute-start | bytes 1572872 | tf_op jit(solution)/shard_map/ppermute | solution.py:26
  34.9 55.4 %collective-permute-start.5 = (bf16[2,256,512]{1,2,0:T(8,128)(2,1)S(1)}, bf16[2,256,512]{1,2,0:T(8,128)(2,1)S(1)}, u32[]{:S(2)}, u32[]{:S(2)}) collective-permute-start(bf16[2,256,512]{1,2,0:T(8,128)(2,1)S(1)} %pad_maximum_fusion), channel_id=1, source_target_pairs={{0,8},{4,12},{8,16},{12,20},{16,24},{20,28},{24,32},{28,36},{32,40... | collective-permute-start | bytes 1572872 | tf_op jit(solution)/shard_map/ppermute | solution.py:26
  38.0 55.9 %collective-permute-start.6 = (bf16[2,256,512]{1,2,0:T(8,128)(2,1)S(1)}, bf16[2,256,512]{1,2,0:T(8,128)(2,1)S(1)}, u32[]{:S(2)}, u32[]{:S(2)}) collective-permute-start(bf16[2,256,512]{1,2,0:T(8,128)(2,1)S(1)} %pad_maximum_fusion), channel_id=1, source_target_pairs={{0,4},{4,8},{8,12},{12,16},{16,20},{20,24},{24,28},{28,32},{32,36}... | collective-permute-start | bytes 1572872 | tf_op jit(solution)/shard_map/ppermute | solution.py:26
  100.2 2.3 %copy-start.2 = (bf16[1280,4,128]{2,1,0:T(4,128)(2,1)S(1)}, bf16[1280,4,128]{2,1,0:T(4,128)(2,1)}, u32[]{:S(2)}) copy-start(bf16[1280,4,128]{2,1,0:T(4,128)(2,1)} %reshape_squeeze.7) | copy-start | bytes 3932164
  102.5 3.2 %copy-start.3 = (bf16[1280,4,128]{2,1,0:T(4,128)(2,1)S(1)}, bf16[1280,4,128]{2,1,0:T(4,128)(2,1)}, u32[]{:S(2)}) copy-start(bf16[1280,4,128]{2,1,0:T(4,128)(2,1)} %reshape_squeeze.7) | copy-start | bytes 3932164
  105.7 7.8 %copy-start.7 = (f32[1024]{0:T(1024)S(1)}, f32[1024]{0:T(1024)}, u32[]{:S(2)}) copy-start(f32[1024]{0:T(1024)} %param.13) | copy-start | bytes 12292
  105.7 7.9 %copy-start.4 = (bf16[256,512]{1,0:T(8,128)(2,1)S(1)}, bf16[256,512]{1,0:T(8,128)(2,1)}, u32[]{:S(2)}) copy-start(bf16[256,512]{1,0:T(8,128)(2,1)} %param.9) | copy-start | bytes 786436
  105.7 8.2 %copy-start.1 = (bf16[256,4,128]{0,2,1:T(8,128)(2,1)S(1)}, bf16[256,4,128]{0,2,1:T(8,128)(2,1)}, u32[]{:S(2)}) copy-start(bf16[256,4,128]{0,2,1:T(8,128)(2,1)} %copy-done) | copy-start | bytes 786436
  109.9 11.6 %collective-permute-start.8 = (bf16[256,512]{1,0:T(8,128)(2,1)S(1)}, bf16[256,512]{1,0:T(8,128)(2,1)S(1)}, u32[]{:S(2)}, u32[]{:S(2)}) collective-permute-start(bf16[256,512]{1,0:T(8,128)(2,1)S(1)} %copy.76), channel_id=1, source_target_pairs={{0,1},{1,2},{2,3},{3,0},{4,5},{5,6},{6,7},{7,4},{8,9},{9,10},{10,1... | collective-permute-start | bytes 786440 | tf_op jit(solution)/shard_map/ppermute | solution.py:38
  114.3 9.7 %collective-permute-start.7 = (bf16[256,512]{1,0:T(8,128)(2,1)S(1)}, bf16[256,512]{1,0:T(8,128)(2,1)S(1)}, u32[]{:S(2)}, u32[]{:S(2)}) collective-permute-start(bf16[256,512]{1,0:T(8,128)(2,1)S(1)} %copy.76), channel_id=1, source_target_pairs={{0,3},{1,0},{2,1},{3,2},{4,7},{5,4},{6,5},{7,6},{8,11},{9,8},{10,9... | collective-permute-start | bytes 786440 | tf_op jit(solution)/shard_map/ppermute | solution.py:41
  117.9 16.5 %collective-permute-start.10 = (bf16[2048,512]{1,0:T(8,128)(2,1)}, bf16[2048,512]{1,0:T(8,128)(2,1)}, u32[]{:S(2)}, u32[]{:S(2)}) collective-permute-start(bf16[2048,512]{1,0:T(8,128)(2,1)} %all-gather.2.cloned.1.call-done), channel_id=1, source_target_pairs={{0,4},{4,0},{1,5},{5,1},{2,6},{6,2},{3,7},{7,3},{8,12},{12,8},{9,1... | collective-permute-start | bytes 6291464 | tf_op jit(solution)/shard_map/ppermute | solution.py:104
  121.5 12.1 %copy-start.8 = (bf16[2048,512]{1,0:T(8,128)(2,1)S(1)}, bf16[2048,512]{1,0:T(8,128)(2,1)}, u32[]{:S(2)}) copy-start(bf16[2048,512]{1,0:T(8,128)(2,1)} %all-gather.2.cloned.1.call-done) | copy-start | bytes 6291460
  121.5 11.9 %collective-permute-start.9 = (bf16[256,512]{1,0:T(8,128)(2,1)S(1)}, bf16[256,512]{1,0:T(8,128)(2,1)S(1)}, u32[]{:S(2)}, u32[]{:S(2)}) collective-permute-start(bf16[256,512]{1,0:T(8,128)(2,1)S(1)} %collective-permute-done.8), channel_id=1, source_target_pairs={{0,1},{1,2},{2,3},{3,0},{4,5},{5,6},{6,7},{7,4},{8,9},{9,10},{10,1... | collective-permute-start | bytes 786440 | tf_op jit(solution)/shard_map/ppermute | solution.py:38
Sparse Core Ops, SparseCore 0:
  29.0 67.4 all-gather.1

commit v8 on v7

--- a/solution.py
+++ b/solution.py
@@ -75,17 +75,21 @@
     return turned.astype(jnp.bfloat16)
 
 
-def attend_block(query_rot, key_rot, value_rows, query_id, query_token, key_id, key_token):
-    scores = jnp.einsum("qhd,khd->hqk", query_rot, key_rot, preferred_element_type=jnp.float32) * (
-        1.0 / math.sqrt(DH)
-    )
+def attend_heads(query_rot, key_rot, value_rows, query_id, query_token, key_id, key_token):
     allowed = (query_id[:, None] == key_id[None, :]) & (key_token[None, :] <= query_token[:, None])
-    scores = jnp.where(allowed[None], scores, -jnp.inf)
-    row_max = jnp.max(scores, axis=-1, keepdims=True)
-    raised = jnp.exp(scores - row_max)
-    probs = (raised / jnp.sum(raised, axis=-1, keepdims=True)).astype(jnp.bfloat16)
-    mixed = jnp.einsum("hqk,khd->qhd", probs, value_rows, preferred_element_type=jnp.float32)
-    return mixed.astype(jnp.bfloat16)
+    outputs = []
+    for head in range(query_rot.shape[1] // DH):
+        columns = slice(head * DH, (head + 1) * DH)
+        scores = jnp.dot(
+            query_rot[:, columns], key_rot[:, columns].T, preferred_element_type=jnp.float32
+        ) * (1.0 / math.sqrt(DH))
+        scores = jnp.where(allowed, scores, -jnp.inf)
+        row_max = jnp.max(scores, axis=-1, keepdims=True)
+        raised = jnp.exp(scores - row_max)
+        probs = (raised / jnp.sum(raised, axis=-1, keepdims=True)).astype(jnp.bfloat16)
+        mixed = jnp.dot(probs, value_rows[:, columns], preferred_element_type=jnp.float32)
+        outputs.append(mixed.astype(jnp.bfloat16))
+    return jnp.concatenate(outputs, axis=1)
 
 
 def local_body(query_proj, key_proj, value_proj, lengths, page_table, out_weight, out_bias):
@@ -95,8 +99,7 @@
     half = out_weight.shape[1] // 2
     weight_pair = lax.all_gather(out_weight, "core", axis=0, tiled=True)
     weight_rows = lax.dynamic_slice_in_dim(weight_pair, core_rank * half, half, 1)
-    weight_rows = ring_gather(weight_rows, "x")
-    weight_rows = weight_rows.reshape(-1, half)
+    weight_rows = lax.all_gather(weight_rows, "x", axis=0, tiled=True)
     weight_rows, query_proj, key_proj = lax.optimization_barrier(
         (weight_rows, query_proj, key_proj)
     )
@@ -113,16 +116,20 @@
     halo_list = [halo]
     for distance in range(1, REACH + 1):
         halo_list.append(passed_along(halo, REQ, distance))
-    halo_stack = jnp.stack(halo_list[::-1], axis=1)
-    key_stack = halo_stack[0]
-    value_stack = halo_stack[1]
+    key_all = jnp.concatenate([part[0] for part in halo_list[::-1]], axis=0)
+    value_all = jnp.concatenate([part[1] for part in halo_list[::-1]], axis=0)
     key_rows = (REACH + 1) * TOK_DEV
-    key_all = key_stack.reshape(key_rows, local_heads, DH)
-    value_all = value_stack.reshape(key_rows, local_heads, DH)
     key_tokens = first_token - REACH * TOK_DEV + jnp.arange(key_rows, dtype=jnp.int32)
     key_id, _ = request_info(lengths, key_tokens)
-    mixed = attend_block(query_rot, key_all, value_all, request_id, own_tokens, key_id, key_tokens)
-    heads_out = mixed.reshape(TOK_DEV, local_heads * DH)
+    heads_out = attend_heads(
+        query_rot.reshape(TOK_DEV, local_heads * DH),
+        key_all,
+        value_all,
+        request_id,
+        own_tokens,
+        key_id,
+        key_tokens,
+    )
     heads_all = ring_gather(heads_out, "head")
     groups = heads_all.shape[0]
     weight_rows = weight_rows.reshape(groups, -1, half)

time: 145 us -> 147 us (1.014)
  the two profiles are of different devices: /device:TPU:256 before, /device:TPU:1 now
where the time goes in v8:
time: 147 us; the launch traced here: 145 us
  waiting for transfers between devices  57.1 us (39%)
  starting transfers between devices  32.3 us (22%)
  blocking collectives  18.4 us (13%)
  between operations  14.5 us (10%)
  local copies, waits for them, and re-layouts  9.13 us (6%)
  matrix products  7.75 us (5%)
  other arithmetic  5.95 us (4%)
    all_gather x1, waiting for transfers between devices, local_body(): weight_rows = lax.all_gather(weight_rows, 'z', axis=0, tiled=True)  24.9 us
    ppermute x4, waiting for transfers between devices, passed_along(): return lax.ppermute(array, axis, pairs)  24.4 us
    ppermute x4, starting transfers between devices, passed_along(): return lax.ppermute(array, axis, pairs)  12.9 us
    ppermute x1, starting transfers between devices, local_body(): weight_other = lax.ppermute(weight_rows, 'core', [(0, 1), (1, 0)])  11 us
    all_gather x1, blocking collectives, local_body(): weight_rows = lax.all_gather(weight_rows, 'x', axis=0, tiled=True)  9.83 us
    all_gather x1, blocking collectives, local_body(): weight_pair = lax.all_gather(out_weight, 'core', axis=0, tiled=True)  8.55 us
    ppermute x2, waiting for transfers between devices, ring_gather(): sent_ahead = lax.ppermute(sent_ahead, axis, forward)  7.82 us
    ppermute x2, starting transfers between devices, ring_gather(): sent_ahead = lax.ppermute(sent_ahead, axis, forward)  6.41 us
  transfers between devices with their start and end apart: 9, of which 5 were waited for; matrix products, arithmetic and copies ran while one was open for 9% of the time, Pallas kernels for 0%

profile of v8, /device:TPU:1, one launch (start us, length us, event | category | flops | bytes accessed | tf_op | source)
XLA Modules:
  0.0 145.2 jit_solution(10717948612411015482)
XLA Ops:
  7.2 0.7 copy.25
  8.2 0.7 multiply_subtract_fusion.1
  9.3 8.6 %all_gather.9 = bf16[32,1024]{1,0:T(8,128)(2,1)S(1)} all-gather(bf16[16,1024]{1,0:T(8,128)(2,1)} %param.12), channel_id=1, replica_groups=mesh['z'=16,'x'=4,'core'=2,'head'=4] {'core'}, dimensions={0}, use_global_device_ids=true | all-gather | bytes 98304 | tf_op jit(solution)/shard_map/all_gather | solution.py:100
  17.9 9.8 %all_gather.10 = bf16[128,512]{1,0:T(8,128)(2,1)} all-gather(bf16[32,512]{1,0:T(8,128)(2,1)S(1)} %constant_dynamic-slice_fusion), channel_id=1, replica_groups=mesh['z'=16,'x'=4,'core'=2,'head'=4] {'x'}, dimensions={0}, use_global_device_ids=true | all-gather | bytes 163840 | tf_op jit(solution)/shard_map/all_gather | solution.py:102
  27.7 1.1 reshape.160
  29.1 0.5 multiply_subtract_fusion
  29.6 0.6 maximum_convert_fusion
  30.4 3.9 %collective-permute-start = (bf16[2,256,512]{2,1,0:T(8,128)(2,1)S(1)}, bf16[2,256,512]{2,1,0:T(8,128)(2,1)}, u32[]{:S(2)}, u32[]{:S(2)}) collective-permute-start(bf16[2,256,512]{2,1,0:T(8,128)(2,1)S(1)} %pad_maximum_fusion), channel_id=1, source_target_pairs={{0,16},{4,20},{8,24},{12,28},{16,32},{20,36},{24,40},{28,44},{32,4... | collective-permute-start | bytes 1572872 | tf_op jit(solution)/shard_map/ppermute | solution.py:26
  34.2 5.1 %collective-permute-start.1 = (bf16[2,256,512]{2,1,0:T(8,128)(2,1)S(1)}, bf16[2,256,512]{2,1,0:T(8,128)(2,1)}, u32[]{:S(2)}, u32[]{:S(2)}) collective-permute-start(bf16[2,256,512]{2,1,0:T(8,128)(2,1)S(1)} %pad_maximum_fusion), channel_id=1, source_target_pairs={{0,12},{4,16},{8,20},{12,24},{16,28},{20,32},{24,36},{28,40},{32,4... | collective-permute-start | bytes 1572872 | tf_op jit(solution)/shard_map/ppermute | solution.py:26
  39.3 2.1 %collective-permute-start.2 = (bf16[2,256,512]{2,1,0:T(8,128)(2,1)S(1)}, bf16[2,256,512]{2,1,0:T(8,128)(2,1)}, u32[]{:S(2)}, u32[]{:S(2)}) collective-permute-start(bf16[2,256,512]{2,1,0:T(8,128)(2,1)S(1)} %pad_maximum_fusion), channel_id=1, source_target_pairs={{0,8},{4,12},{8,16},{12,20},{16,24},{20,28},{24,32},{28,36},{32,40... | collective-permute-start | bytes 1572872 | tf_op jit(solution)/shard_map/ppermute | solution.py:26
  41.4 1.9 %collective-permute-start.3 = (bf16[2,256,512]{2,1,0:T(8,128)(2,1)S(1)}, bf16[2,256,512]{2,1,0:T(8,128)(2,1)S(1)}, u32[]{:S(2)}, u32[]{:S(2)}) collective-permute-start(bf16[2,256,512]{2,1,0:T(8,128)(2,1)S(1)} %pad_maximum_fusion), channel_id=1, source_target_pairs={{0,4},{4,8},{8,12},{12,16},{16,20},{20,24},{24,28},{28,32},{32,36}... | collective-permute-start | bytes 1572872 | tf_op jit(solution)/shard_map/ppermute | solution.py:26
  43.7 0.5 subtract_convert_fusion
  44.4 0.6 pad_maximum_fusion.3
  45.7 1.1 fusion.26
  46.8 6.0 %collective-permute-done.1 = bf16[2,256,512]{2,1,0:T(8,128)(2,1)} collective-permute-done((bf16[2,256,512]{2,1,0:T(8,128)(2,1)S(1)}, bf16[2,256,512]{2,1,0:T(8,128)(2,1)}, u32[]{:S(2)}, u32[]{:S(2)}) %collective-permute-start.1) | collective-permute-done | bytes 524320 | tf_op jit(solution)/shard_map/ppermute | solution.py:26
  52.8 1.1 fusion.25
  53.8 10.2 %collective-permute-done.2 = bf16[2,256,512]{2,1,0:T(8,128)(2,1)} collective-permute-done((bf16[2,256,512]{2,1,0:T(8,128)(2,1)S(1)}, bf16[2,256,512]{2,1,0:T(8,128)(2,1)}, u32[]{:S(2)}, u32[]{:S(2)}) %collective-permute-start.2) | collective-permute-done | bytes 524320 | tf_op jit(solution)/shard_map/ppermute | solution.py:26
  64.0 1.1 fusion.24
  65.1 8.3 %collective-permute-done.3 = bf16[2,256,512]{2,1,0:T(8,128)(2,1)S(1)} collective-permute-done((bf16[2,256,512]{2,1,0:T(8,128)(2,1)S(1)}, bf16[2,256,512]{2,1,0:T(8,128)(2,1)S(1)}, u32[]{:S(2)}, u32[]{:S(2)}) %collective-permute-start.3) | collective-permute-done | bytes 524320 | tf_op jit(solution)/shard_map/ppermute | solution.py:26
  74.3 0.5 fusion.45
  78.8 1.9 %collective-permute-start.4 = (bf16[256,512]{0,1:T(8,128)(2,1)S(1)}, bf16[256,512]{0,1:T(8,128)(2,1)S(1)}, u32[]{:S(2)}, u32[]{:S(2)}) collective-permute-start(bf16[256,512]{0,1:T(8,128)(2,1)S(1)} %pad_maximum_fusion.4), channel_id=1, source_target_pairs={{0,3},{1,0},{2,1},{3,2},{4,7},{5,4},{6,5},{7,6},{8,11},{9,8},{10,9... | collective-permute-start | bytes 786440 | tf_op jit(solution)/shard_map/ppermute | solution.py:41
  80.8 3.4 %collective-permute-start.5 = (bf16[256,512]{0,1:T(8,128)(2,1)S(1)}, bf16[256,512]{0,1:T(8,128)(2,1)S(1)}, u32[]{:S(2)}, u32[]{:S(2)}) collective-permute-start(bf16[256,512]{0,1:T(8,128)(2,1)S(1)} %pad_maximum_fusion.4), channel_id=1, source_target_pairs={{0,1},{1,2},{2,3},{3,0},{4,5},{5,6},{6,7},{7,4},{8,9},{9,10},{10,1... | collective-permute-start | bytes 786440 | tf_op jit(solution)/shard_map/ppermute | solution.py:38
  84.1 24.9 %all-gather.2.cloned.1.call-done = bf16[2048,512]{1,0:T(8,128)(2,1)} async-done(((bf16[128,512]{1,0:T(8,128)(2,1)}), bf16[2048,512]{1,0:T(8,128)(2,1)}) %all-gather.2.cloned.1.call-update) | async-done | bytes 2097168 | tf_op jit(solution)/shard_map/all_gather | solution.py:106
  109.1 11.0 %collective-permute-start.7 = (bf16[2048,512]{1,0:T(8,128)(2,1)}, bf16[2048,512]{1,0:T(8,128)(2,1)}, u32[]{:S(2)}, u32[]{:S(2)}) collective-permute-start(bf16[2048,512]{1,0:T(8,128)(2,1)} %all-gather.2.cloned.1.call-done), channel_id=1, source_target_pairs={{0,4},{4,0},{1,5},{5,1},{2,6},{6,2},{3,7},{7,3},{8,12},{12,8},{9,1... | collective-permute-start | bytes 6291464 | tf_op jit(solution)/shard_map/ppermute | solution.py:107
  120.1 0.7 convolution_convert_fusion
  120.8 0.9 copy.32
  121.7 3.1 %collective-permute-start.6 = (bf16[256,512]{0,1:T(8,128)(2,1)S(1)}, bf16[256,512]{0,1:T(8,128)(2,1)S(1)}, u32[]{:S(2)}, u32[]{:S(2)}) collective-permute-start(bf16[256,512]{0,1:T(8,128)(2,1)S(1)} %collective-permute-done.5), channel_id=1, source_target_pairs={{0,1},{1,2},{2,3},{3,0},{4,5},{5,6},{6,7},{7,4},{8,9},{9,10},{10,1... | collective-permute-start | bytes 786440 | tf_op jit(solution)/shard_map/ppermute | solution.py:38
  124.9 7.8 %collective-permute-done.6 = bf16[256,512]{0,1:T(8,128)(2,1)S(1)} collective-permute-done((bf16[256,512]{0,1:T(8,128)(2,1)S(1)}, bf16[256,512]{0,1:T(8,128)(2,1)S(1)}, u32[]{:S(2)}, u32[]{:S(2)}) %collective-permute-start.6) | collective-permute-done | bytes 262176 | tf_op jit(solution)/shard_map/ppermute | solution.py:38
  132.9 1.4 copy-done.3
  134.3 0.7 fusion.7
  135.1 2.3 %fusion.6 = bf16[256,512]{1,0:T(8,128)(2,1)S(1)} fusion(bf16[4,512,512]{2,1,0:T(8,128)(2,1)} %bitcast.16, bf16[8,256,512]{1,2,0:T(8,128)(2,1)S(1)} %bitcast_dynamic-update-slice_fusion.2, s32[]{:T(128)S(6)} %select_n.53, f32[512]{0:T(512)S(1)} %get-tuple-element.31), kind=kOutput, calls=%fused_computation.22 | convolution fusion | flops 537133056 | bytes 3409924 | tf_op jit(solution)/shard_map/gtk,gkc->tc/dot_general | solution.py:143
  137.4 0.9 maximum_select_fusion
  (63 shorter events, 7.5 us)
Async XLA Ops:
  7.2 101.9 %all-gather.2.cloned.1.call-start = ((), (), s32[]{:S(2)}) async-start(), calls=%async_computation | async-start | bytes 2228224 | tf_op jit(solution)/shard_map/all_gather | solution.py:106
  29.0 1.2 copy-start
  29.6 13.8 %copy-start.1 = (bf16[256,512]{1,0:T(8,128)(2,1)S(1)}, bf16[256,512]{1,0:T(8,128)(2,1)}, u32[]{:S(2)}) copy-start(bf16[256,512]{1,0:T(8,128)(2,1)} %param.7) | copy-start | bytes 786436
  30.4 15.4 %collective-permute-start = (bf16[2,256,512]{2,1,0:T(8,128)(2,1)S(1)}, bf16[2,256,512]{2,1,0:T(8,128)(2,1)}, u32[]{:S(2)}, u32[]{:S(2)}) collective-permute-start(bf16[2,256,512]{2,1,0:T(8,128)(2,1)S(1)} %pad_maximum_fusion), channel_id=1, source_target_pairs={{0,16},{4,20},{8,24},{12,28},{16,32},{20,36},{24,40},{28,44},{32,4... | collective-permute-start | bytes 1572872 | tf_op jit(solution)/shard_map/ppermute | solution.py:26
  34.2 18.5 %collective-permute-start.1 = (bf16[2,256,512]{2,1,0:T(8,128)(2,1)S(1)}, bf16[2,256,512]{2,1,0:T(8,128)(2,1)}, u32[]{:S(2)}, u32[]{:S(2)}) collective-permute-start(bf16[2,256,512]{2,1,0:T(8,128)(2,1)S(1)} %pad_maximum_fusion), channel_id=1, source_target_pairs={{0,12},{4,16},{8,20},{12,24},{16,28},{20,32},{24,36},{28,40},{32,4... | collective-permute-start | bytes 1572872 | tf_op jit(solution)/shard_map/ppermute | solution.py:26
  39.3 24.7 %collective-permute-start.2 = (bf16[2,256,512]{2,1,0:T(8,128)(2,1)S(1)}, bf16[2,256,512]{2,1,0:T(8,128)(2,1)}, u32[]{:S(2)}, u32[]{:S(2)}) collective-permute-start(bf16[2,256,512]{2,1,0:T(8,128)(2,1)S(1)} %pad_maximum_fusion), channel_id=1, source_target_pairs={{0,8},{4,12},{8,16},{12,20},{16,24},{20,28},{24,32},{28,36},{32,40... | collective-permute-start | bytes 1572872 | tf_op jit(solution)/shard_map/ppermute | solution.py:26
  41.4 31.9 %collective-permute-start.3 = (bf16[2,256,512]{2,1,0:T(8,128)(2,1)S(1)}, bf16[2,256,512]{2,1,0:T(8,128)(2,1)S(1)}, u32[]{:S(2)}, u32[]{:S(2)}) collective-permute-start(bf16[2,256,512]{2,1,0:T(8,128)(2,1)S(1)} %pad_maximum_fusion), channel_id=1, source_target_pairs={{0,4},{4,8},{8,12},{12,16},{16,20},{20,24},{24,28},{28,32},{32,36}... | collective-permute-start | bytes 1572872 | tf_op jit(solution)/shard_map/ppermute | solution.py:26
  43.5 0.9 copy-start.4
  78.8 42.8 %copy-start.2 = (f32[1024]{0:T(1024)S(1)}, f32[1024]{0:T(1024)}, u32[]{:S(2)}) copy-start(f32[1024]{0:T(1024)} %param.13) | copy-start | bytes 12292
  78.8 46.0 %collective-permute-start.4 = (bf16[256,512]{0,1:T(8,128)(2,1)S(1)}, bf16[256,512]{0,1:T(8,128)(2,1)S(1)}, u32[]{:S(2)}, u32[]{:S(2)}) collective-permute-start(bf16[256,512]{0,1:T(8,128)(2,1)S(1)} %pad_maximum_fusion.4), channel_id=1, source_target_pairs={{0,3},{1,0},{2,1},{3,2},{4,7},{5,4},{6,5},{7,6},{8,11},{9,8},{10,9... | collective-permute-start | bytes 786440 | tf_op jit(solution)/shard_map/ppermute | solution.py:41
  80.8 41.0 %collective-permute-start.5 = (bf16[256,512]{0,1:T(8,128)(2,1)S(1)}, bf16[256,512]{0,1:T(8,128)(2,1)S(1)}, u32[]{:S(2)}, u32[]{:S(2)}) collective-permute-start(bf16[256,512]{0,1:T(8,128)(2,1)S(1)} %pad_maximum_fusion.4), channel_id=1, source_target_pairs={{0,1},{1,2},{2,3},{3,0},{4,5},{5,6},{6,7},{7,4},{8,9},{9,10},{10,1... | collective-permute-start | bytes 786440 | tf_op jit(solution)/shard_map/ppermute | solution.py:38
  109.1 26.0 %collective-permute-start.7 = (bf16[2048,512]{1,0:T(8,128)(2,1)}, bf16[2048,512]{1,0:T(8,128)(2,1)}, u32[]{:S(2)}, u32[]{:S(2)}) collective-permute-start(bf16[2048,512]{1,0:T(8,128)(2,1)} %all-gather.2.cloned.1.call-done), channel_id=1, source_target_pairs={{0,4},{4,0},{1,5},{5,1},{2,6},{6,2},{3,7},{7,3},{8,12},{12,8},{9,1... | collective-permute-start | bytes 6291464 | tf_op jit(solution)/shard_map/ppermute | solution.py:107
  121.7 10.9 %collective-permute-start.6 = (bf16[256,512]{0,1:T(8,128)(2,1)S(1)}, bf16[256,512]{0,1:T(8,128)(2,1)S(1)}, u32[]{:S(2)}, u32[]{:S(2)}) collective-permute-start(bf16[256,512]{0,1:T(8,128)(2,1)S(1)} %collective-permute-done.5), channel_id=1, source_target_pairs={{0,1},{1,2},{2,3},{3,0},{4,5},{5,6},{6,7},{7,4},{8,9},{9,10},{10,1... | collective-permute-start | bytes 786440 | tf_op jit(solution)/shard_map/ppermute | solution.py:38
  132.7 1.6 %copy-start.3 = (bf16[2048,512]{1,0:T(8,128)(2,1)S(1)}, bf16[2048,512]{1,0:T(8,128)(2,1)}, u32[]{:S(2)}) copy-start(bf16[2048,512]{1,0:T(8,128)(2,1)} %all-gather.2.cloned.1.call-done) | copy-start | bytes 6291460
Sparse Core Ops, SparseCore 0:
  43.5 65.5 all-gather.1

commit v9 on v8

--- a/solution.py
+++ b/solution.py
@@ -44,6 +44,15 @@
     return jnp.roll(relative, lax.axis_index(axis), axis=0)
 
 
+def direct_gather(piece, axis):
+    count = lax.axis_size(axis)
+    relative = [piece]
+    for distance in range(1, count):
+        pairs = [(i, (i - distance) % count) for i in range(count)]
+        relative.append(lax.ppermute(piece, axis, pairs))
+    return jnp.roll(jnp.stack(relative, axis=0), lax.axis_index(axis), axis=0)
+
+
 def request_info(lengths, token_index):
     request_ends = jnp.cumsum(lengths) * PAGE
     request_starts = request_ends - lengths * PAGE
@@ -99,7 +108,8 @@
     half = out_weight.shape[1] // 2
     weight_pair = lax.all_gather(out_weight, "core", axis=0, tiled=True)
     weight_rows = lax.dynamic_slice_in_dim(weight_pair, core_rank * half, half, 1)
-    weight_rows = lax.all_gather(weight_rows, "x", axis=0, tiled=True)
+    weight_rows = direct_gather(weight_rows, "x")
+    weight_rows = weight_rows.reshape(-1, half)
     weight_rows, query_proj, key_proj = lax.optimization_barrier(
         (weight_rows, query_proj, key_proj)
     )

time: 147 us -> 146 us (level)
  blocking collectives: 18.4 us -> 8.68 us
  starting transfers between devices: 32.3 us -> 40.6 us
  waiting for transfers between devices: 57.1 us -> 61.4 us
  local copies, waits for them, and re-layouts: 9.13 us -> 6.82 us
  matrix products: 7.75 us -> 6.19 us
    all_gather x1 -> x0, blocking collectives: 9.83 us -> none  [local_body(): weight_rows = lax.all_gather(weight_rows, 'x', axis=0, tiled=True)]
    ppermute x0 -> x3, starting transfers between devices: none -> 7.19 us  [direct_gather(): relative.append(lax.ppermute(piece, axis, pairs))]
    ppermute x4, waiting for transfers between devices: 24.4 us -> 29.2 us  [passed_along(): return lax.ppermute(array, axis, pairs)]
    ppermute x1, starting transfers between devices: 1.92 us -> 4.57 us  [ring_gather(): sent_behind = lax.ppermute(sent_behind, axis, backward)]
    unnamed x21 -> x30, local copies, waits for them, and re-layouts: 5.69 us -> 3.66 us
    all_gather x1, waiting for transfers between devices: 24.9 us -> 23.1 us  [local_body(): weight_rows = lax.all_gather(weight_rows, 'z', axis=0, tiled=True)]
    dot_general x1, matrix products: 2.32 us -> 0.74 us  [local_body(): jnp.einsum('gtk,gkc->tc', heads_all, weight_other, preferred_element_type...]
  transfers between devices with their start and end apart: 9 -> 12, of which waited for: 5 -> 7; matrix products, arithmetic and copies ran while one was open for 9% -> 9% of each run, Pallas kernels for 0% -> 0%
where the time goes in v9:
time: 146 us; the launch traced here: 144 us
  waiting for transfers between devices  61.4 us (42%)
  starting transfers between devices  40.6 us (28%)
  between operations  14.6 us (10%)
  blocking collectives  8.68 us (6%)
  local copies, waits for them, and re-layouts  6.82 us (5%)
  matrix products  6.19 us (4%)
  other arithmetic  5.9 us (4%)
    ppermute x4, waiting for transfers between devices, passed_along(): return lax.ppermute(array, axis, pairs)  29.2 us
    all_gather x1, waiting for transfers between devices, local_body(): weight_rows = lax.all_gather(weight_rows, 'z', axis=0, tiled=True)  23.1 us
    ppermute x4, starting transfers between devices, passed_along(): return lax.ppermute(array, axis, pairs)  12.1 us
    ppermute x1, starting transfers between devices, local_body(): weight_other = lax.ppermute(weight_rows, 'core', [(0, 1), (1, 0)])  11.7 us
    all_gather x1, blocking collectives, local_body(): weight_pair = lax.all_gather(out_weight, 'core', axis=0, tiled=True)  8.68 us
    ppermute x2, waiting for transfers between devices, ring_gather(): sent_ahead = lax.ppermute(sent_ahead, axis, forward)  7.75 us
    ppermute x3, starting transfers between devices, direct_gather(): relative.append(lax.ppermute(piece, axis, pairs))  7.19 us
    ppermute x2, starting transfers between devices, ring_gather(): sent_ahead = lax.ppermute(sent_ahead, axis, forward)  5.04 us
  transfers between devices with their start and end apart: 12, of which 7 were waited for; matrix products, arithmetic and copies ran while one was open for 9% of the time, Pallas kernels for 0%

profile of v9, /device:TPU:1, one launch (start us, length us, event | category | flops | bytes accessed | tf_op | source)
XLA Modules:
  0.0 144.2 jit_solution(16662934482946102160)
XLA Ops:
  7.2 8.7 %all_gather.6 = bf16[32,1024]{1,0:T(8,128)(2,1)S(1)} all-gather(bf16[16,1024]{1,0:T(8,128)(2,1)} %param.12), channel_id=1, replica_groups=mesh['z'=16,'x'=4,'core'=2,'head'=4] {'core'}, dimensions={0}, use_global_device_ids=true | all-gather | bytes 98304 | tf_op jit(solution)/shard_map/all_gather | solution.py:109
  15.9 1.9 %collective-permute-start = (bf16[32,512]{1,0:T(8,128)(2,1)S(1)}, bf16[32,512]{1,0:T(8,128)(2,1)S(1)}, u32[]{:S(2)}, u32[]{:S(2)}) collective-permute-start(bf16[32,512]{1,0:T(8,128)(2,1)S(1)} %get-tuple-element.19), channel_id=1, source_target_pairs={{0,24},{8,0},{16,8},{24,16},{1,25},{9,1},{17,9},{25,17},{2,26},{10... | collective-permute-start | bytes 98312 | tf_op jit(solution)/shard_map/ppermute | solution.py:52
  17.8 1.9 %collective-permute-start.1 = (bf16[32,512]{1,0:T(8,128)(2,1)S(1)}, bf16[32,512]{1,0:T(8,128)(2,1)S(1)}, u32[]{:S(2)}, u32[]{:S(2)}) collective-permute-start(bf16[32,512]{1,0:T(8,128)(2,1)S(1)} %get-tuple-element.19), channel_id=1, source_target_pairs={{0,16},{8,24},{16,0},{24,8},{1,17},{9,25},{17,1},{25,9},{2,18},{10... | collective-permute-start | bytes 98312 | tf_op jit(solution)/shard_map/ppermute | solution.py:52
  19.8 3.4 %collective-permute-start.2 = (bf16[32,512]{1,0:T(8,128)(2,1)S(1)}, bf16[32,512]{1,0:T(8,128)(2,1)S(1)}, u32[]{:S(2)}, u32[]{:S(2)}) collective-permute-start(bf16[32,512]{1,0:T(8,128)(2,1)S(1)} %get-tuple-element.19), channel_id=1, source_target_pairs={{0,8},{8,16},{16,24},{24,0},{1,9},{9,17},{17,25},{25,1},{2,10},{10... | collective-permute-start | bytes 98312 | tf_op jit(solution)/shard_map/ppermute | solution.py:52
  23.2 0.7 copy.25
  24.1 0.7 multiply_subtract_fusion.1
  25.4 1.4 collective-permute-done.2
  26.8 0.7 constant_dynamic-slice_fusion
  28.4 0.6 maximum_convert_fusion
  29.2 5.0 %collective-permute-start.3 = (bf16[2,256,512]{2,1,0:T(8,128)(2,1)S(1)}, bf16[2,256,512]{2,1,0:T(8,128)(2,1)}, u32[]{:S(2)}, u32[]{:S(2)}) collective-permute-start(bf16[2,256,512]{2,1,0:T(8,128)(2,1)S(1)} %pad_maximum_fusion), channel_id=1, source_target_pairs={{0,16},{4,20},{8,24},{12,28},{16,32},{20,36},{24,40},{28,44},{32,4... | collective-permute-start | bytes 1572872 | tf_op jit(solution)/shard_map/ppermute | solution.py:26
  34.1 2.3 %collective-permute-start.4 = (bf16[2,256,512]{2,1,0:T(8,128)(2,1)S(1)}, bf16[2,256,512]{2,1,0:T(8,128)(2,1)S(1)}, u32[]{:S(2)}, u32[]{:S(2)}) collective-permute-start(bf16[2,256,512]{2,1,0:T(8,128)(2,1)S(1)} %pad_maximum_fusion), channel_id=1, source_target_pairs={{0,12},{4,16},{8,20},{12,24},{16,28},{20,32},{24,36},{28,40},{32,4... | collective-permute-start | bytes 1572872 | tf_op jit(solution)/shard_map/ppermute | solution.py:26
  36.4 2.6 %collective-permute-start.5 = (bf16[2,256,512]{2,1,0:T(8,128)(2,1)S(1)}, bf16[2,256,512]{2,1,0:T(8,128)(2,1)S(1)}, u32[]{:S(2)}, u32[]{:S(2)}) collective-permute-start(bf16[2,256,512]{2,1,0:T(8,128)(2,1)S(1)} %pad_maximum_fusion), channel_id=1, source_target_pairs={{0,8},{4,12},{8,16},{12,20},{16,24},{20,28},{24,32},{28,36},{32,40... | collective-permute-start | bytes 1572872 | tf_op jit(solution)/shard_map/ppermute | solution.py:26
  39.0 2.3 %collective-permute-start.6 = (bf16[2,256,512]{2,1,0:T(8,128)(2,1)S(1)}, bf16[2,256,512]{2,1,0:T(8,128)(2,1)S(1)}, u32[]{:S(2)}, u32[]{:S(2)}) collective-permute-start(bf16[2,256,512]{2,1,0:T(8,128)(2,1)S(1)} %pad_maximum_fusion), channel_id=1, source_target_pairs={{0,4},{4,8},{8,12},{12,16},{16,20},{20,24},{24,28},{28,32},{32,36}... | collective-permute-start | bytes 1572872 | tf_op jit(solution)/shard_map/ppermute | solution.py:26
  42.2 0.6 pad_maximum_fusion.3
  42.9 0.6 collective-permute-done.3
  43.4 1.1 fusion.26
  44.5 10.2 %collective-permute-done.4 = bf16[2,256,512]{2,1,0:T(8,128)(2,1)S(1)} collective-permute-done((bf16[2,256,512]{2,1,0:T(8,128)(2,1)S(1)}, bf16[2,256,512]{2,1,0:T(8,128)(2,1)S(1)}, u32[]{:S(2)}, u32[]{:S(2)}) %collective-permute-start.4) | collective-permute-done | bytes 524320 | tf_op jit(solution)/shard_map/ppermute | solution.py:26
  54.7 11.2 %collective-permute-done.5 = bf16[2,256,512]{2,1,0:T(8,128)(2,1)S(1)} collective-permute-done((bf16[2,256,512]{2,1,0:T(8,128)(2,1)S(1)}, bf16[2,256,512]{2,1,0:T(8,128)(2,1)S(1)}, u32[]{:S(2)}, u32[]{:S(2)}) %collective-permute-start.5) | collective-permute-done | bytes 524320 | tf_op jit(solution)/shard_map/ppermute | solution.py:26
  65.9 7.2 %collective-permute-done.6 = bf16[2,256,512]{2,1,0:T(8,128)(2,1)S(1)} collective-permute-done((bf16[2,256,512]{2,1,0:T(8,128)(2,1)S(1)}, bf16[2,256,512]{2,1,0:T(8,128)(2,1)S(1)}, u32[]{:S(2)}, u32[]{:S(2)}) %collective-permute-start.6) | collective-permute-done | bytes 524320 | tf_op jit(solution)/shard_map/ppermute | solution.py:26
  75.0 0.5 fusion.44
  78.7 1.9 %collective-permute-start.8 = (bf16[256,512]{0,1:T(8,128)(2,1)S(1)}, bf16[256,512]{0,1:T(8,128)(2,1)S(1)}, u32[]{:S(2)}, u32[]{:S(2)}) collective-permute-start(bf16[256,512]{0,1:T(8,128)(2,1)S(1)} %pad_maximum_fusion.4), channel_id=1, source_target_pairs={{0,1},{1,2},{2,3},{3,0},{4,5},{5,6},{6,7},{7,4},{8,9},{9,10},{10,1... | collective-permute-start | bytes 786440 | tf_op jit(solution)/shard_map/ppermute | solution.py:38
  81.4 4.6 %collective-permute-start.7 = (bf16[256,512]{0,1:T(8,128)(2,1)S(1)}, bf16[256,512]{0,1:T(8,128)(2,1)S(1)}, u32[]{:S(2)}, u32[]{:S(2)}) collective-permute-start(bf16[256,512]{0,1:T(8,128)(2,1)S(1)} %pad_maximum_fusion.4), channel_id=1, source_target_pairs={{0,3},{1,0},{2,1},{3,2},{4,7},{5,4},{6,5},{7,6},{8,11},{9,8},{10,9... | collective-permute-start | bytes 786440 | tf_op jit(solution)/shard_map/ppermute | solution.py:41
  86.0 23.1 %all-gather.2.cloned.1.call-done = bf16[2048,512]{1,0:T(8,128)(2,1)} async-done(((bf16[128,512]{1,0:T(8,128)(2,1)}), bf16[2048,512]{1,0:T(8,128)(2,1)}) %all-gather.2.cloned.1.call-update) | async-done | bytes 2097168 | tf_op jit(solution)/shard_map/all_gather | solution.py:116
  109.1 11.7 %collective-permute-start.10 = (bf16[2048,512]{1,0:T(8,128)(2,1)}, bf16[2048,512]{1,0:T(8,128)(2,1)S(1)}, u32[]{:S(2)}, u32[]{:S(2)}) collective-permute-start(bf16[2048,512]{1,0:T(8,128)(2,1)} %all-gather.2.cloned.1.call-done), channel_id=1, source_target_pairs={{0,4},{4,0},{1,5},{5,1},{2,6},{6,2},{3,7},{7,3},{8,12},{12,8},{9,1... | collective-permute-start | bytes 6291464 | tf_op jit(solution)/shard_map/ppermute | solution.py:117
  120.8 0.7 convolution_convert_fusion
  121.5 0.9 copy.32
  122.3 3.1 %collective-permute-start.9 = (bf16[256,512]{0,1:T(8,128)(2,1)S(1)}, bf16[256,512]{0,1:T(8,128)(2,1)S(1)}, u32[]{:S(2)}, u32[]{:S(2)}) collective-permute-start(bf16[256,512]{0,1:T(8,128)(2,1)S(1)} %collective-permute-done.8), channel_id=1, source_target_pairs={{0,1},{1,2},{2,3},{3,0},{4,5},{5,6},{6,7},{7,4},{8,9},{9,10},{10,1... | collective-permute-start | bytes 786440 | tf_op jit(solution)/shard_map/ppermute | solution.py:38
  125.5 7.7 %collective-permute-done.9 = bf16[256,512]{0,1:T(8,128)(2,1)S(1)} collective-permute-done((bf16[256,512]{0,1:T(8,128)(2,1)S(1)}, bf16[256,512]{0,1:T(8,128)(2,1)S(1)}, u32[]{:S(2)}, u32[]{:S(2)}) %collective-permute-start.9) | collective-permute-done | bytes 262176 | tf_op jit(solution)/shard_map/ppermute | solution.py:38
  133.5 1.4 %copy-done.4 = bf16[2048,512]{1,0:T(8,128)(2,1)S(1)} copy-done((bf16[2048,512]{1,0:T(8,128)(2,1)S(1)}, bf16[2048,512]{1,0:T(8,128)(2,1)}, u32[]{:S(2)}) %copy-start.4) | copy-done | bytes 2097176
  134.9 0.7 fusion.7
  135.7 0.7 fusion.6
  136.4 0.9 maximum_select_fusion
  (78 shorter events, 8.7 us)
Async XLA Ops:
  7.2 20.4 %copy-start.1 = (bf16[256,512]{1,0:T(8,128)(2,1)S(1)}, bf16[256,512]{1,0:T(8,128)(2,1)}, u32[]{:S(2)}) copy-start(bf16[256,512]{1,0:T(8,128)(2,1)} %param.8) | copy-start | bytes 786436
  7.2 101.9 %all-gather.2.cloned.1.call-start = ((), (), s32[]{:S(2)}) async-start(), calls=%async_computation | async-start | bytes 2228224 | tf_op jit(solution)/shard_map/all_gather | solution.py:116
  15.9 9.5 %collective-permute-start = (bf16[32,512]{1,0:T(8,128)(2,1)S(1)}, bf16[32,512]{1,0:T(8,128)(2,1)S(1)}, u32[]{:S(2)}, u32[]{:S(2)}) collective-permute-start(bf16[32,512]{1,0:T(8,128)(2,1)S(1)} %get-tuple-element.19), channel_id=1, source_target_pairs={{0,24},{8,0},{16,8},{24,16},{1,25},{9,1},{17,9},{25,17},{2,26},{10... | collective-permute-start | bytes 98312 | tf_op jit(solution)/shard_map/ppermute | solution.py:52
  17.8 7.6 %collective-permute-start.1 = (bf16[32,512]{1,0:T(8,128)(2,1)S(1)}, bf16[32,512]{1,0:T(8,128)(2,1)S(1)}, u32[]{:S(2)}, u32[]{:S(2)}) collective-permute-start(bf16[32,512]{1,0:T(8,128)(2,1)S(1)} %get-tuple-element.19), channel_id=1, source_target_pairs={{0,16},{8,24},{16,0},{24,8},{1,17},{9,25},{17,1},{25,9},{2,18},{10... | collective-permute-start | bytes 98312 | tf_op jit(solution)/shard_map/ppermute | solution.py:52
  19.8 7.0 %collective-permute-start.2 = (bf16[32,512]{1,0:T(8,128)(2,1)S(1)}, bf16[32,512]{1,0:T(8,128)(2,1)S(1)}, u32[]{:S(2)}, u32[]{:S(2)}) collective-permute-start(bf16[32,512]{1,0:T(8,128)(2,1)S(1)} %get-tuple-element.19), channel_id=1, source_target_pairs={{0,8},{8,16},{16,24},{24,0},{1,9},{9,17},{17,25},{25,1},{2,10},{10... | collective-permute-start | bytes 98312 | tf_op jit(solution)/shard_map/ppermute | solution.py:52
  27.9 1.2 copy-start
  28.4 5.7 %copy-start.5 = (s32[2]{0:T(128)S(1)}, s32[2]{0:T(128)}, u32[]{:S(2)}) copy-start(s32[2]{0:T(128)} %param.11) | copy-start | bytes 28
  28.4 12.9 %copy-start.2 = (bf16[256,512]{1,0:T(8,128)(2,1)S(1)}, bf16[256,512]{1,0:T(8,128)(2,1)}, u32[]{:S(2)}) copy-start(bf16[256,512]{1,0:T(8,128)(2,1)} %param.7) | copy-start | bytes 786436
  29.2 14.3 %collective-permute-start.3 = (bf16[2,256,512]{2,1,0:T(8,128)(2,1)S(1)}, bf16[2,256,512]{2,1,0:T(8,128)(2,1)}, u32[]{:S(2)}, u32[]{:S(2)}) collective-permute-start(bf16[2,256,512]{2,1,0:T(8,128)(2,1)S(1)} %pad_maximum_fusion), channel_id=1, source_target_pairs={{0,16},{4,20},{8,24},{12,28},{16,32},{20,36},{24,40},{28,44},{32,4... | collective-permute-start | bytes 1572872 | tf_op jit(solution)/shard_map/ppermute | solution.py:26
  34.1 20.5 %collective-permute-start.4 = (bf16[2,256,512]{2,1,0:T(8,128)(2,1)S(1)}, bf16[2,256,512]{2,1,0:T(8,128)(2,1)S(1)}, u32[]{:S(2)}, u32[]{:S(2)}) collective-permute-start(bf16[2,256,512]{2,1,0:T(8,128)(2,1)S(1)} %pad_maximum_fusion), channel_id=1, source_target_pairs={{0,12},{4,16},{8,20},{12,24},{16,28},{20,32},{24,36},{28,40},{32,4... | collective-permute-start | bytes 1572872 | tf_op jit(solution)/shard_map/ppermute | solution.py:26
  36.4 29.5 %collective-permute-start.5 = (bf16[2,256,512]{2,1,0:T(8,128)(2,1)S(1)}, bf16[2,256,512]{2,1,0:T(8,128)(2,1)S(1)}, u32[]{:S(2)}, u32[]{:S(2)}) collective-permute-start(bf16[2,256,512]{2,1,0:T(8,128)(2,1)S(1)} %pad_maximum_fusion), channel_id=1, source_target_pairs={{0,8},{4,12},{8,16},{12,20},{16,24},{20,28},{24,32},{28,36},{32,40... | collective-permute-start | bytes 1572872 | tf_op jit(solution)/shard_map/ppermute | solution.py:26
  39.0 34.2 %collective-permute-start.6 = (bf16[2,256,512]{2,1,0:T(8,128)(2,1)S(1)}, bf16[2,256,512]{2,1,0:T(8,128)(2,1)S(1)}, u32[]{:S(2)}, u32[]{:S(2)}) collective-permute-start(bf16[2,256,512]{2,1,0:T(8,128)(2,1)S(1)} %pad_maximum_fusion), channel_id=1, source_target_pairs={{0,4},{4,8},{8,12},{12,16},{16,20},{20,24},{24,28},{28,32},{32,36}... | collective-permute-start | bytes 1572872 | tf_op jit(solution)/shard_map/ppermute | solution.py:26
  78.2 2.5 %copy-start.3 = (f32[1024]{0:T(1024)S(1)}, f32[1024]{0:T(1024)}, u32[]{:S(2)}) copy-start(f32[1024]{0:T(1024)} %param.13) | copy-start | bytes 12292
  78.7 43.6 %collective-permute-start.8 = (bf16[256,512]{0,1:T(8,128)(2,1)S(1)}, bf16[256,512]{0,1:T(8,128)(2,1)S(1)}, u32[]{:S(2)}, u32[]{:S(2)}) collective-permute-start(bf16[256,512]{0,1:T(8,128)(2,1)S(1)} %pad_maximum_fusion.4), channel_id=1, source_target_pairs={{0,1},{1,2},{2,3},{3,0},{4,5},{5,6},{6,7},{7,4},{8,9},{9,10},{10,1... | collective-permute-start | bytes 786440 | tf_op jit(solution)/shard_map/ppermute | solution.py:38
  81.4 44.1 %collective-permute-start.7 = (bf16[256,512]{0,1:T(8,128)(2,1)S(1)}, bf16[256,512]{0,1:T(8,128)(2,1)S(1)}, u32[]{:S(2)}, u32[]{:S(2)}) collective-permute-start(bf16[256,512]{0,1:T(8,128)(2,1)S(1)} %pad_maximum_fusion.4), channel_id=1, source_target_pairs={{0,3},{1,0},{2,1},{3,2},{4,7},{5,4},{6,5},{7,6},{8,11},{9,8},{10,9... | collective-permute-start | bytes 786440 | tf_op jit(solution)/shard_map/ppermute | solution.py:41
  109.1 26.6 %collective-permute-start.10 = (bf16[2048,512]{1,0:T(8,128)(2,1)}, bf16[2048,512]{1,0:T(8,128)(2,1)S(1)}, u32[]{:S(2)}, u32[]{:S(2)}) collective-permute-start(bf16[2048,512]{1,0:T(8,128)(2,1)} %all-gather.2.cloned.1.call-done), channel_id=1, source_target_pairs={{0,4},{4,0},{1,5},{5,1},{2,6},{6,2},{3,7},{7,3},{8,12},{12,8},{9,1... | collective-permute-start | bytes 6291464 | tf_op jit(solution)/shard_map/ppermute | solution.py:117
  122.3 10.9 %collective-permute-start.9 = (bf16[256,512]{0,1:T(8,128)(2,1)S(1)}, bf16[256,512]{0,1:T(8,128)(2,1)S(1)}, u32[]{:S(2)}, u32[]{:S(2)}) collective-permute-start(bf16[256,512]{0,1:T(8,128)(2,1)S(1)} %collective-permute-done.8), channel_id=1, source_target_pairs={{0,1},{1,2},{2,3},{3,0},{4,5},{5,6},{6,7},{7,4},{8,9},{9,10},{10,1... | collective-permute-start | bytes 786440 | tf_op jit(solution)/shard_map/ppermute | solution.py:38
  133.3 1.6 %copy-start.4 = (bf16[2048,512]{1,0:T(8,128)(2,1)S(1)}, bf16[2048,512]{1,0:T(8,128)(2,1)}, u32[]{:S(2)}) copy-start(bf16[2048,512]{1,0:T(8,128)(2,1)} %all-gather.2.cloned.1.call-done) | copy-start | bytes 6291460
Sparse Core Ops, SparseCore 0:
  43.0 66.0 all-gather.1
